TPU v7x, 128 devices: a whole 4x4x4 slice. The times are simulated.
128 devices in a mesh: space: 32 (over y, x, core), shell: 4 (over z).
Axes of the slice: x: 4, y: 4, z: 4, core: 2. Of those that a mesh axis runs over, the one named last changes fastest.
Arguments:
- weights: float32 [262144], P(('space', 'shell')), may hold values from 0.02 to 1.5
- seg_streamline: int32 [32, 4, 32, 256], P('space', 'shell'), may hold values from 0 to 2047
- seg_features: float32 [32, 4, 32, 256, 128], P('space', 'shell'), may hold values from -12 to 12
- pair_counts: int32 [32, 4, 32], P('space', 'shell'), may hold values from 32 to 256, as said below
- seg_voxel: int32 [32, 4, 32, 256], P('space', 'shell'), may hold values from 0 to 4095
- dictionary: float32 [128, 256], P(None, 'shell'), may hold values from -0.375 to 0.375
- measured: float32 [256, 131072], P('shell', 'space'), may hold values from -6 to 6
Outputs:
- new_weights: float32 [262144], P(('space', 'shell'))
- residual: float32 [256, 131072], P('shell', 'space')
Inputs may be any that keep to these rules, and one draw needn't show every extreme that they name: In each shell group q one voxel block d has pair_counts[s, q, d] = 256 for every s.
All inputs are finite; a program needn't handle non-finite values.
Results may differ from a plain program's by a relative error of at most 0.0003.
Values sent between devices are 32-bit elements; how exact they have to be, the bound alone decides.
No kernel may reach another device: no remote copies, remote signals or barrier semaphores. Data moves between devices by JAX's collectives and lax.ppermute only.
A program may use at most 64 MiB of HBM per device.

v0:
```python
import jax
import jax.numpy as jnp
from jax import lax
from jax.sharding import PartitionSpec as P

ITERS = 2


def on_device(weights, seg_streamline, seg_features, pair_counts, seg_voxel, dictionary, measured):
    blocks = seg_streamline.shape[2]
    slots = seg_streamline.shape[3]
    coeffs = seg_features.shape[4]
    voxel_count = measured.shape[1]
    stream_index = seg_streamline.reshape(blocks, slots)
    voxel_index = seg_voxel.reshape(blocks * slots)
    counts = pair_counts.reshape(blocks)
    live_slot = lax.broadcasted_iota(jnp.int32, (blocks, slots), 1) < counts[:, None]
    masked = jnp.where(
        live_slot[:, :, None], seg_features.reshape(blocks, slots, coeffs), jnp.float32(0.0)
    )
    column_sq = (
        jnp.zeros(weights.shape, jnp.float32).at[stream_index].add(jnp.sum(masked * masked, axis=2))
    )
    scaling = 0.5 / (0.5 + column_sq)
    current = weights
    residual = jnp.zeros(measured.shape, jnp.float32)
    for iteration in range(ITERS):
        picked = current[stream_index]
        seg_terms = lax.all_to_all(
            picked[:, :, None] * masked, "space", split_axis=0, concat_axis=0, tiled=True
        )
        partial_coeff = (
            jnp.zeros((voxel_count, coeffs), jnp.float32)
            .at[voxel_index]
            .add(seg_terms.reshape(blocks * slots, coeffs))
        )
        coeff_sum = lax.psum(partial_coeff, "shell")
        residual = (
            jnp.einsum("jg,vj->gv", dictionary, coeff_sum, precision=lax.Precision.HIGHEST)
            - measured
        )
        adjoint = lax.psum(
            jnp.einsum("gv,jg->vj", residual, dictionary, precision=lax.Precision.HIGHEST), "shell"
        )
        adj_rows = adjoint[voxel_index].reshape(blocks, slots, coeffs)
        grad_slot = jnp.sum(
            masked * lax.all_to_all(adj_rows, "space", split_axis=0, concat_axis=0, tiled=True),
            axis=2,
        )
        gradient = jnp.zeros(weights.shape, jnp.float32).at[stream_index].add(grad_slot)
        current = jnp.maximum(current - scaling * gradient, 0.0)
    return (current, residual)


def solution(mesh):
    in_specs = (
        P(("space", "shell")),
        P("space", "shell", None, None),
        P("space", "shell", None, None, None),
        P("space", "shell", None),
        P("space", "shell", None, None),
        P(None, "shell"),
        P("shell", "space"),
    )
    out_specs = (P(("space", "shell")), P("shell", "space"))
    return jax.shard_map(
        on_device, mesh=mesh, in_specs=in_specs, out_specs=out_specs, check_vma=False
    )
```

profile of v0, /device:TPU:1, one launch (start us, length us, event | category | flops | bytes accessed | tf_op | source)
XLA Modules:
  0.0 890.1 jit_solution(17388944566047050254)
XLA Ops:
  8.7 45.5 %gather_fusion = f32[8192]{0:T(1024)S(1)} fusion(f32[2048]{0:T(1024)S(1)} %copy-done.1, s32[8192]{0:T(1024)S(1)} %broadcast_clamp_fusion.1), kind=kCustom, calls=%fused_computation | custom fusion | bytes 98304 | tf_op jit(solution)/shard_map/gather | solution.py:28
  54.3 7.7 fusion.3
  62.0 8.8 all-to-all-start
  70.9 50.1 %all-to-all-done = f32[32,256,128]{2,1,0:T(8,128)} async-done(((f32[32,256,128]{2,1,0:T(8,128)}), f32[32,256,128]{2,1,0:T(8,128)}, u32[]{:S(2)}, u32[]{:S(2)}) %all-to-all-start) | async-done | bytes 4194336 | tf_op jit(solution)/shard_map/all_to_all | solution.py:29
  121.0 45.7 %scatter_custom_fusion.1 = f32[4096,128]{1,0:T(8,128)} fusion(s32[8192]{0:T(1024)S(1)} %bitcast.60, f32[8192,128]{1,0:T(8,128)} %bitcast.4, f32[]{:T(128)} %constant.0.clone.1), kind=kCustom, calls=%fused_computation.21 | custom fusion | flops 1048576 | bytes 2097664 | tf_op jit(solution)/shard_map/scatter-add | solution.py:35
  166.8 59.8 %all-reduce.5.cloned.1.call-done = f32[4096,128]{1,0:T(8,128)} async-done(((f32[4096,128]{1,0:T(8,128)}), f32[4096,128]{1,0:T(8,128)}) %all-reduce.5.cloned.1.call-update) | async-done | bytes 2097168 | tf_op jit(solution)/shard_map/psum | solution.py:37
  226.6 4.0 fusion.1
  230.6 4.8 fusion.15
  235.5 58.7 %all-reduce.7.cloned.1.call-done = f32[4096,128]{1,0:T(8,128)} async-done(((f32[4096,128]{1,0:T(8,128)}), f32[4096,128]{1,0:T(8,128)}) %all-reduce.7.cloned.1.call-update) | async-done | bytes 2097168 | tf_op jit(solution)/shard_map/psum | solution.py:42
  294.2 29.3 %gather_fusion.1 = f32[8192,128]{1,0:T(8,128)} fusion(f32[4096,128]{1,0:T(8,128)} %all-reduce.7.cloned.1.call-done, s32[8192]{0:T(1024)S(1)} %broadcast_clamp_fusion), kind=kCustom, calls=%fused_computation.1 | custom fusion | bytes 8421376 | tf_op jit(solution)/shard_map/gather | solution.py:45
  323.5 58.7 %all_to_all.20 = f32[32,256,128]{2,1,0:T(8,128)S(1)} all-to-all(f32[32,256,128]{2,1,0:T(8,128)} %bitcast.51), channel_id=1, replica_groups=mesh['space'=32,'shell'=4] {'space'}, dimensions={0} | all-to-all | bytes 8388608 | tf_op jit(solution)/shard_map/all_to_all | solution.py:47
  385.9 43.7 %scatter_custom_fusion.2 = f32[2048]{0:T(1024)S(1)} fusion(s32[8192]{0:T(1024)S(1)} %bitcast.57, f32[8192]{0:T(1024)S(1)} %bitcast.66, f32[]{:T(128)} %constant.0.clone.1), kind=kCustom, calls=%fused_computation.33 | custom fusion | flops 8192 | bytes 8196 | tf_op jit(solution)/shard_map/scatter-add | solution.py:50
  429.6 43.5 %scatter_custom_fusion = f32[2048]{0:T(1024)S(1)} fusion(s32[8192]{0:T(1024)S(1)} %bitcast.58, f32[8192]{0:T(1024)S(1)} %bitcast.64, f32[]{:T(128)} %constant.5.clone.1), kind=kCustom, calls=%fused_computation.36 | custom fusion | flops 8192 | bytes 8196 | tf_op jit(solution)/shard_map/scatter-add | solution.py:22
  473.2 45.5 %gather_fusion.2 = f32[8192]{0:T(1024)S(1)} fusion(f32[2048]{0:T(1024)S(1)} %subtract_maximum_fusion.1, s32[8192]{0:T(1024)S(1)} %broadcast_clamp_fusion.1), kind=kCustom, calls=%fused_computation.2 | custom fusion | bytes 98304 | tf_op jit(solution)/shard_map/gather | solution.py:28
  518.7 6.1 fusion.2
  524.8 54.7 %all_to_all.21 = f32[32,256,128]{2,1,0:T(8,128)} all-to-all(f32[32,256,128]{2,1,0:T(8,128)S(1)} %fusion.2), channel_id=1, replica_groups=mesh['space'=32,'shell'=4] {'space'}, dimensions={0} | all-to-all | bytes 8388608 | tf_op jit(solution)/shard_map/all_to_all | solution.py:29
  579.5 45.7 %scatter_custom_fusion.3 = f32[4096,128]{1,0:T(8,128)} fusion(s32[8192]{0:T(1024)S(1)} %bitcast.62, f32[8192,128]{1,0:T(8,128)} %bitcast.52, f32[]{:T(128)} %constant.0.clone.1), kind=kCustom, calls=%fused_computation.19 | custom fusion | flops 1048576 | bytes 2097664 | tf_op jit(solution)/shard_map/scatter-add | solution.py:35
  625.3 55.9 %all-reduce.9.cloned.1.call-done = f32[4096,128]{1,0:T(8,128)} async-done(((f32[4096,128]{1,0:T(8,128)}), f32[4096,128]{1,0:T(8,128)}) %all-reduce.9.cloned.1.call-update) | async-done | bytes 2097168 | tf_op jit(solution)/shard_map/psum | solution.py:37
  681.2 4.0 fusion
  685.2 4.8 fusion.16
  690.0 58.8 %all-reduce.11.cloned.1.call-done = f32[4096,128]{1,0:T(8,128)} async-done(((f32[4096,128]{1,0:T(8,128)}), f32[4096,128]{1,0:T(8,128)}) %all-reduce.11.cloned.1.call-update) | async-done | bytes 2097168 | tf_op jit(solution)/shard_map/psum | solution.py:42
  748.8 29.3 %gather_fusion.3 = f32[8192,128]{1,0:T(8,128)} fusion(f32[4096,128]{1,0:T(8,128)} %all-reduce.11.cloned.1.call-done, s32[8192]{0:T(1024)S(1)} %broadcast_clamp_fusion), kind=kCustom, calls=%fused_computation.3 | custom fusion | bytes 8421376 | tf_op jit(solution)/shard_map/gather | solution.py:45
  778.1 58.7 %all_to_all.22 = f32[32,256,128]{2,1,0:T(8,128)S(1)} all-to-all(f32[32,256,128]{2,1,0:T(8,128)} %bitcast.50), channel_id=1, replica_groups=mesh['space'=32,'shell'=4] {'space'}, dimensions={0} | all-to-all | bytes 8388608 | tf_op jit(solution)/shard_map/all_to_all | solution.py:47
  839.4 43.5 %scatter_custom_fusion.4 = f32[2048]{0:T(1024)S(1)} fusion(s32[8192]{0:T(1024)S(1)} %bitcast.59, f32[8192]{0:T(1024)S(1)} %bitcast.65, f32[]{:T(128)} %constant.0.clone.1), kind=kCustom, calls=%fused_computation.31 | custom fusion | flops 8192 | bytes 8196 | tf_op jit(solution)/shard_map/scatter-add | solution.py:50
  (38 shorter events, 8.9 us)
Async XLA Ops:
  7.2 219.4 %copy-start = (f32[128,64]{0,1:T(8,128)S(1)}, f32[128,64]{0,1:T(8,128)}, u32[]{:S(2)}) copy-start(f32[128,64]{0,1:T(8,128)} %param.12) | copy-start | bytes 98308
  7.2 1.6 copy-start.1
  62.0 8.8 copy-start.6
  62.0 59.0 %all-to-all-start = ((f32[32,256,128]{2,1,0:T(8,128)}), f32[32,256,128]{2,1,0:T(8,128)}, u32[]{:S(2)}, u32[]{:S(2)}) async-start(f32[32,256,128]{2,1,0:T(8,128)} %fusion.3), calls=%async_computation | async-start | bytes 8388608 | tf_op jit(solution)/shard_map/all_to_all | solution.py:29
  70.7 155.8 %copy-start.5 = (f32[64,4096]{1,0:T(8,128)S(1)}, f32[64,4096]{1,0:T(8,128)}, u32[]{:S(2)}) copy-start(f32[64,4096]{1,0:T(8,128)} %param.13) | copy-start | bytes 3145732
  70.8 155.8 %all-reduce.5.cloned.1.call-start = ((), (), s32[]{:S(2)}) async-start(), calls=%async_computation.4 | async-start | bytes 4194304 | tf_op jit(solution)/shard_map/psum | solution.py:37
  166.8 127.4 %all-reduce.7.cloned.1.call-start = ((), (), s32[]{:S(2)}) async-start(), calls=%async_computation.5 | async-start | bytes 4194304 | tf_op jit(solution)/shard_map/psum | solution.py:42
  235.4 445.8 %all-reduce.9.cloned.1.call-start = ((), (), s32[]{:S(2)}) async-start(), calls=%async_computation.6 | async-start | bytes 4194304 | tf_op jit(solution)/shard_map/psum | solution.py:37
  323.5 58.7 %copy-start.2 = (f32[1,1,32,256,128]{4,3,2,1,0:T(8,128)S(1)}, f32[1,1,32,256,128]{4,3,2,1,0:T(8,128)}, u32[]{:S(2)}) copy-start(f32[1,1,32,256,128]{4,3,2,1,0:T(8,128)} %param.9) | copy-start | bytes 12582916
  625.2 123.6 %all-reduce.11.cloned.1.call-start = ((), (), s32[]{:S(2)}) async-start(), calls=%async_computation.7 | async-start | bytes 4194304 | tf_op jit(solution)/shard_map/psum | solution.py:42
  685.2 92.9 %copy-start.4 = (f32[64,4096]{1,0:T(8,128)}, f32[64,4096]{1,0:T(8,128)S(1)}, u32[]{:S(2)}) copy-start(f32[64,4096]{1,0:T(8,128)S(1)} %fusion) | copy-start | bytes 3145732
  778.1 58.7 %copy-start.3 = (f32[1,1,32,256,128]{4,3,2,1,0:T(8,128)S(1)}, f32[1,1,32,256,128]{4,3,2,1,0:T(8,128)}, u32[]{:S(2)}) copy-start(f32[1,1,32,256,128]{4,3,2,1,0:T(8,128)} %param.9) | copy-start | bytes 12582916
Sparse Core Ops, SparseCore 0:
  166.9 59.6 all-reduce.4
  235.5 58.6 all-reduce.6
  625.3 55.8 all-reduce.8
  690.1 58.6 all-reduce.10
where the time goes:
time: 891 us; the launch traced here: 890 us
  waiting for transfers between devices  283 us (32%)
  other arithmetic  244 us (27%)
  blocking collectives  172 us (19%)
  local copies, waits for them, and re-layouts  150 us (17%)
  matrix products  17.6 us (2%)
  between operations  14 us (2%)
  starting transfers between devices  8.94 us (1%)
    psum x2, waiting for transfers between devices, on_device(): lax.psum(jnp.einsum('gv,jg->vj', residual, dictionary, precision=lax.Prec...  118 us
    all_to_all x2, blocking collectives, on_device(): lax.all_to_all(adj_rows, 'space', split_axis=0, concat_axis=0, tiled=True)  117 us
    psum x2, waiting for transfers between devices, on_device(): coeff_sum = lax.psum(partial_coeff, 'shell')  116 us
    scatter-add x2, other arithmetic, on_device(): partial_coeff = jnp.zeros((voxel_count, coeffs), jnp.float32).at[voxel_in...  91.4 us
    gather x4, local copies, waits for them, and re-layouts, on_device(): picked = current[stream_index]  91.1 us
    scatter-add x2, other arithmetic, on_device(): jnp.zeros(weights.shape, jnp.float32).at[stream_index].add(grad_slot)  87.2 us
    gather x2, local copies, waits for them, and re-layouts, on_device(): adj_rows = adjoint[voxel_index].reshape(blocks, slots, coeffs)  58.6 us
    all_to_all x1, blocking collectives, on_device(): lax.all_to_all(picked[:, :, None] * masked, 'space', split_axis=0, concat...  54.7 us
  transfers between devices with their start and end apart: 5, of which 5 were waited for; matrix products, arithmetic and copies ran while one was open for 0% of the time, Pallas kernels for 0%

commit v1 on v0

v1 whole, which is shorter than its diff:
```python
import jax
import jax.numpy as jnp
from jax import lax
from jax.sharding import PartitionSpec as P

ITERS = 2
HI = lax.Precision.HIGHEST


def one_hot_pair(index, count):
    low_count = 64
    high_count = count // low_count
    flat = index.reshape(-1)
    high = (flat // low_count)[:, None] == lax.broadcasted_iota(jnp.int32, (1, high_count), 1)
    low = (flat % low_count)[:, None] == lax.broadcasted_iota(jnp.int32, (1, low_count), 1)
    return high.astype(jnp.float32), low.astype(jnp.float32)


def pick(table, high, low):
    rows = jnp.dot(high, table.reshape(high.shape[1], low.shape[1]), precision=HI)
    return jnp.sum(rows * low, axis=1)


def spread(values, high, low):
    return jnp.dot(high.T, values.reshape(-1)[:, None] * low, precision=HI).reshape(-1)


def on_device(weights, seg_streamline, seg_features, pair_counts, seg_voxel, dictionary, measured):
    blocks = seg_streamline.shape[2]
    slots = seg_streamline.shape[3]
    coeffs = seg_features.shape[4]
    streams = weights.shape[0]
    stream_index = seg_streamline.reshape(blocks, slots)
    voxel_index = seg_voxel.reshape(blocks * slots)
    counts = pair_counts.reshape(blocks)
    live_slot = lax.broadcasted_iota(jnp.int32, (blocks, slots), 1) < counts[:, None]
    masked = jnp.where(
        live_slot[:, :, None], seg_features.reshape(blocks, slots, coeffs), jnp.float32(0.0)
    )
    local_feat = lax.all_to_all(masked, "space", split_axis=0, concat_axis=0, tiled=True)
    local_feat = local_feat.reshape(blocks * slots, coeffs)
    gram = lax.psum(jnp.dot(dictionary, dictionary.T, precision=HI), "shell")
    data_proj = lax.psum(jnp.dot(measured.T, dictionary.T, precision=HI), "shell")
    high, low = one_hot_pair(stream_index, streams)
    column_sq = spread(jnp.sum(masked * masked, axis=2), high, low)
    scaling = 0.5 / (0.5 + column_sq)
    current = weights
    residual = jnp.zeros(measured.shape, jnp.float32)
    for iteration in range(ITERS):
        picked = pick(current, high, low).reshape(blocks, slots)
        local_x = lax.all_to_all(picked, "space", split_axis=0, concat_axis=0, tiled=True)
        seg_terms = local_x.reshape(blocks * slots, 1) * local_feat
        partial_coeff = (
            jnp.zeros((measured.shape[1], coeffs), jnp.float32).at[voxel_index].add(seg_terms)
        )
        coeff_sum = lax.psum(partial_coeff, "shell")
        if iteration == ITERS - 1:
            residual = (
                jnp.einsum("jg,vj->gv", dictionary, coeff_sum, precision=HI) - measured
            )
        adjoint = jnp.dot(coeff_sum, gram, precision=HI) - data_proj
        local_grad = jnp.sum(local_feat * adjoint[voxel_index], axis=1).reshape(blocks, slots)
        grad_slot = lax.all_to_all(local_grad, "space", split_axis=0, concat_axis=0, tiled=True)
        gradient = spread(grad_slot, high, low)
        current = jnp.maximum(current - scaling * gradient, 0.0)
    return (current, residual)


def solution(mesh):
    in_specs = (
        P(("space", "shell")),
        P("space", "shell", None, None),
        P("space", "shell", None, None, None),
        P("space", "shell", None),
        P("space", "shell", None, None),
        P(None, "shell"),
        P("shell", "space"),
    )
    out_specs = (P(("space", "shell")), P("shell", "space"))
    return jax.shard_map(
        on_device, mesh=mesh, in_specs=in_specs, out_specs=out_specs, check_vma=False
    )
```

time: 891 us -> 460 us (0.52)
  blocking collectives: 172 us -> 10.7 us
  other arithmetic: 244 us -> 116 us
  local copies, waits for them, and re-layouts: 150 us -> 58.6 us
  waiting for transfers between devices: 283 us -> 206 us
  starting transfers between devices: 8.94 us -> 29.8 us
    all_to_all x3 -> x1, blocking collectives: 172 us -> 10.7 us  [on_device(): lax.all_to_all(picked, 'space', split_axis=0, concat_axis=0, tiled=True)]
    scatter-add x5 -> x2, other arithmetic: 222 us -> 91.5 us  [on_device(): jnp.zeros((measured.shape[1], coeffs), jnp.float32).at[voxel_index]]
    gather x6 -> x2, local copies, waits for them, and re-layouts: 150 us -> 55.5 us  [on_device(): adjoint[voxel_index]]
    psum x2 -> x1, waiting for transfers between devices: 116 us -> 55 us  [on_device(): coeff_sum = lax.psum(partial_coeff, 'shell')]
    psum x2 -> x1, waiting for transfers between devices: 118 us -> 95.3 us  [on_device(): lax.psum(jnp.dot(measured.T, dictionary.T, precision=HI), 'shell')]
    all_to_all x1 -> x4, starting transfers between devices: 8.77 us -> 29.8 us  [the longest x2 15.1 us: on_device(): lax.all_to_all(local_grad, 'space', split_axis=0, concat_axis=0, tiled=True)]
    dot_general x4 -> x10, matrix products: 17.6 us -> 24.4 us  [the longest x2 8.05 us: on_device(): adjoint = jnp.dot(coeff_sum, gram, precision=HI) - data_proj]
    all_to_all x1 -> x4, waiting for transfers between devices: 50.1 us -> 55.6 us  [the longest x1 44.5 us: on_device(): lax.all_to_all(masked, 'space', split_axis=0, concat_axis=0, tiled=True)]
  transfers between devices with their start and end apart: 5 -> 6, of which waited for: 5 -> 6; matrix products, arithmetic and copies ran while one was open for 0% -> 4% of each run, Pallas kernels for 0% -> 0%
where the time goes in v1:
time: 460 us; the launch traced here: 459 us
  waiting for transfers between devices  206 us (45%)
  other arithmetic  116 us (25%)
  local copies, waits for them, and re-layouts  58.6 us (13%)
  starting transfers between devices  29.8 us (6%)
  matrix products  24.4 us (5%)
  between operations  14.2 us (3%)
  blocking collectives  10.7 us (2%)
    psum x1, waiting for transfers between devices, on_device(): lax.psum(jnp.dot(measured.T, dictionary.T, precision=HI), 'shell')  95.3 us
    scatter-add x2, other arithmetic, on_device(): jnp.zeros((measured.shape[1], coeffs), jnp.float32).at[voxel_index]  91.5 us
    gather x2, local copies, waits for them, and re-layouts, on_device(): adjoint[voxel_index]  55.5 us
    psum x1, waiting for transfers between devices, on_device(): coeff_sum = lax.psum(partial_coeff, 'shell')  55 us
    all_to_all x1, waiting for transfers between devices, on_device(): lax.all_to_all(masked, 'space', split_axis=0, concat_axis=0, tiled=True)  44.5 us
    all_to_all x2, starting transfers between devices, on_device(): lax.all_to_all(local_grad, 'space', split_axis=0, concat_axis=0, tiled=True)  15.1 us
    all_to_all x1, blocking collectives, on_device(): lax.all_to_all(picked, 'space', split_axis=0, concat_axis=0, tiled=True)  10.7 us
    all_to_all x2, waiting for transfers between devices, on_device(): lax.all_to_all(local_grad, 'space', split_axis=0, concat_axis=0, tiled=True)  9.62 us
  transfers between devices with their start and end apart: 6, of which 6 were waited for; matrix products, arithmetic and copies ran while one was open for 4% of the time, Pallas kernels for 0%

profile of v1, /device:TPU:1, one launch (start us, length us, event | category | flops | bytes accessed | tf_op | source)
XLA Modules:
  0.0 459.4 jit_solution(13455062039578054822)
XLA Ops:
  8.8 1.8 fusion.7
  10.6 8.6 %all-to-all-start.1 = ((f32[32,1,256]{2,1,0:T(1,128)}), f32[32,1,256]{2,1,0:T(1,128)S(1)}, u32[]{:S(2)}, u32[]{:S(2)}) async-start(f32[32,1,256]{2,1,0:T(1,128)} %bitcast.3), calls=%async_computation.1 | async-start | bytes 65536 | tf_op jit(solution)/shard_map/all_to_all | solution.py:51
  19.3 5.7 %multiply_reduce_fusion.2 = (f32[32,256]{1,0:T(8,128)S(1)}, f32[32,256,128]{2,1,0:T(8,128)}) fusion(f32[1,1,32,256,128]{4,3,2,1,0:T(8,128)} %param.9, pred[32,256]{1,0:T(8,128)(4,1)S(1)} %iota_compare_fusion.10), kind=kLoop, calls=%fused_computation.15 | loop fusion | flops 3137536 | bytes 8429568 | tf_op jit(solution)/shard_map/reduce_sum | solution.py:45
  26.5 6.1 %all-to-all-start = ((f32[32,256,128]{2,1,0:T(8,128)}), f32[32,256,128]{2,1,0:T(8,128)}, u32[]{:S(2)}, u32[]{:S(2)}) async-start(f32[32,256,128]{2,1,0:T(8,128)} %get-tuple-element.6), calls=%async_computation | async-start | bytes 8388608 | tf_op jit(solution)/shard_map/all_to_all | solution.py:40
  33.6 4.7 %fusion.45 = f32[4096,128]{1,0:T(8,128)} fusion(f32[64,4096]{1,0:T(8,128)S(1)} %copy-done.2, f32[128,64]{0,1:T(8,128)S(1)} %copy-done), kind=kOutput, calls=%fused_computation.65 | convolution fusion | flops 402653184 | bytes 3178496 | tf_op jit(solution)/shard_map/dot_general | solution.py:43
  38.4 44.5 %all-to-all-done = f32[32,256,128]{2,1,0:T(8,128)} async-done(((f32[32,256,128]{2,1,0:T(8,128)}), f32[32,256,128]{2,1,0:T(8,128)}, u32[]{:S(2)}, u32[]{:S(2)}) %all-to-all-start) | async-done | bytes 4194336 | tf_op jit(solution)/shard_map/all_to_all | solution.py:40
  82.9 4.2 bitcast_multiply_fusion.1
  87.0 45.8 %scatter_custom_fusion = f32[4096,128]{1,0:T(8,128)} fusion(s32[8192]{0:T(1024)S(1)} %bitcast.46, f32[8192,128]{1,0:T(8,128)} %bitcast_multiply_fusion.1, f32[]{:T(128)} %constant.40.clone.1), kind=kCustom, calls=%fused_computation.33 | custom fusion | flops 1048576 | bytes 2097664 | tf_op jit(solution)/shard_map/scatter-add | solution.py:54
  132.8 95.3 %all-reduce.6.cloned.1.call-done = (f32[4096,128]{1,0:T(8,128)}, f32[4096,128]{1,0:T(8,128)}, f32[128,128]{1,0:T(8,128)}) async-done(((f32[4096,128]{1,0:T(8,128)}, f32[4096,128]{1,0:T(8,128)}, f32[128,128]{1,0:T(8,128)}), (f32[4096,128]{1,0:T(8,128)}, f32[4096,128]{1,0:T(8,128)}, f32[128,128]{1,0:T(8,128)})) %all-reduce.6.cloned.1.call-update) | async-done | bytes 4259856 | tf_op jit(solution)/shard_map/psum | solution.py:43
  228.2 4.0 convolution_subtract_fusion.1
  232.2 27.7 %gather_fusion = f32[8192,128]{1,0:T(8,128)} fusion(f32[4096,128]{1,0:T(8,128)S(1)} %convolution_subtract_fusion.1, s32[8192]{0:T(1024)S(1)} %broadcast_clamp_fusion), kind=kCustom, calls=%fused_computation | custom fusion | bytes 8421376 | tf_op jit(solution)/shard_map/gather | solution.py:62
  260.0 4.6 %multiply_reduce_fusion.1 = f32[32,256]{1,0:T(8,128)S(1)} fusion(f32[32,256,128]{2,1,0:T(8,128)} %all-to-all-done, f32[32,256,128]{2,1,0:T(8,128)} %bitcast.41), kind=kLoop, calls=%fused_computation.14 | loop fusion | flops 2088960 | bytes 8421376 | tf_op jit(solution)/shard_map/reduce_sum | solution.py:62
  265.2 7.5 %all-to-all-start.2 = ((f32[32,1,256]{2,1,0:T(1,128)}), f32[32,1,256]{2,1,0:T(1,128)S(1)}, u32[]{:S(2)}, u32[]{:S(2)}) async-start(f32[32,1,256]{2,1,0:T(1,128)} %all_to_all.30), calls=%async_computation.2 | async-start | bytes 65536 | tf_op jit(solution)/shard_map/all_to_all | solution.py:63
  274.3 5.8 %all-to-all-done.2 = f32[32,1,256]{2,1,0:T(1,128)S(1)} async-done(((f32[32,1,256]{2,1,0:T(1,128)}), f32[32,1,256]{2,1,0:T(1,128)S(1)}, u32[]{:S(2)}, u32[]{:S(2)}) %all-to-all-start.2) | async-done | bytes 32800 | tf_op jit(solution)/shard_map/all_to_all | solution.py:63
  282.9 10.7 %all_to_all.41 = f32[32,1,256]{2,1,0:T(1,128)S(1)} all-to-all(f32[32,1,256]{2,1,0:T(1,128)S(1)} %bitcast.54), channel_id=1, replica_groups=mesh['space'=32,'shell'=4] {'space'}, dimensions={0} | all-to-all | bytes 65536 | tf_op jit(solution)/shard_map/all_to_all | solution.py:51
  293.6 4.2 bitcast_multiply_fusion
  297.8 45.8 %scatter_custom_fusion.1 = f32[4096,128]{1,0:T(8,128)} fusion(s32[8192]{0:T(1024)S(1)} %bitcast.48, f32[8192,128]{1,0:T(8,128)} %bitcast_multiply_fusion, f32[]{:T(128)} %constant.40.clone.1), kind=kCustom, calls=%fused_computation.31 | custom fusion | flops 1048576 | bytes 2097664 | tf_op jit(solution)/shard_map/scatter-add | solution.py:54
  343.6 55.0 %all-reduce.4.cloned.1.call-done = f32[4096,128]{1,0:T(8,128)} async-done(((f32[4096,128]{1,0:T(8,128)}), f32[4096,128]{1,0:T(8,128)}) %all-reduce.4.cloned.1.call-update) | async-done | bytes 2097168 | tf_op jit(solution)/shard_map/psum | solution.py:56
  398.5 4.0 convolution_subtract_fusion
  402.6 27.7 %gather_fusion.1 = f32[8192,128]{1,0:T(8,128)} fusion(f32[4096,128]{1,0:T(8,128)S(1)} %convolution_subtract_fusion, s32[8192]{0:T(1024)S(1)} %broadcast_clamp_fusion), kind=kCustom, calls=%fused_computation.1 | custom fusion | bytes 8421376 | tf_op jit(solution)/shard_map/gather | solution.py:62
  430.3 4.8 %multiply_reduce_fusion = f32[32,256]{1,0:T(8,128)S(1)} fusion(f32[32,256,128]{2,1,0:T(8,128)} %all-to-all-done, f32[32,256,128]{2,1,0:T(8,128)} %bitcast.40), kind=kLoop, calls=%fused_computation.13 | loop fusion | flops 2088960 | bytes 8421376 | tf_op jit(solution)/shard_map/reduce_sum | solution.py:62
  435.7 7.5 %all-to-all-start.4 = ((f32[32,1,256]{2,1,0:T(1,128)}), f32[32,1,256]{2,1,0:T(1,128)S(1)}, u32[]{:S(2)}, u32[]{:S(2)}) async-start(f32[32,1,256]{2,1,0:T(1,128)} %all_to_all.34), calls=%async_computation.4 | async-start | bytes 65536 | tf_op jit(solution)/shard_map/all_to_all | solution.py:63
  443.2 3.4 fusion
  446.6 3.9 all-to-all-done.4
  (39 shorter events, 11.9 us)
Async XLA Ops:
  7.2 25.5 %copy-start = (f32[128,64]{0,1:T(8,128)S(1)}, f32[128,64]{0,1:T(8,128)}, u32[]{:S(2)}) copy-start(f32[128,64]{0,1:T(8,128)} %param.12) | copy-start | bytes 98308
  7.2 12.0 %copy-start.6 = (s32[1,1,32]{2,1,0:T(1,128)S(1)}, s32[1,1,32]{2,1,0:T(1,128)}, u32[]{:S(2)}) copy-start(s32[1,1,32]{2,1,0:T(1,128)} %param.10) | copy-start | bytes 388
  10.6 15.8 %all-to-all-start.1 = ((f32[32,1,256]{2,1,0:T(1,128)}), f32[32,1,256]{2,1,0:T(1,128)S(1)}, u32[]{:S(2)}, u32[]{:S(2)}) async-start(f32[32,1,256]{2,1,0:T(1,128)} %bitcast.3), calls=%async_computation.1 | async-start | bytes 65536 | tf_op jit(solution)/shard_map/all_to_all | solution.py:51
  26.5 6.2 %copy-start.5 = (s32[1,1,32,256]{3,2,1,0:T(8,128)S(1)}, s32[1,1,32,256]{3,2,1,0:T(8,128)}, u32[]{:S(2)}) copy-start(s32[1,1,32,256]{3,2,1,0:T(8,128)} %param.11) | copy-start | bytes 98308
  26.5 7.1 %copy-start.2 = (f32[64,4096]{1,0:T(8,128)S(1)}, f32[64,4096]{1,0:T(8,128)}, u32[]{:S(2)}) copy-start(f32[64,4096]{1,0:T(8,128)} %param.13) | copy-start | bytes 3145732
  26.5 56.4 %all-to-all-start = ((f32[32,256,128]{2,1,0:T(8,128)}), f32[32,256,128]{2,1,0:T(8,128)}, u32[]{:S(2)}, u32[]{:S(2)}) async-start(f32[32,256,128]{2,1,0:T(8,128)} %get-tuple-element.6), calls=%async_computation | async-start | bytes 8388608 | tf_op jit(solution)/shard_map/all_to_all | solution.py:40
  32.6 195.6 %all-reduce.6.cloned.1.call-start = ((), (), s32[]{:S(2)}) async-start(), calls=%async_computation.6 | async-start | bytes 8519680 | tf_op jit(solution)/shard_map/psum | solution.py:43
  264.6 16.9 %copy-start.4 = (f32[2048]{0:T(1024)S(1)}, f32[2048]{0:T(1024)}, u32[]{:S(2)}) copy-start(f32[2048]{0:T(1024)} %param.7) | copy-start | bytes 24580
  265.2 14.8 %all-to-all-start.2 = ((f32[32,1,256]{2,1,0:T(1,128)}), f32[32,1,256]{2,1,0:T(1,128)S(1)}, u32[]{:S(2)}, u32[]{:S(2)}) async-start(f32[32,1,256]{2,1,0:T(1,128)} %all_to_all.30), calls=%async_computation.2 | async-start | bytes 65536 | tf_op jit(solution)/shard_map/all_to_all | solution.py:63
  272.8 125.8 %all-reduce.4.cloned.1.call-start = ((), (), s32[]{:S(2)}) async-start(), calls=%async_computation.5 | async-start | bytes 4194304 | tf_op jit(solution)/shard_map/psum | solution.py:56
  297.8 100.8 %copy-start.3 = (f32[128,128]{1,0:T(8,128)S(1)}, f32[128,128]{1,0:T(8,128)}, u32[]{:S(2)}) copy-start(f32[128,128]{1,0:T(8,128)} %get-tuple-element.4) | copy-start | bytes 196612
  430.3 12.9 %copy-start.1 = (f32[4096,128]{1,0:T(8,128)S(1)}, f32[4096,128]{1,0:T(8,128)}, u32[]{:S(2)}) copy-start(f32[4096,128]{1,0:T(8,128)} %all-reduce.4.cloned.1.call-done) | copy-start | bytes 6291460
  435.7 14.8 %all-to-all-start.4 = ((f32[32,1,256]{2,1,0:T(1,128)}), f32[32,1,256]{2,1,0:T(1,128)S(1)}, u32[]{:S(2)}, u32[]{:S(2)}) async-start(f32[32,1,256]{2,1,0:T(1,128)} %all_to_all.34), calls=%async_computation.4 | async-start | bytes 65536 | tf_op jit(solution)/shard_map/all_to_all | solution.py:63
Sparse Core Ops, SparseCore 0:
  132.9 95.2 all-reduce.5
  343.7 54.8 all-reduce.3

commit v2 on v1

--- a/solution.py
+++ b/solution.py
@@ -37,10 +37,17 @@
     masked = jnp.where(
         live_slot[:, :, None], seg_features.reshape(blocks, slots, coeffs), jnp.float32(0.0)
     )
-    local_feat = lax.all_to_all(masked, "space", split_axis=0, concat_axis=0, tiled=True)
-    local_feat = local_feat.reshape(blocks * slots, coeffs)
+    half = slots // 2
+    feat_parts = [
+        lax.all_to_all(masked[:, h * half:(h + 1) * half], "space", 0, 0, tiled=True)
+        for h in range(2)
+    ]
     gram = lax.psum(jnp.dot(dictionary, dictionary.T, precision=HI), "shell")
     data_proj = lax.psum(jnp.dot(measured.T, dictionary.T, precision=HI), "shell")
+    feat_parts[1], gram, data_proj = lax.optimization_barrier((feat_parts[1], gram, data_proj))
+    vox_parts = [voxel_index.reshape(blocks, slots)[:, h * half:(h + 1) * half].reshape(-1)
+                 for h in range(2)]
+    local_feat = jnp.concatenate(feat_parts, axis=1).reshape(blocks * slots, coeffs)
     high, low = one_hot_pair(stream_index, streams)
     column_sq = spread(jnp.sum(masked * masked, axis=2), high, low)
     scaling = 0.5 / (0.5 + column_sq)
@@ -49,10 +56,12 @@
     for iteration in range(ITERS):
         picked = pick(current, high, low).reshape(blocks, slots)
         local_x = lax.all_to_all(picked, "space", split_axis=0, concat_axis=0, tiled=True)
-        seg_terms = local_x.reshape(blocks * slots, 1) * local_feat
-        partial_coeff = (
-            jnp.zeros((measured.shape[1], coeffs), jnp.float32).at[voxel_index].add(seg_terms)
-        )
+        partial_coeff = jnp.zeros((measured.shape[1], coeffs), jnp.float32)
+        for h in range(2):
+            part_x = local_x[:, h * half:(h + 1) * half].reshape(-1, 1)
+            partial_coeff = partial_coeff.at[vox_parts[h]].add(
+                part_x * feat_parts[h].reshape(-1, coeffs)
+            )
         coeff_sum = lax.psum(partial_coeff, "shell")
         if iteration == ITERS - 1:
             residual = (

time: 460 us -> 422 us (0.917)
  waiting for transfers between devices: 206 us -> 149 us
  starting transfers between devices: 29.8 us -> 37.7 us
  other arithmetic: 116 us -> 123 us
    psum x1, waiting for transfers between devices: 95.3 us -> 5.62 us  [on_device(): gram = lax.psum(jnp.dot(dictionary, dictionary.T, precision=HI), 'shell')]
    psum x1 -> x2, waiting for transfers between devices: 55 us -> 109 us  [on_device(): coeff_sum = lax.psum(partial_coeff, 'shell')]
    all_to_all x1 -> x2, waiting for transfers between devices: 44.5 us -> 24.7 us  [on_device(): lax.all_to_all(masked[:, h * half:(h + 1) * half], 'space', 0, 0, tiled=T...]
    all_to_all x1 -> x2, starting transfers between devices: 6.1 us -> 13.8 us  [on_device(): lax.all_to_all(masked[:, h * half:(h + 1) * half], 'space', 0, 0, tiled=T...]
    concatenate x0 -> x1, other arithmetic: none -> 4.65 us  [on_device(): jnp.concatenate(feat_parts, axis=1).reshape(blocks * slots, coeffs)]
    scatter-add x2 -> x4, other arithmetic: 91.5 us -> 93.4 us  [on_device(): partial_coeff.at[vox_parts[h]]]
    mul x2 -> x3, other arithmetic: 8.35 us -> 9.26 us  [on_device(): part_x * feat_parts[h].reshape(-1, coeffs)]
  transfers between devices with their start and end apart: 6 -> 8, of which waited for: 6 -> 8; matrix products, arithmetic and copies ran while one was open for 4% -> 11% of each run, Pallas kernels for 0% -> 0%
where the time goes in v2:
time: 422 us
  waiting for transfers between devices  149 us (35%)
  other arithmetic  123 us (29%)
  local copies, waits for them, and re-layouts  62.1 us (15%)
  starting transfers between devices  37.7 us (9%)
  matrix products  24.4 us (6%)
  between operations  14 us (3%)
  blocking collectives  10.7 us (3%)
    psum x2, waiting for transfers between devices, on_device(): coeff_sum = lax.psum(partial_coeff, 'shell')  109 us
    scatter-add x4, other arithmetic, on_device(): partial_coeff.at[vox_parts[h]]  93.4 us
    gather x2, local copies, waits for them, and re-layouts, on_device(): adjoint[voxel_index]  55.4 us
    all_to_all x2, waiting for transfers between devices, on_device(): lax.all_to_all(masked[:, h * half:(h + 1) * half], 'space', 0, 0, tiled=T...  24.7 us
    all_to_all x2, starting transfers between devices, on_device(): lax.all_to_all(local_grad, 'space', split_axis=0, concat_axis=0, tiled=True)  15.2 us
    all_to_all x2, starting transfers between devices, on_device(): lax.all_to_all(masked[:, h * half:(h + 1) * half], 'space', 0, 0, tiled=T...  13.8 us
    all_to_all x1, blocking collectives, on_device(): lax.all_to_all(picked, 'space', split_axis=0, concat_axis=0, tiled=True)  10.7 us
    reduce_sum x2, other arithmetic, on_device(): jnp.sum(local_feat * adjoint[voxel_index], axis=1).reshape(blocks, slots)  10.6 us
  transfers between devices with their start and end apart: 8, of which 8 were waited for; matrix products, arithmetic and copies ran while one was open for 11% of the time, Pallas kernels for 0%

profile of v2, /device:TPU:1, one launch (start us, length us, event | category | flops | bytes accessed | tf_op | source)
XLA Modules:
  0.0 421.6 jit_solution(4449629302932283)
XLA Ops:
  10.6 8.6 %all-to-all-start.2 = ((f32[32,1,256]{2,1,0:T(1,128)}), f32[32,1,256]{2,1,0:T(1,128)S(1)}, u32[]{:S(2)}, u32[]{:S(2)}) async-start(f32[32,1,256]{2,1,0:T(1,128)} %bitcast.6), calls=%async_computation.2 | async-start | bytes 65536 | tf_op jit(solution)/shard_map/all_to_all | solution.py:58
  19.3 4.5 %multiply_reduce_fusion = (f32[32,256]{1,0:T(8,128)S(1)}, f32[32,256,128]{2,1,0:T(8,128)S(1)}) fusion(f32[1,1,32,256,128]{4,3,2,1,0:T(8,128)} %param.9, pred[32,256]{1,0:T(8,128)(4,1)S(1)} %iota_compare_fusion.10), kind=kLoop, calls=%fused_computation.18 | loop fusion | flops 3137536 | bytes 8429568 | tf_op jit(solution)/shard_map/reduce_sum | solution.py:52
  26.5 7.1 %all-to-all-start = ((f32[32,128,128]{2,1,0:T(8,128)}), f32[32,128,128]{2,1,0:T(8,128)S(1)}, u32[]{:S(2)}, u32[]{:S(2)}) async-start(f32[32,128,128]{2,1,0:T(8,128)} %get-tuple-element.12), calls=%async_computation | async-start | bytes 4194304 | tf_op jit(solution)/shard_map/all_to_all | solution.py:42
  34.5 4.8 %fusion.49 = f32[4096,128]{1,0:T(8,128)} fusion(f32[64,4096]{1,0:T(8,128)S(1)} %copy-done.6, f32[128,64]{0,1:T(8,128)S(1)} %copy-done), kind=kOutput, calls=%fused_computation.82 | convolution fusion | flops 402653184 | bytes 3178496 | tf_op jit(solution)/shard_map/dot_general | solution.py:46
  39.4 21.9 %all-to-all-done = f32[32,128,128]{2,1,0:T(8,128)S(1)} async-done(((f32[32,128,128]{2,1,0:T(8,128)}), f32[32,128,128]{2,1,0:T(8,128)S(1)}, u32[]{:S(2)}, u32[]{:S(2)}) %all-to-all-start) | async-done | bytes 2097184 | tf_op jit(solution)/shard_map/all_to_all | solution.py:42
  61.4 6.7 %all-to-all-start.1 = ((f32[32,128,128]{2,1,0:T(8,128)}), f32[32,128,128]{2,1,0:T(8,128)}, u32[]{:S(2)}, u32[]{:S(2)}) async-start(f32[32,128,128]{2,1,0:T(8,128)} %get-tuple-element.13), calls=%async_computation.1 | async-start | bytes 4194304 | tf_op jit(solution)/shard_map/all_to_all | solution.py:42
  70.2 23.2 %scatter_custom_fusion = f32[4096,128]{1,0:T(8,128)S(1)} fusion(s32[4096]{0:T(1024)S(1)} %bitcast.83, f32[4096,128]{1,0:T(8,128)} %bitcast_multiply_fusion.5, f32[]{:T(128)} %constant.42.clone.1), kind=kCustom, calls=%fused_computation.40 | custom fusion | flops 524288 | bytes 2097664 | tf_op jit(solution)/shard_map/scatter-add | solution.py:62
  96.1 5.6 %all-reduce.9.cloned.1.call-done = (f32[128,128]{1,0:T(8,128)}, f32[4096,128]{1,0:T(8,128)}) async-done(((f32[128,128]{1,0:T(8,128)}, f32[4096,128]{1,0:T(8,128)}), (f32[128,128]{1,0:T(8,128)}, f32[4096,128]{1,0:T(8,128)})) %all-reduce.9.cloned.1.call-update) | async-done | bytes 2162704 | tf_op jit(solution)/shard_map/psum | solution.py:45
  105.3 23.6 %scatter_fusion = f32[4096,128]{1,0:T(8,128)S(1)} fusion(f32[4096,128]{1,0:T(8,128)S(1)} %scatter_custom_fusion, s32[4096]{0:T(1024)S(1)} %bitcast.67, f32[4096,128]{1,0:T(8,128)} %bitcast_multiply_fusion.3), kind=kCustom, calls=%fused_computation.3 | custom fusion | flops 524288 | bytes 6307840 | tf_op jit(solution)/shard_map/scatter-add | solution.py:62
  130.3 4.7 %pad_maximum_fusion = f32[32,256,128]{2,1,0:T(8,128)} fusion(f32[32,128,128]{2,1,0:T(8,128)} %all-to-all-done.1, f32[32,128,128]{2,1,0:T(8,128)} %copy-done.3), kind=kLoop, calls=%fused_computation.12 | loop fusion | flops 1048576 | bytes 8388608 | tf_op jit(solution)/shard_map/concatenate | solution.py:50
  135.0 54.1 %all-reduce.5.cloned.1.call-done = f32[4096,128]{1,0:T(8,128)} async-done(((f32[4096,128]{1,0:T(8,128)}), f32[4096,128]{1,0:T(8,128)}) %all-reduce.5.cloned.1.call-update) | async-done | bytes 2097168 | tf_op jit(solution)/shard_map/psum | solution.py:65
  189.0 4.0 convolution_subtract_fusion.1
  193.0 27.7 %gather_fusion = f32[8192,128]{1,0:T(8,128)} fusion(f32[4096,128]{1,0:T(8,128)S(1)} %convolution_subtract_fusion.1, s32[8192]{0:T(1024)S(1)} %broadcast_clamp_fusion), kind=kCustom, calls=%fused_computation | custom fusion | bytes 8421376 | tf_op jit(solution)/shard_map/gather | solution.py:71
  220.7 5.2 %fusion.1 = f32[8192]{0:T(1024)} fusion(f32[8192,128]{1,0:T(8,128)} %gather_fusion, f32[32,256,128]{2,1,0:T(8,128)} %pad_maximum_fusion), kind=kLoop, calls=%fused_computation.15 | loop fusion | flops 2088960 | bytes 8421376 | tf_op jit(solution)/shard_map/reduce_sum | solution.py:71
  226.0 7.7 %all-to-all-start.3 = ((f32[32,1,256]{2,1,0:T(1,128)}), f32[32,1,256]{2,1,0:T(1,128)S(1)}, u32[]{:S(2)}, u32[]{:S(2)}) async-start(f32[32,1,256]{2,1,0:T(1,128)} %bitcast.14), calls=%async_computation.3 | async-start | bytes 65536 | tf_op jit(solution)/shard_map/all_to_all | solution.py:72
  235.1 5.8 %all-to-all-done.3 = f32[32,1,256]{2,1,0:T(1,128)S(1)} async-done(((f32[32,1,256]{2,1,0:T(1,128)}), f32[32,1,256]{2,1,0:T(1,128)S(1)}, u32[]{:S(2)}, u32[]{:S(2)}) %all-to-all-start.3) | async-done | bytes 32800 | tf_op jit(solution)/shard_map/all_to_all | solution.py:72
  243.7 10.7 %all_to_all.52 = f32[32,1,256]{2,1,0:T(1,128)S(1)} all-to-all(f32[32,1,256]{2,1,0:T(1,128)S(1)} %bitcast.82), channel_id=1, replica_groups=mesh['space'=32,'shell'=4] {'space'}, dimensions={0} | all-to-all | bytes 65536 | tf_op jit(solution)/shard_map/all_to_all | solution.py:58
  258.3 23.2 %scatter_custom_fusion.2 = f32[4096,128]{1,0:T(8,128)S(1)} fusion(s32[4096]{0:T(1024)S(1)} %bitcast.84, f32[4096,128]{1,0:T(8,128)} %get-tuple-element.23, f32[]{:T(128)} %constant.42.clone.1), kind=kCustom, calls=%fused_computation.38 | custom fusion | flops 524288 | bytes 2097664 | tf_op jit(solution)/shard_map/scatter-add | solution.py:62
  281.4 23.4 %scatter_fusion.1 = f32[4096,128]{1,0:T(8,128)S(1)} fusion(f32[4096,128]{1,0:T(8,128)S(1)} %scatter_custom_fusion.2, s32[4096]{0:T(1024)S(1)} %bitcast.68, f32[4096,128]{1,0:T(8,128)} %get-tuple-element.22), kind=kCustom, calls=%fused_computation.5 | custom fusion | flops 524288 | bytes 6307840 | tf_op jit(solution)/shard_map/scatter-add | solution.py:62
  306.2 54.9 %all-reduce.7.cloned.1.call-done = f32[4096,128]{1,0:T(8,128)} async-done(((f32[4096,128]{1,0:T(8,128)}), f32[4096,128]{1,0:T(8,128)}) %all-reduce.7.cloned.1.call-update) | async-done | bytes 2097168 | tf_op jit(solution)/shard_map/psum | solution.py:65
  361.2 4.0 convolution_subtract_fusion
  365.2 27.7 %gather_fusion.1 = f32[8192,128]{1,0:T(8,128)} fusion(f32[4096,128]{1,0:T(8,128)S(1)} %convolution_subtract_fusion, s32[8192]{0:T(1024)S(1)} %broadcast_clamp_fusion), kind=kCustom, calls=%fused_computation.1 | custom fusion | bytes 8421376 | tf_op jit(solution)/shard_map/gather | solution.py:71
  392.9 5.4 %fusion.2 = f32[8192]{0:T(1024)} fusion(f32[8192,128]{1,0:T(8,128)} %gather_fusion.1, f32[32,256,128]{2,1,0:T(8,128)} %pad_maximum_fusion), kind=kLoop, calls=%fused_computation.16 | loop fusion | flops 2088960 | bytes 8421376 | tf_op jit(solution)/shard_map/reduce_sum | solution.py:71
  398.2 7.5 %all-to-all-start.5 = ((f32[32,1,256]{2,1,0:T(1,128)}), f32[32,1,256]{2,1,0:T(1,128)S(1)}, u32[]{:S(2)}, u32[]{:S(2)}) async-start(f32[32,1,256]{2,1,0:T(1,128)} %bitcast.19), calls=%async_computation.5 | async-start | bytes 65536 | tf_op jit(solution)/shard_map/all_to_all | solution.py:72
  (62 shorter events, 35.7 us)
Async XLA Ops:
  7.2 26.4 %copy-start = (f32[128,64]{0,1:T(8,128)S(1)}, f32[128,64]{0,1:T(8,128)}, u32[]{:S(2)}) copy-start(f32[128,64]{0,1:T(8,128)} %param.12) | copy-start | bytes 98308
  7.2 12.0 %copy-start.10 = (s32[1,1,32]{2,1,0:T(1,128)S(1)}, s32[1,1,32]{2,1,0:T(1,128)}, u32[]{:S(2)}) copy-start(s32[1,1,32]{2,1,0:T(1,128)} %param.10) | copy-start | bytes 388
  10.6 15.8 %all-to-all-start.2 = ((f32[32,1,256]{2,1,0:T(1,128)}), f32[32,1,256]{2,1,0:T(1,128)S(1)}, u32[]{:S(2)}, u32[]{:S(2)}) async-start(f32[32,1,256]{2,1,0:T(1,128)} %bitcast.6), calls=%async_computation.2 | async-start | bytes 65536 | tf_op jit(solution)/shard_map/all_to_all | solution.py:58
  26.5 8.1 %copy-start.6 = (f32[64,4096]{1,0:T(8,128)S(1)}, f32[64,4096]{1,0:T(8,128)}, u32[]{:S(2)}) copy-start(f32[64,4096]{1,0:T(8,128)} %param.13) | copy-start | bytes 3145732
  26.5 34.9 %all-to-all-start = ((f32[32,128,128]{2,1,0:T(8,128)}), f32[32,128,128]{2,1,0:T(8,128)S(1)}, u32[]{:S(2)}, u32[]{:S(2)}) async-start(f32[32,128,128]{2,1,0:T(8,128)} %get-tuple-element.12), calls=%async_computation | async-start | bytes 4194304 | tf_op jit(solution)/shard_map/all_to_all | solution.py:42
  33.6 68.2 %all-reduce.9.cloned.1.call-start = ((), (), s32[]{:S(2)}) async-start(), calls=%async_computation.8 | async-start | bytes 4325376 | tf_op jit(solution)/shard_map/psum | solution.py:45
  34.5 4.8 %copy-start.8 = (s32[1,1,32,256]{3,2,1,0:T(8,128)S(1)}, s32[1,1,32,256]{3,2,1,0:T(8,128)}, u32[]{:S(2)}) copy-start(s32[1,1,32,256]{3,2,1,0:T(8,128)} %param.11) | copy-start | bytes 98308
  61.4 6.8 %copy-start.3 = (f32[32,128,128]{2,1,0:T(8,128)}, f32[32,128,128]{2,1,0:T(8,128)S(1)}, u32[]{:S(2)}) copy-start(f32[32,128,128]{2,1,0:T(8,128)S(1)} %all-to-all-done) | copy-start | bytes 6291460
  61.4 34.7 %all-to-all-start.1 = ((f32[32,128,128]{2,1,0:T(8,128)}), f32[32,128,128]{2,1,0:T(8,128)}, u32[]{:S(2)}, u32[]{:S(2)}) async-start(f32[32,128,128]{2,1,0:T(8,128)} %get-tuple-element.13), calls=%async_computation.1 | async-start | bytes 4194304 | tf_op jit(solution)/shard_map/all_to_all | solution.py:42
  68.1 120.9 %all-reduce.5.cloned.1.call-start = ((), (), s32[]{:S(2)}) async-start(), calls=%async_computation.6 | async-start | bytes 4194304 | tf_op jit(solution)/shard_map/psum | solution.py:65
  128.9 1.3 copy-start.1
  130.3 58.7 %copy-start.7 = (f32[128,128]{1,0:T(8,128)S(1)}, f32[128,128]{1,0:T(8,128)}, u32[]{:S(2)}) copy-start(f32[128,128]{1,0:T(8,128)} %get-tuple-element.6) | copy-start | bytes 196612
  226.0 16.4 %copy-start.9 = (f32[2048]{0:T(1024)S(1)}, f32[2048]{0:T(1024)}, u32[]{:S(2)}) copy-start(f32[2048]{0:T(1024)} %param.7) | copy-start | bytes 24580
  226.0 14.9 %all-to-all-start.3 = ((f32[32,1,256]{2,1,0:T(1,128)}), f32[32,1,256]{2,1,0:T(1,128)S(1)}, u32[]{:S(2)}, u32[]{:S(2)}) async-start(f32[32,1,256]{2,1,0:T(1,128)} %bitcast.14), calls=%async_computation.3 | async-start | bytes 65536 | tf_op jit(solution)/shard_map/all_to_all | solution.py:72
  233.6 127.5 %all-reduce.7.cloned.1.call-start = ((), (), s32[]{:S(2)}) async-start(), calls=%async_computation.7 | async-start | bytes 4194304 | tf_op jit(solution)/shard_map/psum | solution.py:65
  240.9 13.6 %copy-start.4 = (f32[32,128,128]{2,1,0:T(8,128)S(1)}, f32[32,128,128]{2,1,0:T(8,128)}, u32[]{:S(2)}) copy-start(f32[32,128,128]{2,1,0:T(8,128)} %copy-done.3) | copy-start | bytes 6291460
  304.9 1.3 copy-start.2
  392.9 12.9 %copy-start.5 = (f32[4096,128]{1,0:T(8,128)S(1)}, f32[4096,128]{1,0:T(8,128)}, u32[]{:S(2)}) copy-start(f32[4096,128]{1,0:T(8,128)} %all-reduce.7.cloned.1.call-done) | copy-start | bytes 6291460
  398.2 14.8 %all-to-all-start.5 = ((f32[32,1,256]{2,1,0:T(1,128)}), f32[32,1,256]{2,1,0:T(1,128)S(1)}, u32[]{:S(2)}, u32[]{:S(2)}) async-start(f32[32,1,256]{2,1,0:T(1,128)} %bitcast.19), calls=%async_computation.5 | async-start | bytes 65536 | tf_op jit(solution)/shard_map/all_to_all | solution.py:72
Sparse Core Ops, SparseCore 0:
  39.4 62.2 all-reduce.8
  130.4 58.6 all-reduce.4
  306.3 54.7 all-reduce.6

commit v3 on v2

--- a/solution.py
+++ b/solution.py
@@ -2,6 +2,8 @@
 import jax.numpy as jnp
 from jax import lax
 from jax.sharding import PartitionSpec as P
+from jax.experimental import pallas as pl
+from jax.experimental.pallas import tpu as pltpu
 
 ITERS = 2
 HI = lax.Precision.HIGHEST
@@ -23,6 +25,64 @@
 
 def spread(values, high, low):
     return jnp.dot(high.T, values.reshape(-1)[:, None] * low, precision=HI).reshape(-1)
+
+
+UNROLL = 8
+ACCS = 4
+
+
+def scatter_kernel(idx_ref, xs_ref, feat_ref, init_ref, out_ref, *accs):
+    accs[0][...] = init_ref[...]
+    for acc in accs[1:]:
+        acc[...] = jnp.zeros(acc.shape, acc.dtype)
+
+    def body(step, carry):
+        for u in range(UNROLL):
+            k = step * UNROLL + u
+            acc = accs[u % ACCS]
+            acc[pl.ds(idx_ref[k], 1), :] += xs_ref[k] * feat_ref[pl.ds(k, 1), :]
+        return carry
+
+    lax.fori_loop(0, feat_ref.shape[0] // UNROLL, body, 0)
+    total = accs[0][...]
+    for acc in accs[1:]:
+        total = total + acc[...]
+    out_ref[...] = total
+
+
+def row_scatter(idx, xs, feat, init):
+    smem = pl.BlockSpec(memory_space=pltpu.SMEM)
+    vmem = pl.BlockSpec(memory_space=pltpu.VMEM)
+    return pl.pallas_call(
+        scatter_kernel,
+        out_shape=jax.ShapeDtypeStruct(init.shape, jnp.float32),
+        in_specs=[smem, smem, vmem, vmem],
+        out_specs=vmem,
+        scratch_shapes=[pltpu.VMEM(init.shape, jnp.float32) for _ in range(ACCS)],
+    )(idx, xs, feat, init)
+
+
+def gather_kernel(idx_ref, table_ref, feat_ref, out_ref, rows_ref):
+    def body(step, carry):
+        for u in range(UNROLL):
+            k = step * UNROLL + u
+            rows_ref[pl.ds(k, 1), :] = table_ref[pl.ds(idx_ref[k], 1), :]
+        return carry
+
+    lax.fori_loop(0, feat_ref.shape[0] // UNROLL, body, 0)
+    out_ref[...] = jnp.sum(rows_ref[...] * feat_ref[...], axis=1, keepdims=True)
+
+
+def row_gather_dot(idx, table, feat):
+    smem = pl.BlockSpec(memory_space=pltpu.SMEM)
+    vmem = pl.BlockSpec(memory_space=pltpu.VMEM)
+    return pl.pallas_call(
+        gather_kernel,
+        out_shape=jax.ShapeDtypeStruct((feat.shape[0], 1), jnp.float32),
+        in_specs=[smem, vmem, vmem],
+        out_specs=vmem,
+        scratch_shapes=[pltpu.VMEM(feat.shape, jnp.float32)],
+    )(idx, table, feat)
 
 
 def on_device(weights, seg_streamline, seg_features, pair_counts, seg_voxel, dictionary, measured):
@@ -58,9 +118,9 @@
         local_x = lax.all_to_all(picked, "space", split_axis=0, concat_axis=0, tiled=True)
         partial_coeff = jnp.zeros((measured.shape[1], coeffs), jnp.float32)
         for h in range(2):
-            part_x = local_x[:, h * half:(h + 1) * half].reshape(-1, 1)
-            partial_coeff = partial_coeff.at[vox_parts[h]].add(
-                part_x * feat_parts[h].reshape(-1, coeffs)
+            part_x = local_x[:, h * half:(h + 1) * half].reshape(-1)
+            partial_coeff = row_scatter(
+                vox_parts[h], part_x, feat_parts[h].reshape(-1, coeffs), partial_coeff
             )
         coeff_sum = lax.psum(partial_coeff, "shell")
         if iteration == ITERS - 1:
@@ -68,7 +128,7 @@
                 jnp.einsum("jg,vj->gv", dictionary, coeff_sum, precision=HI) - measured
             )
         adjoint = jnp.dot(coeff_sum, gram, precision=HI) - data_proj
-        local_grad = jnp.sum(local_feat * adjoint[voxel_index], axis=1).reshape(blocks, slots)
+        local_grad = row_gather_dot(voxel_index, adjoint, local_feat).reshape(blocks, slots)
         grad_slot = lax.all_to_all(local_grad, "space", split_axis=0, concat_axis=0, tiled=True)
         gradient = spread(grad_slot, high, low)
         current = jnp.maximum(current - scaling * gradient, 0.0)

time: 422 us -> 358 us (0.85)
  other arithmetic: 123 us -> 17.2 us
  Pallas kernels: 0 us -> 83.7 us
  local copies, waits for them, and re-layouts: 62.1 us -> 10.3 us
  waiting for transfers between devices: 149 us -> 157 us
    scatter-add x4 -> x0, other arithmetic: 93.4 us -> none  [on_device(): partial_coeff.at[vox_parts[h]]]
    pallas_call x0 -> x6, Pallas kernels: none -> 83.7 us  [the longest x4 50.2 us: row_scatter(): pl.pallas_call(scatter_kernel, out_shape=jax.ShapeDtypeStruct(init.shape,...]
    gather x2 -> x0, local copies, waits for them, and re-layouts: 55.4 us -> none  [on_device(): adjoint[voxel_index]]
    reduce_sum x2 -> x0, other arithmetic: 10.6 us -> none  [on_device(): jnp.sum(local_feat * adjoint[voxel_index], axis=1).reshape(blocks, slots)]
    all_to_all x2, waiting for transfers between devices: 24.7 us -> 34.6 us  [on_device(): lax.all_to_all(masked[:, h * half:(h + 1) * half], 'space', 0, 0, tiled=T...]
    mul x3 -> x0, other arithmetic: 9.26 us -> none  [on_device(): part_x * feat_parts[h].reshape(-1, coeffs)]
    pallas_call x0 -> x2, other arithmetic: none -> 8.05 us  [row_gather_dot(): pl.pallas_call(gather_kernel, out_shape=jax.ShapeDtypeStruct((feat.shape[...]
  transfers between devices with their start and end apart: 8 -> 8, of which waited for: 8 -> 8; matrix products, arithmetic and copies ran while one was open for 11% -> 7% of each run, Pallas kernels for 0% -> 4%
where the time goes in v3:
time: 358 us; the launch traced here: 357 us
  waiting for transfers between devices  157 us (44%)
  Pallas kernels  83.7 us (23%)
  starting transfers between devices  37.9 us (11%)
  matrix products  26.4 us (7%)
  other arithmetic  17.2 us (5%)
  between operations  13.9 us (4%)
  blocking collectives  10.7 us (3%)
  local copies, waits for them, and re-layouts  10.3 us (3%)
    psum x2, waiting for transfers between devices, on_device(): coeff_sum = lax.psum(partial_coeff, 'shell')  108 us
    pallas_call x4, Pallas kernels, row_scatter(): pl.pallas_call(scatter_kernel, out_shape=jax.ShapeDtypeStruct(init.shape,...  50.2 us
    all_to_all x2, waiting for transfers between devices, on_device(): lax.all_to_all(masked[:, h * half:(h + 1) * half], 'space', 0, 0, tiled=T...  34.6 us
    pallas_call x2, Pallas kernels, row_gather_dot(): pl.pallas_call(gather_kernel, out_shape=jax.ShapeDtypeStruct((feat.shape[...  33.5 us
    all_to_all x2, starting transfers between devices, on_device(): lax.all_to_all(local_grad, 'space', split_axis=0, concat_axis=0, tiled=True)  15.2 us
    all_to_all x2, starting transfers between devices, on_device(): lax.all_to_all(masked[:, h * half:(h + 1) * half], 'space', 0, 0, tiled=T...  13.8 us
    all_to_all x1, blocking collectives, on_device(): lax.all_to_all(picked, 'space', split_axis=0, concat_axis=0, tiled=True)  10.7 us
    dot_general x2, matrix products, on_device(): adjoint = jnp.dot(coeff_sum, gram, precision=HI) - data_proj  10.1 us
  transfers between devices with their start and end apart: 8, of which 8 were waited for; matrix products, arithmetic and copies ran while one was open for 7% of the time, Pallas kernels for 4%

profile of v3, /device:TPU:1, one launch (start us, length us, event | category | flops | bytes accessed | tf_op | source)
XLA Modules:
  0.0 357.3 jit_solution(9234783461877287147)
XLA Ops:
  10.6 8.6 %all-to-all-start = ((f32[32,1,256]{2,1,0:T(1,128)}), f32[32,1,256]{2,1,0:T(1,128)S(1)}, u32[]{:S(2)}, u32[]{:S(2)}) async-start(f32[32,1,256]{2,1,0:T(1,128)} %bitcast.4), calls=%async_computation | async-start | bytes 65536 | tf_op jit(solution)/shard_map/all_to_all | solution.py:118
  19.3 4.5 %multiply_reduce_fusion = (f32[32,256]{1,0:T(8,128)S(1)}, f32[32,256,128]{2,1,0:T(8,128)S(1)}) fusion(f32[1,1,32,256,128]{4,3,2,1,0:T(8,128)} %param.9, pred[32,256]{1,0:T(8,128)(4,1)S(1)} %iota_compare_fusion.10), kind=kLoop, calls=%fused_computation.8 | loop fusion | flops 3137536 | bytes 8429568 | tf_op jit(solution)/shard_map/reduce_sum | solution.py:112
  26.5 7.1 %all-to-all-start.2 = ((f32[32,128,128]{2,1,0:T(8,128)}), f32[32,128,128]{2,1,0:T(8,128)S(1)}, u32[]{:S(2)}, u32[]{:S(2)}) async-start(f32[32,128,128]{2,1,0:T(8,128)} %get-tuple-element.12), calls=%async_computation.2 | async-start | bytes 4194304 | tf_op jit(solution)/shard_map/all_to_all | solution.py:102
  34.5 4.8 %fusion.42 = f32[4096,128]{1,0:T(8,128)} fusion(f32[64,4096]{1,0:T(8,128)S(1)} %copy-done.5, f32[128,64]{0,1:T(8,128)S(1)} %copy-done), kind=kOutput, calls=%fused_computation.61 | convolution fusion | flops 402653184 | bytes 3178496 | tf_op jit(solution)/shard_map/dot_general | solution.py:106
  39.3 22.1 %all-to-all-done.2 = f32[32,128,128]{2,1,0:T(8,128)S(1)} async-done(((f32[32,128,128]{2,1,0:T(8,128)}), f32[32,128,128]{2,1,0:T(8,128)S(1)}, u32[]{:S(2)}, u32[]{:S(2)}) %all-to-all-start.2) | async-done | bytes 2097184 | tf_op jit(solution)/shard_map/all_to_all | solution.py:102
  62.7 6.7 %all-to-all-start.1 = ((f32[32,128,128]{2,1,0:T(8,128)}), f32[32,128,128]{2,1,0:T(8,128)}, u32[]{:S(2)}, u32[]{:S(2)}) async-start(f32[32,128,128]{2,1,0:T(8,128)} %get-tuple-element.13), calls=%async_computation.1 | async-start | bytes 4194304 | tf_op jit(solution)/shard_map/all_to_all | solution.py:102
  72.4 12.6 %shard_map.86.init_ref = f32[4096,128]{1,0:T(8,128)} custom-call(s32[4096]{0:T(1024)} %get-tuple-element.18.idx_ref, f32[4096]{0:T(1024)} %get-tuple-element.16.xs_ref, f32[4096,128]{1,0:T(8,128)} %bitcast.56, f32[4096,128]{1,0:T(8,128)} %broadcast_6_init_ref.2.init_ref), custom_call_target="tpu_custom_call" | custom-call | tf_op jit(solution)/shard_map/pallas_call | solution.py:56
  84.9 12.5 %all-to-all-done.1 = f32[32,128,128]{2,1,0:T(8,128)} async-done(((f32[32,128,128]{2,1,0:T(8,128)}), f32[32,128,128]{2,1,0:T(8,128)}, u32[]{:S(2)}, u32[]{:S(2)}) %all-to-all-start.1) | async-done | bytes 2097184 | tf_op jit(solution)/shard_map/all_to_all | solution.py:102
  97.5 4.3 %all-reduce.9.cloned.1.call-done = (f32[128,128]{1,0:T(8,128)}, f32[4096,128]{1,0:T(8,128)}) async-done(((f32[128,128]{1,0:T(8,128)}, f32[4096,128]{1,0:T(8,128)}), (f32[128,128]{1,0:T(8,128)}, f32[4096,128]{1,0:T(8,128)})) %all-reduce.9.cloned.1.call-update) | async-done | bytes 2162704 | tf_op jit(solution)/shard_map/psum | solution.py:105
  101.7 12.6 %shard_map.87 = f32[4096,128]{1,0:T(8,128)} custom-call(s32[4096]{0:T(1024)} %get-tuple-element.19.idx_ref, f32[4096]{0:T(1024)} %get-tuple-element.17.xs_ref, f32[4096,128]{1,0:T(8,128)} %bitcast.6.feat_ref, f32[4096,128]{1,0:T(8,128)} %shard_map.86.init_ref), custom_call_target="tpu_custom_call" | custom-call | tf_op jit(solution)/shard_map/pallas_call | solution.py:56
  119.8 53.3 %all-reduce.5.cloned.1.call-done = f32[4096,128]{1,0:T(8,128)} async-done(((f32[4096,128]{1,0:T(8,128)}), f32[4096,128]{1,0:T(8,128)}) %all-reduce.5.cloned.1.call-update) | async-done | bytes 2097168 | tf_op jit(solution)/shard_map/psum | solution.py:125
  173.1 5.3 %convolution_subtract_fusion.1.table_ref = f32[4096,128]{1,0:T(8,128)} fusion(f32[4096,128]{1,0:T(8,128)} %get-tuple-element.7, f32[4096,128]{1,0:T(8,128)} %all-reduce.5.cloned.1.call-done, f32[128,128]{1,0:T(8,128)S(1)} %copy-done.6), kind=kOutput, calls=%fused_computation.3 | convolution fusion | flops 805830656 | bytes 6356992 | tf_op jit(solution)/shard_map/dot_general | solution.py:130
  178.4 16.7 %shard_map.88 = f32[8192,1]{1,0:T(8,128)} custom-call(s32[8192]{0:T(1024)} %bitcast.58, f32[4096,128]{1,0:T(8,128)} %convolution_subtract_fusion.1.table_ref, f32[8192,128]{1,0:T(8,128)} %bitcast.54), custom_call_target="tpu_custom_call" | custom-call | tf_op jit(solution)/shard_map/pallas_call | solution.py:79
  195.2 4.0 %reduce = f32[8192]{0:T(1024)} reduce(f32[8192,1]{1,0:T(8,128)} %shard_map.88, f32[]{:T(128)} %constant.43), dimensions={1}, to_apply=%pallas_call.20.reduce_sub_computation | reduce | bytes 65540 | tf_op jit(solution)/shard_map/pallas_call | solution.py:79
  199.1 7.7 %all-to-all-start.3 = ((f32[32,1,256]{2,1,0:T(1,128)}), f32[32,1,256]{2,1,0:T(1,128)S(1)}, u32[]{:S(2)}, u32[]{:S(2)}) async-start(f32[32,1,256]{2,1,0:T(1,128)} %bitcast.19), calls=%async_computation.3 | async-start | bytes 65536 | tf_op jit(solution)/shard_map/all_to_all | solution.py:132
  208.3 5.8 %all-to-all-done.3 = f32[32,1,256]{2,1,0:T(1,128)S(1)} async-done(((f32[32,1,256]{2,1,0:T(1,128)}), f32[32,1,256]{2,1,0:T(1,128)S(1)}, u32[]{:S(2)}, u32[]{:S(2)}) %all-to-all-start.3) | async-done | bytes 32800 | tf_op jit(solution)/shard_map/all_to_all | solution.py:132
  216.9 10.7 %all_to_all.54 = f32[32,1,256]{2,1,0:T(1,128)S(1)} all-to-all(f32[32,1,256]{2,1,0:T(1,128)S(1)} %bitcast.70), channel_id=1, replica_groups=mesh['space'=32,'shell'=4] {'space'}, dimensions={0} | all-to-all | bytes 65536 | tf_op jit(solution)/shard_map/all_to_all | solution.py:118
  228.2 12.6 %shard_map.89.init_ref = f32[4096,128]{1,0:T(8,128)} custom-call(s32[4096]{0:T(1024)} %get-tuple-element.18.idx_ref, f32[4096]{0:T(1024)} %get-tuple-element.14.xs_ref, f32[4096,128]{1,0:T(8,128)} %bitcast.57, f32[4096,128]{1,0:T(8,128)} %broadcast_6_init_ref.2.init_ref), custom_call_target="tpu_custom_call" | custom-call | tf_op jit(solution)/shard_map/pallas_call | solution.py:56
  240.8 12.6 %shard_map.90 = f32[4096,128]{1,0:T(8,128)} custom-call(s32[4096]{0:T(1024)} %get-tuple-element.19.idx_ref, f32[4096]{0:T(1024)} %get-tuple-element.15.xs_ref, f32[4096,128]{1,0:T(8,128)} %bitcast.6.feat_ref, f32[4096,128]{1,0:T(8,128)} %shard_map.89.init_ref), custom_call_target="tpu_custom_call" | custom-call | tf_op jit(solution)/shard_map/pallas_call | solution.py:56
  253.4 54.9 %all-reduce.7.cloned.1.call-done = f32[4096,128]{1,0:T(8,128)} async-done(((f32[4096,128]{1,0:T(8,128)}), f32[4096,128]{1,0:T(8,128)}) %all-reduce.7.cloned.1.call-update) | async-done | bytes 2097168 | tf_op jit(solution)/shard_map/psum | solution.py:125
  308.3 4.7 %convolution_subtract_fusion.table_ref = f32[4096,128]{1,0:T(8,128)} fusion(f32[4096,128]{1,0:T(8,128)S(1)} %copy-done.3, f32[4096,128]{1,0:T(8,128)} %all-reduce.7.cloned.1.call-done, f32[128,128]{1,0:T(8,128)S(1)} %copy-done.6), kind=kOutput, calls=%fused_computation.2 | convolution fusion | flops 805830656 | bytes 6356992 | tf_op jit(solution)/shard_map/dot_general | solution.py:130
  313.1 16.7 %shard_map.91 = f32[8192,1]{1,0:T(8,128)} custom-call(s32[8192]{0:T(1024)} %bitcast.59, f32[4096,128]{1,0:T(8,128)} %convolution_subtract_fusion.table_ref, f32[8192,128]{1,0:T(8,128)} %bitcast.55), custom_call_target="tpu_custom_call" | custom-call | tf_op jit(solution)/shard_map/pallas_call | solution.py:79
  329.8 4.1 %reduce.1 = f32[8192]{0:T(1024)} reduce(f32[8192,1]{1,0:T(8,128)} %shard_map.91, f32[]{:T(128)} %constant.43), dimensions={1}, to_apply=%pallas_call.23.reduce_sub_computation | reduce | bytes 65540 | tf_op jit(solution)/shard_map/pallas_call | solution.py:79
  333.9 7.5 %all-to-all-start.5 = ((f32[32,1,256]{2,1,0:T(1,128)}), f32[32,1,256]{2,1,0:T(1,128)S(1)}, u32[]{:S(2)}, u32[]{:S(2)}) async-start(f32[32,1,256]{2,1,0:T(1,128)} %bitcast.20), calls=%async_computation.5 | async-start | bytes 65536 | tf_op jit(solution)/shard_map/all_to_all | solution.py:132
  (54 shorter events, 31.2 us)
Async XLA Ops:
  7.2 26.5 %copy-start = (f32[128,64]{0,1:T(8,128)S(1)}, f32[128,64]{0,1:T(8,128)}, u32[]{:S(2)}) copy-start(f32[128,64]{0,1:T(8,128)} %param.12) | copy-start | bytes 98308
  7.2 12.0 %copy-start.9 = (s32[1,1,32]{2,1,0:T(1,128)S(1)}, s32[1,1,32]{2,1,0:T(1,128)}, u32[]{:S(2)}) copy-start(s32[1,1,32]{2,1,0:T(1,128)} %param.10) | copy-start | bytes 388
  10.6 15.8 %all-to-all-start = ((f32[32,1,256]{2,1,0:T(1,128)}), f32[32,1,256]{2,1,0:T(1,128)S(1)}, u32[]{:S(2)}, u32[]{:S(2)}) async-start(f32[32,1,256]{2,1,0:T(1,128)} %bitcast.4), calls=%async_computation | async-start | bytes 65536 | tf_op jit(solution)/shard_map/all_to_all | solution.py:118
  26.5 8.1 %copy-start.5 = (f32[64,4096]{1,0:T(8,128)S(1)}, f32[64,4096]{1,0:T(8,128)}, u32[]{:S(2)}) copy-start(f32[64,4096]{1,0:T(8,128)} %param.13) | copy-start | bytes 3145732
  26.5 34.9 %all-to-all-start.2 = ((f32[32,128,128]{2,1,0:T(8,128)}), f32[32,128,128]{2,1,0:T(8,128)S(1)}, u32[]{:S(2)}, u32[]{:S(2)}) async-start(f32[32,128,128]{2,1,0:T(8,128)} %get-tuple-element.12), calls=%async_computation.2 | async-start | bytes 4194304 | tf_op jit(solution)/shard_map/all_to_all | solution.py:102
  33.6 68.2 %all-reduce.9.cloned.1.call-start = ((), (), s32[]{:S(2)}) async-start(), calls=%async_computation.8 | async-start | bytes 4325376 | tf_op jit(solution)/shard_map/psum | solution.py:105
  61.4 1.3 copy-start.1
  61.4 8.3 %copy-start.7 = (s32[1,1,32,256]{3,2,1,0:T(8,128)S(1)}, s32[1,1,32,256]{3,2,1,0:T(8,128)}, u32[]{:S(2)}) copy-start(s32[1,1,32,256]{3,2,1,0:T(8,128)} %param.11) | copy-start | bytes 98308
  62.7 34.7 %all-to-all-start.1 = ((f32[32,128,128]{2,1,0:T(8,128)}), f32[32,128,128]{2,1,0:T(8,128)}, u32[]{:S(2)}, u32[]{:S(2)}) async-start(f32[32,128,128]{2,1,0:T(8,128)} %get-tuple-element.13), calls=%async_computation.1 | async-start | bytes 4194304 | tf_op jit(solution)/shard_map/all_to_all | solution.py:102
  69.5 103.6 %all-reduce.5.cloned.1.call-start = ((), (), s32[]{:S(2)}) async-start(), calls=%async_computation.6 | async-start | bytes 4194304 | tf_op jit(solution)/shard_map/psum | solution.py:125
  114.3 1.6 copy-start.2
  115.9 57.2 %copy-start.6 = (f32[128,128]{1,0:T(8,128)S(1)}, f32[128,128]{1,0:T(8,128)}, u32[]{:S(2)}) copy-start(f32[128,128]{1,0:T(8,128)} %get-tuple-element.6) | copy-start | bytes 196612
  199.1 16.4 %copy-start.8 = (f32[2048]{0:T(1024)S(1)}, f32[2048]{0:T(1024)}, u32[]{:S(2)}) copy-start(f32[2048]{0:T(1024)} %param.7) | copy-start | bytes 24580
  199.1 14.9 %all-to-all-start.3 = ((f32[32,1,256]{2,1,0:T(1,128)}), f32[32,1,256]{2,1,0:T(1,128)S(1)}, u32[]{:S(2)}, u32[]{:S(2)}) async-start(f32[32,1,256]{2,1,0:T(1,128)} %bitcast.19), calls=%async_computation.3 | async-start | bytes 65536 | tf_op jit(solution)/shard_map/all_to_all | solution.py:132
  206.8 101.5 %all-reduce.7.cloned.1.call-start = ((), (), s32[]{:S(2)}) async-start(), calls=%async_computation.7 | async-start | bytes 4194304 | tf_op jit(solution)/shard_map/psum | solution.py:125
  253.4 55.0 %copy-start.3 = (f32[4096,128]{1,0:T(8,128)S(1)}, f32[4096,128]{1,0:T(8,128)}, u32[]{:S(2)}) copy-start(f32[4096,128]{1,0:T(8,128)} %get-tuple-element.7) | copy-start | bytes 6291460
  329.8 11.6 %copy-start.4 = (f32[4096,128]{1,0:T(8,128)S(1)}, f32[4096,128]{1,0:T(8,128)}, u32[]{:S(2)}) copy-start(f32[4096,128]{1,0:T(8,128)} %all-reduce.7.cloned.1.call-done) | copy-start | bytes 6291460
  333.9 14.8 %all-to-all-start.5 = ((f32[32,1,256]{2,1,0:T(1,128)}), f32[32,1,256]{2,1,0:T(1,128)S(1)}, u32[]{:S(2)}, u32[]{:S(2)}) async-start(f32[32,1,256]{2,1,0:T(1,128)} %bitcast.20), calls=%async_computation.5 | async-start | bytes 65536 | tf_op jit(solution)/shard_map/all_to_all | solution.py:132
Sparse Core Ops, SparseCore 0:
  39.5 62.2 all-reduce.8
  114.4 58.6 all-reduce.4
  253.5 54.7 all-reduce.6

commit v4 on v3

--- a/solution.py
+++ b/solution.py
@@ -97,37 +97,54 @@
     masked = jnp.where(
         live_slot[:, :, None], seg_features.reshape(blocks, slots, coeffs), jnp.float32(0.0)
     )
+    high, low = one_hot_pair(stream_index, streams)
+    column_sq = spread(jnp.sum(masked * masked, axis=2), high, low)
+    scaling = 0.5 / (0.5 + column_sq)
     half = slots // 2
+    picked = pick(weights, high, low).reshape(blocks, slots // coeffs, coeffs)
+    pad_rows = 8 - slots // coeffs
+    first = jnp.concatenate(
+        [masked[:, :half], picked, jnp.zeros((blocks, pad_rows, coeffs), jnp.float32)], axis=1
+    )
+    first = lax.all_to_all(first, "space", 0, 0, tiled=True)
     feat_parts = [
-        lax.all_to_all(masked[:, h * half:(h + 1) * half], "space", 0, 0, tiled=True)
-        for h in range(2)
+        first[:, :half],
+        lax.all_to_all(masked[:, half:], "space", 0, 0, tiled=True),
     ]
+    local_x = first[:, half:half + slots // coeffs].reshape(blocks, slots)
     gram = lax.psum(jnp.dot(dictionary, dictionary.T, precision=HI), "shell")
-    data_proj = lax.psum(jnp.dot(measured.T, dictionary.T, precision=HI), "shell")
-    feat_parts[1], gram, data_proj = lax.optimization_barrier((feat_parts[1], gram, data_proj))
+    shell_proj = jnp.dot(measured.T, dictionary.T, precision=HI)
     vox_parts = [voxel_index.reshape(blocks, slots)[:, h * half:(h + 1) * half].reshape(-1)
                  for h in range(2)]
     local_feat = jnp.concatenate(feat_parts, axis=1).reshape(blocks * slots, coeffs)
-    high, low = one_hot_pair(stream_index, streams)
-    column_sq = spread(jnp.sum(masked * masked, axis=2), high, low)
-    scaling = 0.5 / (0.5 + column_sq)
     current = weights
     residual = jnp.zeros(measured.shape, jnp.float32)
+    data_proj = None
     for iteration in range(ITERS):
-        picked = pick(current, high, low).reshape(blocks, slots)
-        local_x = lax.all_to_all(picked, "space", split_axis=0, concat_axis=0, tiled=True)
+        if iteration > 0:
+            picked = pick(current, high, low).reshape(blocks, slots)
+            local_x = lax.all_to_all(picked, "space", split_axis=0, concat_axis=0, tiled=True)
+            if data_proj is not None:
+                data_proj, local_x = lax.optimization_barrier((data_proj, local_x))
         partial_coeff = jnp.zeros((measured.shape[1], coeffs), jnp.float32)
         for h in range(2):
             part_x = local_x[:, h * half:(h + 1) * half].reshape(-1)
             partial_coeff = row_scatter(
                 vox_parts[h], part_x, feat_parts[h].reshape(-1, coeffs), partial_coeff
             )
-        coeff_sum = lax.psum(partial_coeff, "shell")
-        if iteration == ITERS - 1:
+        if iteration < ITERS - 1:
+            adjoint = lax.psum(jnp.dot(partial_coeff, gram, precision=HI) - shell_proj, "shell")
+            if data_proj is None:
+                shell_proj, adjoint = lax.optimization_barrier((shell_proj, adjoint))
+                data_proj = lax.psum(shell_proj, "shell")
+        else:
+            coeff_sum = lax.psum(partial_coeff, "shell")
             residual = (
                 jnp.einsum("jg,vj->gv", dictionary, coeff_sum, precision=HI) - measured
             )
-        adjoint = jnp.dot(coeff_sum, gram, precision=HI) - data_proj
+            if data_proj is None:
+                data_proj = lax.psum(shell_proj, "shell")
+            adjoint = jnp.dot(coeff_sum, gram, precision=HI) - data_proj
         local_grad = row_gather_dot(voxel_index, adjoint, local_feat).reshape(blocks, slots)
         grad_slot = lax.all_to_all(local_grad, "space", split_axis=0, concat_axis=0, tiled=True)
         gradient = spread(grad_slot, high, low)

time: 358 us -> 367 us (1.025)
  blocking collectives: 10.7 us -> 49.4 us
  starting transfers between devices: 37.9 us -> 19.7 us
  waiting for transfers between devices: 157 us -> 143 us
    psum x0 -> x2, waiting for transfers between devices: none -> 68.4 us  [the longest x1 61.2 us: on_device(): lax.psum(jnp.dot(partial_coeff, gram, precision=HI) - shell_proj, 'shell')]
    psum x2 -> x1, waiting for transfers between devices: 108 us -> 58.8 us  [on_device(): coeff_sum = lax.psum(partial_coeff, 'shell')]
    all_to_all x0 -> x1, blocking collectives: none -> 38.6 us  [on_device(): first = lax.all_to_all(first, 'space', 0, 0, tiled=True)]
    all_to_all x3 -> x1, waiting for transfers between devices: 35 us -> 2.75 us  [on_device(): lax.all_to_all(masked[:, half:], 'space', 0, 0, tiled=True)]
    all_to_all x3 -> x1, starting transfers between devices: 22.4 us -> 4.18 us  [on_device(): lax.all_to_all(masked[:, half:], 'space', 0, 0, tiled=True)]
    dot_general x1 -> x2, matrix products: 4.77 us -> 10.2 us  [the longest x1 5.4 us: on_device(): jnp.dot(partial_coeff, gram, precision=HI) - shell_proj]
    dot_general x2 -> x1, matrix products: 10.1 us -> 4.72 us  [on_device(): adjoint = jnp.dot(coeff_sum, gram, precision=HI) - data_proj]
  transfers between devices with their start and end apart: 8 -> 7, of which waited for: 8 -> 7; matrix products, arithmetic and copies ran while one was open for 7% -> 8% of each run, Pallas kernels for 4% -> 11%
where the time goes in v4:
time: 367 us; the launch traced here: 366 us
  waiting for transfers between devices  143 us (39%)
  Pallas kernels  83.7 us (23%)
  blocking collectives  49.4 us (13%)
  matrix products  25.9 us (7%)
  starting transfers between devices  19.7 us (5%)
  other arithmetic  18.1 us (5%)
  between operations  13.9 us (4%)
  local copies, waits for them, and re-layouts  13 us (4%)
    psum x1, waiting for transfers between devices, on_device(): lax.psum(jnp.dot(partial_coeff, gram, precision=HI) - shell_proj, 'shell')  61.2 us
    psum x1, waiting for transfers between devices, on_device(): coeff_sum = lax.psum(partial_coeff, 'shell')  58.8 us
    pallas_call x4, Pallas kernels, row_scatter(): pl.pallas_call(scatter_kernel, out_shape=jax.ShapeDtypeStruct(init.shape,...  50.2 us
    all_to_all x1, blocking collectives, on_device(): first = lax.all_to_all(first, 'space', 0, 0, tiled=True)  38.6 us
    pallas_call x2, Pallas kernels, row_gather_dot(): pl.pallas_call(gather_kernel, out_shape=jax.ShapeDtypeStruct((feat.shape[...  33.5 us
    all_to_all x2, starting transfers between devices, on_device(): lax.all_to_all(local_grad, 'space', split_axis=0, concat_axis=0, tiled=True)  15.2 us
    all_to_all x1, blocking collectives, on_device(): lax.all_to_all(picked, 'space', split_axis=0, concat_axis=0, tiled=True)  10.7 us
    all_to_all x2, waiting for transfers between devices, on_device(): lax.all_to_all(local_grad, 'space', split_axis=0, concat_axis=0, tiled=True)  9.62 us
  transfers between devices with their start and end apart: 7, of which 7 were waited for; matrix products, arithmetic and copies ran while one was open for 8% of the time, Pallas kernels for 11%

profile of v4, /device:TPU:1, one launch (start us, length us, event | category | flops | bytes accessed | tf_op | source)
XLA Modules:
  0.0 366.4 jit_solution(15741188811887373022)
XLA Ops:
  9.5 4.5 %multiply_reduce_fusion = (f32[32,256]{1,0:T(8,128)S(1)}, f32[32,256,128]{2,1,0:T(8,128)S(1)}) fusion(f32[1,1,32,256,128]{4,3,2,1,0:T(8,128)} %param.9, pred[32,256]{1,0:T(8,128)(4,1)S(1)} %iota_compare_fusion.10), kind=kLoop, calls=%fused_computation.8 | loop fusion | flops 3137536 | bytes 8429568 | tf_op jit(solution)/shard_map/reduce_sum | solution.py:101
  17.3 38.6 %all_to_all.42 = f32[32,136,128]{2,1,0:T(8,128)} all-to-all(f32[32,136,128]{2,1,0:T(8,128)S(1)} %maximum_maximum_fusion), channel_id=1, replica_groups=mesh['space'=32,'shell'=4] {'space'}, dimensions={0} | all-to-all | bytes 4456448 | tf_op jit(solution)/shard_map/all_to_all | solution.py:109
  55.9 4.2 %all-to-all-start.1 = ((f32[32,128,128]{2,1,0:T(8,128)}), f32[32,128,128]{2,1,0:T(8,128)S(1)}, u32[]{:S(2)}, u32[]{:S(2)}) async-start(f32[32,128,128]{2,1,0:T(8,128)} %get-tuple-element.12), calls=%async_computation.1 | async-start | bytes 4194304 | tf_op jit(solution)/shard_map/all_to_all | solution.py:112
  61.8 4.8 %fusion.41 = f32[4096,128]{1,0:T(8,128)} fusion(f32[64,4096]{1,0:T(8,128)S(1)} %copy-done.4, f32[128,64]{0,1:T(8,128)S(1)} %copy-done), kind=kOutput, calls=%fused_computation.61 | convolution fusion | flops 402653184 | bytes 3178496 | tf_op jit(solution)/shard_map/dot_general | solution.py:116
  72.7 12.6 %shard_map.86.init_ref = f32[4096,128]{1,0:T(8,128)} custom-call(s32[4096]{0:T(1024)} %get-tuple-element.18.idx_ref, f32[4096]{0:T(1024)} %get-tuple-element.16.xs_ref, f32[4096,128]{1,0:T(8,128)} %bitcast.59, f32[4096,128]{1,0:T(8,128)} %broadcast_6_init_ref.2.init_ref), custom_call_target="tpu_custom_call" | custom-call | tf_op jit(solution)/shard_map/pallas_call | solution.py:56
  89.4 12.5 %shard_map.87 = f32[4096,128]{1,0:T(8,128)} custom-call(s32[4096]{0:T(1024)} %get-tuple-element.19.idx_ref, f32[4096]{0:T(1024)} %get-tuple-element.17.xs_ref, f32[4096,128]{1,0:T(8,128)} %bitcast.57, f32[4096,128]{1,0:T(8,128)} %shard_map.86.init_ref), custom_call_target="tpu_custom_call" | custom-call | tf_op jit(solution)/shard_map/pallas_call | solution.py:56
  105.1 5.4 %convolution_subtract_fusion.1 = f32[4096,128]{1,0:T(8,128)} fusion(f32[4096,128]{1,0:T(8,128)} %fusion.41, f32[4096,128]{1,0:T(8,128)} %shard_map.87, f32[128,128]{1,0:T(8,128)} %all-reduce.5.cloned.1.call-done), kind=kOutput, calls=%fused_computation.3 | convolution fusion | flops 805830656 | bytes 6356992 | tf_op jit(solution)/shard_map/dot_general | solution.py:136
  110.7 61.2 %all-reduce.7.cloned.1.call-done.table_ref = f32[4096,128]{1,0:T(8,128)} async-done(((f32[4096,128]{1,0:T(8,128)}), f32[4096,128]{1,0:T(8,128)}) %all-reduce.7.cloned.1.call-update) | async-done | bytes 2097168 | tf_op jit(solution)/shard_map/psum | solution.py:136
  172.6 3.9 %pad_maximum_fusion = f32[32,256,128]{2,1,0:T(8,128)} fusion(f32[32,128,128]{2,1,0:T(8,128)S(1)} %copy-done.2, f32[32,128,128]{2,1,0:T(8,128)} %slice.47), kind=kLoop, calls=%fused_computation.6 | loop fusion | flops 1048576 | bytes 8388608 | tf_op jit(solution)/shard_map/concatenate | solution.py:119
  176.5 16.7 %shard_map.88 = f32[8192,1]{1,0:T(8,128)} custom-call(s32[8192]{0:T(1024)} %bitcast.61, f32[4096,128]{1,0:T(8,128)} %all-reduce.7.cloned.1.call-done.table_ref, f32[8192,128]{1,0:T(8,128)} %bitcast.55), custom_call_target="tpu_custom_call" | custom-call | tf_op jit(solution)/shard_map/pallas_call | solution.py:79
  193.2 4.0 %reduce = f32[8192]{0:T(1024)} reduce(f32[8192,1]{1,0:T(8,128)} %shard_map.88, f32[]{:T(128)} %constant.44), dimensions={1}, to_apply=%pallas_call.20.reduce_sub_computation | reduce | bytes 65540 | tf_op jit(solution)/shard_map/pallas_call | solution.py:79
  197.2 7.7 %all-to-all-start.2 = ((f32[32,1,256]{2,1,0:T(1,128)}), f32[32,1,256]{2,1,0:T(1,128)S(1)}, u32[]{:S(2)}, u32[]{:S(2)}) async-start(f32[32,1,256]{2,1,0:T(1,128)} %bitcast.18), calls=%async_computation.2 | async-start | bytes 65536 | tf_op jit(solution)/shard_map/all_to_all | solution.py:149
  206.4 5.8 %all-to-all-done.2 = f32[32,1,256]{2,1,0:T(1,128)S(1)} async-done(((f32[32,1,256]{2,1,0:T(1,128)}), f32[32,1,256]{2,1,0:T(1,128)S(1)}, u32[]{:S(2)}, u32[]{:S(2)}) %all-to-all-start.2) | async-done | bytes 32800 | tf_op jit(solution)/shard_map/all_to_all | solution.py:149
  215.0 10.7 %all_to_all.43 = f32[32,1,256]{2,1,0:T(1,128)S(1)} all-to-all(f32[32,1,256]{2,1,0:T(1,128)S(1)} %bitcast.75), channel_id=1, replica_groups=mesh['space'=32,'shell'=4] {'space'}, dimensions={0} | all-to-all | bytes 65536 | tf_op jit(solution)/shard_map/all_to_all | solution.py:126
  225.7 7.2 %all-reduce.9.cloned.1.call-done = f32[4096,128]{1,0:T(8,128)} async-done(((f32[4096,128]{1,0:T(8,128)}), f32[4096,128]{1,0:T(8,128)}) %all-reduce.9.cloned.1.call-update) | async-done | bytes 2097168 | tf_op jit(solution)/shard_map/psum | solution.py:139
  233.5 12.5 %shard_map.89.init_ref = f32[4096,128]{1,0:T(8,128)} custom-call(s32[4096]{0:T(1024)} %get-tuple-element.18.idx_ref, f32[4096]{0:T(1024)} %get-tuple-element.14.xs_ref, f32[4096,128]{1,0:T(8,128)} %bitcast.60, f32[4096,128]{1,0:T(8,128)} %broadcast_6_init_ref.2.init_ref), custom_call_target="tpu_custom_call" | custom-call | tf_op jit(solution)/shard_map/pallas_call | solution.py:56
  246.0 12.6 %shard_map.90 = f32[4096,128]{1,0:T(8,128)} custom-call(s32[4096]{0:T(1024)} %get-tuple-element.19.idx_ref, f32[4096]{0:T(1024)} %get-tuple-element.15.xs_ref, f32[4096,128]{1,0:T(8,128)} %bitcast.58, f32[4096,128]{1,0:T(8,128)} %shard_map.89.init_ref), custom_call_target="tpu_custom_call" | custom-call | tf_op jit(solution)/shard_map/pallas_call | solution.py:56
  258.7 58.8 %all-reduce.11.cloned.1.call-done = f32[4096,128]{1,0:T(8,128)} async-done(((f32[4096,128]{1,0:T(8,128)}), f32[4096,128]{1,0:T(8,128)}) %all-reduce.11.cloned.1.call-update) | async-done | bytes 2097168 | tf_op jit(solution)/shard_map/psum | solution.py:141
  317.5 4.7 %convolution_subtract_fusion.table_ref = f32[4096,128]{1,0:T(8,128)} fusion(f32[4096,128]{1,0:T(8,128)S(1)} %copy-done.5, f32[4096,128]{1,0:T(8,128)} %all-reduce.11.cloned.1.call-done, f32[128,128]{1,0:T(8,128)S(1)} %copy-done.6), kind=kOutput, calls=%fused_computation.2 | convolution fusion | flops 805830656 | bytes 6356992 | tf_op jit(solution)/shard_map/dot_general | solution.py:147
  322.2 16.7 %shard_map.91 = f32[8192,1]{1,0:T(8,128)} custom-call(s32[8192]{0:T(1024)} %bitcast.62, f32[4096,128]{1,0:T(8,128)} %convolution_subtract_fusion.table_ref, f32[8192,128]{1,0:T(8,128)} %bitcast.56), custom_call_target="tpu_custom_call" | custom-call | tf_op jit(solution)/shard_map/pallas_call | solution.py:79
  338.9 4.1 %reduce.1 = f32[8192]{0:T(1024)} reduce(f32[8192,1]{1,0:T(8,128)} %shard_map.91, f32[]{:T(128)} %constant.44), dimensions={1}, to_apply=%pallas_call.23.reduce_sub_computation | reduce | bytes 65540 | tf_op jit(solution)/shard_map/pallas_call | solution.py:79
  343.0 7.5 %all-to-all-start.4 = ((f32[32,1,256]{2,1,0:T(1,128)}), f32[32,1,256]{2,1,0:T(1,128)S(1)}, u32[]{:S(2)}, u32[]{:S(2)}) async-start(f32[32,1,256]{2,1,0:T(1,128)} %bitcast.19), calls=%async_computation.4 | async-start | bytes 65536 | tf_op jit(solution)/shard_map/all_to_all | solution.py:149
  350.6 3.4 fusion
  353.9 3.9 %all-to-all-done.4 = f32[32,1,256]{2,1,0:T(1,128)S(1)} async-done(((f32[32,1,256]{2,1,0:T(1,128)}), f32[32,1,256]{2,1,0:T(1,128)S(1)}, u32[]{:S(2)}, u32[]{:S(2)}) %all-to-all-start.4) | async-done | bytes 32800 | tf_op jit(solution)/shard_map/all_to_all | solution.py:149
  (57 shorter events, 28.5 us)
Async XLA Ops:
  7.2 53.0 %copy-start = (f32[128,64]{0,1:T(8,128)S(1)}, f32[128,64]{0,1:T(8,128)}, u32[]{:S(2)}) copy-start(f32[128,64]{0,1:T(8,128)} %param.12) | copy-start | bytes 98308
  55.9 5.2 %copy-start.7 = (s32[1,1,32,256]{3,2,1,0:T(8,128)S(1)}, s32[1,1,32,256]{3,2,1,0:T(8,128)}, u32[]{:S(2)}) copy-start(s32[1,1,32,256]{3,2,1,0:T(8,128)} %param.11) | copy-start | bytes 98308
  55.9 5.9 %copy-start.4 = (f32[64,4096]{1,0:T(8,128)S(1)}, f32[64,4096]{1,0:T(8,128)}, u32[]{:S(2)}) copy-start(f32[64,4096]{1,0:T(8,128)} %param.13) | copy-start | bytes 3145732
  55.9 32.1 %all-to-all-start.1 = ((f32[32,128,128]{2,1,0:T(8,128)}), f32[32,128,128]{2,1,0:T(8,128)S(1)}, u32[]{:S(2)}, u32[]{:S(2)}) async-start(f32[32,128,128]{2,1,0:T(8,128)} %get-tuple-element.12), calls=%async_computation.1 | async-start | bytes 4194304 | tf_op jit(solution)/shard_map/all_to_all | solution.py:112
  60.1 44.9 %all-reduce.5.cloned.1.call-start = ((), (), s32[]{:S(2)}) async-start(), calls=%async_computation.5 | async-start | bytes 131072 | tf_op jit(solution)/shard_map/psum | solution.py:115
  61.1 110.8 %all-reduce.7.cloned.1.call-start = ((), (), s32[]{:S(2)}) async-start(), calls=%async_computation.6 | async-start | bytes 4194304 | tf_op jit(solution)/shard_map/psum | solution.py:136
  88.1 1.3 copy-start.1
  110.5 62.1 %copy-start.2 = (f32[32,128,128]{2,1,0:T(8,128)S(1)}, f32[32,128,128]{2,1,0:T(8,128)}, u32[]{:S(2)}) copy-start(f32[32,128,128]{2,1,0:T(8,128)} %copy-done.1) | copy-start | bytes 6291460
  110.5 122.4 %all-reduce.9.cloned.1.call-start = ((), (), s32[]{:S(2)}) async-start(), calls=%async_computation.7 | async-start | bytes 4194304 | tf_op jit(solution)/shard_map/psum | solution.py:139
  197.2 16.4 %copy-start.8 = (f32[2048]{0:T(1024)S(1)}, f32[2048]{0:T(1024)}, u32[]{:S(2)}) copy-start(f32[2048]{0:T(1024)} %param.7) | copy-start | bytes 24580
  197.2 14.9 %all-to-all-start.2 = ((f32[32,1,256]{2,1,0:T(1,128)}), f32[32,1,256]{2,1,0:T(1,128)S(1)}, u32[]{:S(2)}, u32[]{:S(2)}) async-start(f32[32,1,256]{2,1,0:T(1,128)} %bitcast.18), calls=%async_computation.2 | async-start | bytes 65536 | tf_op jit(solution)/shard_map/all_to_all | solution.py:149
  204.9 112.6 %all-reduce.11.cloned.1.call-start = ((), (), s32[]{:S(2)}) async-start(), calls=%async_computation.8 | async-start | bytes 4194304 | tf_op jit(solution)/shard_map/psum | solution.py:141
  246.0 71.4 %copy-start.6 = (f32[128,128]{1,0:T(8,128)S(1)}, f32[128,128]{1,0:T(8,128)}, u32[]{:S(2)}) copy-start(f32[128,128]{1,0:T(8,128)} %all-reduce.5.cloned.1.call-done) | copy-start | bytes 196612
  258.6 58.8 %copy-start.5 = (f32[4096,128]{1,0:T(8,128)S(1)}, f32[4096,128]{1,0:T(8,128)}, u32[]{:S(2)}) copy-start(f32[4096,128]{1,0:T(8,128)} %all-reduce.9.cloned.1.call-done) | copy-start | bytes 6291460
  338.9 11.6 %copy-start.3 = (f32[4096,128]{1,0:T(8,128)S(1)}, f32[4096,128]{1,0:T(8,128)}, u32[]{:S(2)}) copy-start(f32[4096,128]{1,0:T(8,128)} %all-reduce.11.cloned.1.call-done) | copy-start | bytes 6291460
  343.0 14.8 %all-to-all-start.4 = ((f32[32,1,256]{2,1,0:T(1,128)}), f32[32,1,256]{2,1,0:T(1,128)S(1)}, u32[]{:S(2)}, u32[]{:S(2)}) async-start(f32[32,1,256]{2,1,0:T(1,128)} %bitcast.19), calls=%async_computation.4 | async-start | bytes 65536 | tf_op jit(solution)/shard_map/all_to_all | solution.py:149
Sparse Core Ops, SparseCore 0:
  63.8 41.1 all-reduce.4
  110.6 61.2 all-reduce.6
  174.3 58.5 all-reduce.8
  258.8 58.6 all-reduce.10

commit v5 on v3

--- a/solution.py
+++ b/solution.py
@@ -70,7 +70,15 @@
         return carry
 
     lax.fori_loop(0, feat_ref.shape[0] // UNROLL, body, 0)
-    out_ref[...] = jnp.sum(rows_ref[...] * feat_ref[...], axis=1, keepdims=True)
+    lanes = out_ref.shape[1]
+
+    def reduce_block(block, carry):
+        start = pl.multiple_of(block * lanes, lanes)
+        prod = rows_ref[pl.ds(start, lanes), :] * feat_ref[pl.ds(start, lanes), :]
+        out_ref[pl.ds(block, 1), :] = jnp.sum(prod.T, axis=0, keepdims=True)
+        return carry
+
+    lax.fori_loop(0, out_ref.shape[0], reduce_block, 0)
 
 
 def row_gather_dot(idx, table, feat):
@@ -78,7 +86,7 @@
     vmem = pl.BlockSpec(memory_space=pltpu.VMEM)
     return pl.pallas_call(
         gather_kernel,
-        out_shape=jax.ShapeDtypeStruct((feat.shape[0], 1), jnp.float32),
+        out_shape=jax.ShapeDtypeStruct((feat.shape[0] // 128, 128), jnp.float32),
         in_specs=[smem, vmem, vmem],
         out_specs=vmem,
         scratch_shapes=[pltpu.VMEM(feat.shape, jnp.float32)],
@@ -117,10 +125,15 @@
         picked = pick(current, high, low).reshape(blocks, slots)
         local_x = lax.all_to_all(picked, "space", split_axis=0, concat_axis=0, tiled=True)
         partial_coeff = jnp.zeros((measured.shape[1], coeffs), jnp.float32)
-        for h in range(2):
-            part_x = local_x[:, h * half:(h + 1) * half].reshape(-1)
+        if iteration == 0:
+            for h in range(2):
+                part_x = local_x[:, h * half:(h + 1) * half].reshape(-1)
+                partial_coeff = row_scatter(
+                    vox_parts[h], part_x, feat_parts[h].reshape(-1, coeffs), partial_coeff
+                )
+        else:
             partial_coeff = row_scatter(
-                vox_parts[h], part_x, feat_parts[h].reshape(-1, coeffs), partial_coeff
+                voxel_index, local_x.reshape(-1), local_feat, partial_coeff
             )
         coeff_sum = lax.psum(partial_coeff, "shell")
         if iteration == ITERS - 1:

time: 358 us -> 356 us (level)
  other arithmetic: 17.2 us -> 9.16 us
  Pallas kernels: 83.7 us -> 90.2 us
    pallas_call x2, Pallas kernels: 33.5 us -> 43.7 us  [row_gather_dot(): pl.pallas_call(gather_kernel, out_shape=jax.ShapeDtypeStruct((feat.shape[...]
    pallas_call x2 -> x0, other arithmetic: 8.05 us -> none  [row_gather_dot(): pl.pallas_call(gather_kernel, out_shape=jax.ShapeDtypeStruct((feat.shape[...]
    pallas_call x4 -> x3, Pallas kernels: 50.2 us -> 46.4 us  [row_scatter(): pl.pallas_call(scatter_kernel, out_shape=jax.ShapeDtypeStruct(init.shape,...]
where the time goes in v5:
time: 356 us
  waiting for transfers between devices  157 us (44%)
  Pallas kernels  90.2 us (25%)
  starting transfers between devices  38 us (11%)
  matrix products  26.5 us (7%)
  between operations  13.9 us (4%)
  blocking collectives  11 us (3%)
  local copies, waits for them, and re-layouts  9.76 us (3%)
  other arithmetic  9.16 us (3%)
    psum x2, waiting for transfers between devices, on_device(): coeff_sum = lax.psum(partial_coeff, 'shell')  108 us
    pallas_call x3, Pallas kernels, row_scatter(): pl.pallas_call(scatter_kernel, out_shape=jax.ShapeDtypeStruct(init.shape,...  46.4 us
    pallas_call x2, Pallas kernels, row_gather_dot(): pl.pallas_call(gather_kernel, out_shape=jax.ShapeDtypeStruct((feat.shape[...  43.7 us
    all_to_all x2, waiting for transfers between devices, on_device(): lax.all_to_all(masked[:, h * half:(h + 1) * half], 'space', 0, 0, tiled=T...  34.5 us
    all_to_all x2, starting transfers between devices, on_device(): lax.all_to_all(local_grad, 'space', split_axis=0, concat_axis=0, tiled=True)  15.2 us
    all_to_all x2, starting transfers between devices, on_device(): lax.all_to_all(masked[:, h * half:(h + 1) * half], 'space', 0, 0, tiled=T...  13.9 us
    all_to_all x1, blocking collectives, on_device(): lax.all_to_all(picked, 'space', split_axis=0, concat_axis=0, tiled=True)  11 us
    dot_general x2, matrix products, on_device(): adjoint = jnp.dot(coeff_sum, gram, precision=HI) - data_proj  10.1 us
  transfers between devices with their start and end apart: 8, of which 8 were waited for; matrix products, arithmetic and copies ran while one was open for 7% of the time, Pallas kernels for 4%

profile of v5, /device:TPU:1, one launch (start us, length us, event | category | flops | bytes accessed | tf_op | source)
XLA Modules:
  0.0 355.5 jit_solution(470351700579658914)
XLA Ops:
  10.6 8.6 %all-to-all-start = ((f32[32,1,256]{2,1,0:T(1,128)}), f32[32,1,256]{2,1,0:T(1,128)S(1)}, u32[]{:S(2)}, u32[]{:S(2)}) async-start(f32[32,1,256]{2,1,0:T(1,128)} %bitcast.4), calls=%async_computation | async-start | bytes 65536 | tf_op jit(solution)/shard_map/all_to_all | solution.py:126
  19.3 4.5 %multiply_reduce_fusion = (f32[32,256]{1,0:T(8,128)S(1)}, f32[32,256,128]{2,1,0:T(8,128)S(1)}) fusion(f32[1,1,32,256,128]{4,3,2,1,0:T(8,128)} %param.9, pred[32,256]{1,0:T(8,128)(4,1)S(1)} %iota_compare_fusion.10), kind=kLoop, calls=%fused_computation.8 | loop fusion | flops 3137536 | bytes 8429568 | tf_op jit(solution)/shard_map/reduce_sum | solution.py:120
  26.5 7.1 %all-to-all-start.2 = ((f32[32,128,128]{2,1,0:T(8,128)}), f32[32,128,128]{2,1,0:T(8,128)S(1)}, u32[]{:S(2)}, u32[]{:S(2)}) async-start(f32[32,128,128]{2,1,0:T(8,128)} %get-tuple-element.12), calls=%async_computation.2 | async-start | bytes 4194304 | tf_op jit(solution)/shard_map/all_to_all | solution.py:110
  34.6 4.8 %fusion.42 = f32[4096,128]{1,0:T(8,128)} fusion(f32[64,4096]{1,0:T(8,128)S(1)} %copy-done.5, f32[128,64]{0,1:T(8,128)S(1)} %copy-done), kind=kOutput, calls=%fused_computation.58 | convolution fusion | flops 402653184 | bytes 3178496 | tf_op jit(solution)/shard_map/dot_general | solution.py:114
  39.4 22.1 %all-to-all-done.2 = f32[32,128,128]{2,1,0:T(8,128)S(1)} async-done(((f32[32,128,128]{2,1,0:T(8,128)}), f32[32,128,128]{2,1,0:T(8,128)S(1)}, u32[]{:S(2)}, u32[]{:S(2)}) %all-to-all-start.2) | async-done | bytes 2097184 | tf_op jit(solution)/shard_map/all_to_all | solution.py:110
  62.8 6.7 %all-to-all-start.1 = ((f32[32,128,128]{2,1,0:T(8,128)}), f32[32,128,128]{2,1,0:T(8,128)}, u32[]{:S(2)}, u32[]{:S(2)}) async-start(f32[32,128,128]{2,1,0:T(8,128)} %get-tuple-element.13), calls=%async_computation.1 | async-start | bytes 4194304 | tf_op jit(solution)/shard_map/all_to_all | solution.py:110
  72.5 12.6 %shard_map.86.init_ref = f32[4096,128]{1,0:T(8,128)} custom-call(s32[4096]{0:T(1024)} %get-tuple-element.16.idx_ref, f32[4096]{0:T(1024)} %get-tuple-element.14.xs_ref, f32[4096,128]{1,0:T(8,128)} %bitcast.51, f32[4096,128]{1,0:T(8,128)} %broadcast_6_init_ref.2.init_ref), custom_call_target="tpu_custom_call" | custom-call | tf_op jit(solution)/shard_map/pallas_call | solution.py:56
  85.1 12.5 %all-to-all-done.1 = f32[32,128,128]{2,1,0:T(8,128)} async-done(((f32[32,128,128]{2,1,0:T(8,128)}), f32[32,128,128]{2,1,0:T(8,128)}, u32[]{:S(2)}, u32[]{:S(2)}) %all-to-all-start.1) | async-done | bytes 2097184 | tf_op jit(solution)/shard_map/all_to_all | solution.py:110
  97.5 4.3 %all-reduce.9.cloned.1.call-done = (f32[128,128]{1,0:T(8,128)}, f32[4096,128]{1,0:T(8,128)}) async-done(((f32[128,128]{1,0:T(8,128)}, f32[4096,128]{1,0:T(8,128)}), (f32[128,128]{1,0:T(8,128)}, f32[4096,128]{1,0:T(8,128)})) %all-reduce.9.cloned.1.call-update) | async-done | bytes 2162704 | tf_op jit(solution)/shard_map/psum | solution.py:113
  101.8 12.5 %shard_map.87 = f32[4096,128]{1,0:T(8,128)} custom-call(s32[4096]{0:T(1024)} %get-tuple-element.17.idx_ref, f32[4096]{0:T(1024)} %get-tuple-element.15.xs_ref, f32[4096,128]{1,0:T(8,128)} %bitcast.6.feat_ref, f32[4096,128]{1,0:T(8,128)} %shard_map.86.init_ref), custom_call_target="tpu_custom_call" | custom-call | tf_op jit(solution)/shard_map/pallas_call | solution.py:56
  115.9 4.0 %pad_maximum_fusion = f32[32,256,128]{2,1,0:T(8,128)} fusion(f32[32,128,128]{2,1,0:T(8,128)} %all-to-all-done.1, f32[32,128,128]{2,1,0:T(8,128)S(1)} %copy-done.2), kind=kLoop, calls=%fused_computation.6 | loop fusion | flops 1048576 | bytes 8388608 | tf_op jit(solution)/shard_map/concatenate | solution.py:118
  119.9 53.3 %all-reduce.5.cloned.1.call-done = f32[4096,128]{1,0:T(8,128)} async-done(((f32[4096,128]{1,0:T(8,128)}), f32[4096,128]{1,0:T(8,128)}) %all-reduce.5.cloned.1.call-update) | async-done | bytes 2097168 | tf_op jit(solution)/shard_map/psum | solution.py:138
  173.2 5.4 %convolution_subtract_fusion.1.table_ref = f32[4096,128]{1,0:T(8,128)} fusion(f32[4096,128]{1,0:T(8,128)} %get-tuple-element.7, f32[4096,128]{1,0:T(8,128)} %all-reduce.5.cloned.1.call-done, f32[128,128]{1,0:T(8,128)S(1)} %copy-done.6), kind=kOutput, calls=%fused_computation.3 | convolution fusion | flops 805830656 | bytes 6356992 | tf_op jit(solution)/shard_map/dot_general | solution.py:143
  178.6 21.8 %shard_map.88 = f32[64,128]{1,0:T(8,128)} custom-call(s32[8192]{0:T(1024)} %bitcast.52, f32[4096,128]{1,0:T(8,128)} %convolution_subtract_fusion.1.table_ref, f32[8192,128]{1,0:T(8,128)} %bitcast.48), custom_call_target="tpu_custom_call" | custom-call | tf_op jit(solution)/shard_map/pallas_call | solution.py:87
  200.4 7.7 %all-to-all-start.3 = ((f32[32,1,256]{2,1,0:T(1,128)}), f32[32,1,256]{2,1,0:T(1,128)S(1)}, u32[]{:S(2)}, u32[]{:S(2)}) async-start(f32[32,1,256]{2,1,0:T(1,128)} %bitcast.56), calls=%async_computation.3 | async-start | bytes 65536 | tf_op jit(solution)/shard_map/all_to_all | solution.py:145
  209.5 5.8 %all-to-all-done.3 = f32[32,1,256]{2,1,0:T(1,128)S(1)} async-done(((f32[32,1,256]{2,1,0:T(1,128)}), f32[32,1,256]{2,1,0:T(1,128)S(1)}, u32[]{:S(2)}, u32[]{:S(2)}) %all-to-all-start.3) | async-done | bytes 32800 | tf_op jit(solution)/shard_map/all_to_all | solution.py:145
  218.1 11.0 %all_to_all.49 = f32[32,1,256]{2,1,0:T(1,128)} all-to-all(f32[32,1,256]{2,1,0:T(1,128)S(1)} %bitcast.67), channel_id=1, replica_groups=mesh['space'=32,'shell'=4] {'space'}, dimensions={0} | all-to-all | bytes 65536 | tf_op jit(solution)/shard_map/all_to_all | solution.py:126
  229.1 21.3 %shard_map.89 = f32[4096,128]{1,0:T(8,128)} custom-call(s32[8192]{0:T(1024)} %bitcast.53, f32[8192]{0:T(1024)} %bitcast.58, f32[8192,128]{1,0:T(8,128)} %bitcast.49, f32[4096,128]{1,0:T(8,128)} %broadcast_6_init_ref.2.init_ref), custom_call_target="tpu_custom_call" | custom-call | tf_op jit(solution)/shard_map/pallas_call | solution.py:56
  250.5 54.9 %all-reduce.7.cloned.1.call-done = f32[4096,128]{1,0:T(8,128)} async-done(((f32[4096,128]{1,0:T(8,128)}), f32[4096,128]{1,0:T(8,128)}) %all-reduce.7.cloned.1.call-update) | async-done | bytes 2097168 | tf_op jit(solution)/shard_map/psum | solution.py:138
  305.4 4.7 %convolution_subtract_fusion.table_ref = f32[4096,128]{1,0:T(8,128)} fusion(f32[4096,128]{1,0:T(8,128)S(1)} %copy-done.3, f32[4096,128]{1,0:T(8,128)} %all-reduce.7.cloned.1.call-done, f32[128,128]{1,0:T(8,128)S(1)} %copy-done.6), kind=kOutput, calls=%fused_computation.2 | convolution fusion | flops 805830656 | bytes 6356992 | tf_op jit(solution)/shard_map/dot_general | solution.py:143
  310.2 21.9 %shard_map.90 = f32[64,128]{1,0:T(8,128)} custom-call(s32[8192]{0:T(1024)} %bitcast.54, f32[4096,128]{1,0:T(8,128)} %convolution_subtract_fusion.table_ref, f32[8192,128]{1,0:T(8,128)} %bitcast.50), custom_call_target="tpu_custom_call" | custom-call | tf_op jit(solution)/shard_map/pallas_call | solution.py:87
  332.1 7.5 %all-to-all-start.5 = ((f32[32,1,256]{2,1,0:T(1,128)}), f32[32,1,256]{2,1,0:T(1,128)S(1)}, u32[]{:S(2)}, u32[]{:S(2)}) async-start(f32[32,1,256]{2,1,0:T(1,128)} %bitcast.57), calls=%async_computation.5 | async-start | bytes 65536 | tf_op jit(solution)/shard_map/all_to_all | solution.py:145
  339.7 3.4 fusion
  343.1 3.9 %all-to-all-done.5 = f32[32,1,256]{2,1,0:T(1,128)S(1)} async-done(((f32[32,1,256]{2,1,0:T(1,128)}), f32[32,1,256]{2,1,0:T(1,128)S(1)}, u32[]{:S(2)}, u32[]{:S(2)}) %all-to-all-start.5) | async-done | bytes 32800 | tf_op jit(solution)/shard_map/all_to_all | solution.py:145
  (49 shorter events, 19.4 us)
Async XLA Ops:
  7.2 26.5 %copy-start = (f32[128,64]{0,1:T(8,128)S(1)}, f32[128,64]{0,1:T(8,128)}, u32[]{:S(2)}) copy-start(f32[128,64]{0,1:T(8,128)} %param.12) | copy-start | bytes 98308
  7.2 12.0 %copy-start.9 = (s32[1,1,32]{2,1,0:T(1,128)S(1)}, s32[1,1,32]{2,1,0:T(1,128)}, u32[]{:S(2)}) copy-start(s32[1,1,32]{2,1,0:T(1,128)} %param.10) | copy-start | bytes 388
  10.6 15.8 %all-to-all-start = ((f32[32,1,256]{2,1,0:T(1,128)}), f32[32,1,256]{2,1,0:T(1,128)S(1)}, u32[]{:S(2)}, u32[]{:S(2)}) async-start(f32[32,1,256]{2,1,0:T(1,128)} %bitcast.4), calls=%async_computation | async-start | bytes 65536 | tf_op jit(solution)/shard_map/all_to_all | solution.py:126
  26.5 8.1 %copy-start.5 = (f32[64,4096]{1,0:T(8,128)S(1)}, f32[64,4096]{1,0:T(8,128)}, u32[]{:S(2)}) copy-start(f32[64,4096]{1,0:T(8,128)} %param.13) | copy-start | bytes 3145732
  26.5 35.0 %all-to-all-start.2 = ((f32[32,128,128]{2,1,0:T(8,128)}), f32[32,128,128]{2,1,0:T(8,128)S(1)}, u32[]{:S(2)}, u32[]{:S(2)}) async-start(f32[32,128,128]{2,1,0:T(8,128)} %get-tuple-element.12), calls=%async_computation.2 | async-start | bytes 4194304 | tf_op jit(solution)/shard_map/all_to_all | solution.py:110
  33.6 68.2 %all-reduce.9.cloned.1.call-start = ((), (), s32[]{:S(2)}) async-start(), calls=%async_computation.8 | async-start | bytes 4325376 | tf_op jit(solution)/shard_map/psum | solution.py:113
  61.5 1.3 copy-start.1
  61.5 8.3 %copy-start.7 = (s32[1,1,32,256]{3,2,1,0:T(8,128)S(1)}, s32[1,1,32,256]{3,2,1,0:T(8,128)}, u32[]{:S(2)}) copy-start(s32[1,1,32,256]{3,2,1,0:T(8,128)} %param.11) | copy-start | bytes 98308
  62.8 34.7 %all-to-all-start.1 = ((f32[32,128,128]{2,1,0:T(8,128)}), f32[32,128,128]{2,1,0:T(8,128)}, u32[]{:S(2)}, u32[]{:S(2)}) async-start(f32[32,128,128]{2,1,0:T(8,128)} %get-tuple-element.13), calls=%async_computation.1 | async-start | bytes 4194304 | tf_op jit(solution)/shard_map/all_to_all | solution.py:110
  69.5 103.6 %all-reduce.5.cloned.1.call-start = ((), (), s32[]{:S(2)}) async-start(), calls=%async_computation.6 | async-start | bytes 4194304 | tf_op jit(solution)/shard_map/psum | solution.py:138
  114.3 1.6 copy-start.2
  115.9 57.2 %copy-start.6 = (f32[128,128]{1,0:T(8,128)S(1)}, f32[128,128]{1,0:T(8,128)}, u32[]{:S(2)}) copy-start(f32[128,128]{1,0:T(8,128)} %get-tuple-element.6) | copy-start | bytes 196612
  200.4 16.4 %copy-start.8 = (f32[2048]{0:T(1024)S(1)}, f32[2048]{0:T(1024)}, u32[]{:S(2)}) copy-start(f32[2048]{0:T(1024)} %param.7) | copy-start | bytes 24580
  200.4 14.9 %all-to-all-start.3 = ((f32[32,1,256]{2,1,0:T(1,128)}), f32[32,1,256]{2,1,0:T(1,128)S(1)}, u32[]{:S(2)}, u32[]{:S(2)}) async-start(f32[32,1,256]{2,1,0:T(1,128)} %bitcast.56), calls=%async_computation.3 | async-start | bytes 65536 | tf_op jit(solution)/shard_map/all_to_all | solution.py:145
  208.0 97.4 %all-reduce.7.cloned.1.call-start = ((), (), s32[]{:S(2)}) async-start(), calls=%async_computation.7 | async-start | bytes 4194304 | tf_op jit(solution)/shard_map/psum | solution.py:138
  250.5 55.0 %copy-start.3 = (f32[4096,128]{1,0:T(8,128)S(1)}, f32[4096,128]{1,0:T(8,128)}, u32[]{:S(2)}) copy-start(f32[4096,128]{1,0:T(8,128)} %get-tuple-element.7) | copy-start | bytes 6291460
  310.2 29.5 %copy-start.4 = (f32[4096,128]{1,0:T(8,128)S(1)}, f32[4096,128]{1,0:T(8,128)}, u32[]{:S(2)}) copy-start(f32[4096,128]{1,0:T(8,128)} %all-reduce.7.cloned.1.call-done) | copy-start | bytes 6291460
  332.1 14.8 %all-to-all-start.5 = ((f32[32,1,256]{2,1,0:T(1,128)}), f32[32,1,256]{2,1,0:T(1,128)S(1)}, u32[]{:S(2)}, u32[]{:S(2)}) async-start(f32[32,1,256]{2,1,0:T(1,128)} %bitcast.57), calls=%async_computation.5 | async-start | bytes 65536 | tf_op jit(solution)/shard_map/all_to_all | solution.py:145
Sparse Core Ops, SparseCore 0:
  39.5 62.2 all-reduce.8
  114.5 58.6 all-reduce.4
  250.6 54.7 all-reduce.6

commit v6 on v5

--- a/solution.py
+++ b/solution.py
@@ -75,7 +75,11 @@
     def reduce_block(block, carry):
         start = pl.multiple_of(block * lanes, lanes)
         prod = rows_ref[pl.ds(start, lanes), :] * feat_ref[pl.ds(start, lanes), :]
-        out_ref[pl.ds(block, 1), :] = jnp.sum(prod.T, axis=0, keepdims=True)
+        sums = lax.dot_general(
+            jnp.ones((8, lanes), jnp.float32), prod, (((1,), (1,)), ((), ())),
+            precision=HI, preferred_element_type=jnp.float32,
+        )
+        out_ref[pl.ds(block, 1), :] = sums[0:1, :]
         return carry
 
     lax.fori_loop(0, out_ref.shape[0], reduce_block, 0)

time: 356 us -> 370 us (1.039)
  Pallas kernels: 90.2 us -> 104 us
    pallas_call x2, Pallas kernels: 43.7 us -> 57.9 us  [row_gather_dot(): pl.pallas_call(gather_kernel, out_shape=jax.ShapeDtypeStruct((feat.shape[...]
  transfers between devices with their start and end apart: 8 -> 8, of which waited for: 8 -> 8; matrix products, arithmetic and copies ran while one was open for 7% -> 7% of each run, Pallas kernels for 4% -> 3%
where the time goes in v6:
time: 370 us
  waiting for transfers between devices  157 us (42%)
  Pallas kernels  104 us (28%)
  starting transfers between devices  38 us (10%)
  matrix products  26.5 us (7%)
  between operations  13.9 us (4%)
  blocking collectives  11 us (3%)
  local copies, waits for them, and re-layouts  9.76 us (3%)
  other arithmetic  9.16 us (2%)
    psum x2, waiting for transfers between devices, on_device(): coeff_sum = lax.psum(partial_coeff, 'shell')  108 us
    pallas_call x2, Pallas kernels, row_gather_dot(): pl.pallas_call(gather_kernel, out_shape=jax.ShapeDtypeStruct((feat.shape[...  57.9 us
    pallas_call x3, Pallas kernels, row_scatter(): pl.pallas_call(scatter_kernel, out_shape=jax.ShapeDtypeStruct(init.shape,...  46.4 us
    all_to_all x2, waiting for transfers between devices, on_device(): lax.all_to_all(masked[:, h * half:(h + 1) * half], 'space', 0, 0, tiled=T...  34.5 us
    all_to_all x2, starting transfers between devices, on_device(): lax.all_to_all(local_grad, 'space', split_axis=0, concat_axis=0, tiled=True)  15.2 us
    all_to_all x2, starting transfers between devices, on_device(): lax.all_to_all(masked[:, h * half:(h + 1) * half], 'space', 0, 0, tiled=T...  13.9 us
    all_to_all x1, blocking collectives, on_device(): lax.all_to_all(picked, 'space', split_axis=0, concat_axis=0, tiled=True)  11 us
    dot_general x2, matrix products, on_device(): adjoint = jnp.dot(coeff_sum, gram, precision=HI) - data_proj  10.1 us
  transfers between devices with their start and end apart: 8, of which 8 were waited for; matrix products, arithmetic and copies ran while one was open for 7% of the time, Pallas kernels for 3%

profile of v6, /device:TPU:1, one launch (start us, length us, event | category | flops | bytes accessed | tf_op | source)
XLA Modules:
  0.0 369.7 jit_solution(3829675388300727799)
XLA Ops:
  10.6 8.6 %all-to-all-start = ((f32[32,1,256]{2,1,0:T(1,128)}), f32[32,1,256]{2,1,0:T(1,128)S(1)}, u32[]{:S(2)}, u32[]{:S(2)}) async-start(f32[32,1,256]{2,1,0:T(1,128)} %bitcast.4), calls=%async_computation | async-start | bytes 65536 | tf_op jit(solution)/shard_map/all_to_all | solution.py:130
  19.3 4.5 %multiply_reduce_fusion = (f32[32,256]{1,0:T(8,128)S(1)}, f32[32,256,128]{2,1,0:T(8,128)S(1)}) fusion(f32[1,1,32,256,128]{4,3,2,1,0:T(8,128)} %param.9, pred[32,256]{1,0:T(8,128)(4,1)S(1)} %iota_compare_fusion.10), kind=kLoop, calls=%fused_computation.8 | loop fusion | flops 3137536 | bytes 8429568 | tf_op jit(solution)/shard_map/reduce_sum | solution.py:124
  26.5 7.1 %all-to-all-start.2 = ((f32[32,128,128]{2,1,0:T(8,128)}), f32[32,128,128]{2,1,0:T(8,128)S(1)}, u32[]{:S(2)}, u32[]{:S(2)}) async-start(f32[32,128,128]{2,1,0:T(8,128)} %get-tuple-element.12), calls=%async_computation.2 | async-start | bytes 4194304 | tf_op jit(solution)/shard_map/all_to_all | solution.py:114
  34.6 4.8 %fusion.42 = f32[4096,128]{1,0:T(8,128)} fusion(f32[64,4096]{1,0:T(8,128)S(1)} %copy-done.5, f32[128,64]{0,1:T(8,128)S(1)} %copy-done), kind=kOutput, calls=%fused_computation.58 | convolution fusion | flops 402653184 | bytes 3178496 | tf_op jit(solution)/shard_map/dot_general | solution.py:118
  39.4 22.1 %all-to-all-done.2 = f32[32,128,128]{2,1,0:T(8,128)S(1)} async-done(((f32[32,128,128]{2,1,0:T(8,128)}), f32[32,128,128]{2,1,0:T(8,128)S(1)}, u32[]{:S(2)}, u32[]{:S(2)}) %all-to-all-start.2) | async-done | bytes 2097184 | tf_op jit(solution)/shard_map/all_to_all | solution.py:114
  62.8 6.7 %all-to-all-start.1 = ((f32[32,128,128]{2,1,0:T(8,128)}), f32[32,128,128]{2,1,0:T(8,128)}, u32[]{:S(2)}, u32[]{:S(2)}) async-start(f32[32,128,128]{2,1,0:T(8,128)} %get-tuple-element.13), calls=%async_computation.1 | async-start | bytes 4194304 | tf_op jit(solution)/shard_map/all_to_all | solution.py:114
  72.5 12.6 %shard_map.86.init_ref = f32[4096,128]{1,0:T(8,128)} custom-call(s32[4096]{0:T(1024)} %get-tuple-element.16.idx_ref, f32[4096]{0:T(1024)} %get-tuple-element.14.xs_ref, f32[4096,128]{1,0:T(8,128)} %bitcast.51, f32[4096,128]{1,0:T(8,128)} %broadcast_6_init_ref.2.init_ref), custom_call_target="tpu_custom_call" | custom-call | tf_op jit(solution)/shard_map/pallas_call | solution.py:56
  85.1 12.5 %all-to-all-done.1 = f32[32,128,128]{2,1,0:T(8,128)} async-done(((f32[32,128,128]{2,1,0:T(8,128)}), f32[32,128,128]{2,1,0:T(8,128)}, u32[]{:S(2)}, u32[]{:S(2)}) %all-to-all-start.1) | async-done | bytes 2097184 | tf_op jit(solution)/shard_map/all_to_all | solution.py:114
  97.5 4.3 %all-reduce.9.cloned.1.call-done = (f32[128,128]{1,0:T(8,128)}, f32[4096,128]{1,0:T(8,128)}) async-done(((f32[128,128]{1,0:T(8,128)}, f32[4096,128]{1,0:T(8,128)}), (f32[128,128]{1,0:T(8,128)}, f32[4096,128]{1,0:T(8,128)})) %all-reduce.9.cloned.1.call-update) | async-done | bytes 2162704 | tf_op jit(solution)/shard_map/psum | solution.py:117
  101.8 12.5 %shard_map.87 = f32[4096,128]{1,0:T(8,128)} custom-call(s32[4096]{0:T(1024)} %get-tuple-element.17.idx_ref, f32[4096]{0:T(1024)} %get-tuple-element.15.xs_ref, f32[4096,128]{1,0:T(8,128)} %bitcast.6.feat_ref, f32[4096,128]{1,0:T(8,128)} %shard_map.86.init_ref), custom_call_target="tpu_custom_call" | custom-call | tf_op jit(solution)/shard_map/pallas_call | solution.py:56
  115.9 4.0 %pad_maximum_fusion = f32[32,256,128]{2,1,0:T(8,128)} fusion(f32[32,128,128]{2,1,0:T(8,128)} %all-to-all-done.1, f32[32,128,128]{2,1,0:T(8,128)S(1)} %copy-done.2), kind=kLoop, calls=%fused_computation.6 | loop fusion | flops 1048576 | bytes 8388608 | tf_op jit(solution)/shard_map/concatenate | solution.py:122
  119.9 53.3 %all-reduce.5.cloned.1.call-done = f32[4096,128]{1,0:T(8,128)} async-done(((f32[4096,128]{1,0:T(8,128)}), f32[4096,128]{1,0:T(8,128)}) %all-reduce.5.cloned.1.call-update) | async-done | bytes 2097168 | tf_op jit(solution)/shard_map/psum | solution.py:142
  173.2 5.4 %convolution_subtract_fusion.1.table_ref = f32[4096,128]{1,0:T(8,128)} fusion(f32[4096,128]{1,0:T(8,128)} %get-tuple-element.7, f32[4096,128]{1,0:T(8,128)} %all-reduce.5.cloned.1.call-done, f32[128,128]{1,0:T(8,128)S(1)} %copy-done.6), kind=kOutput, calls=%fused_computation.3 | convolution fusion | flops 805830656 | bytes 6356992 | tf_op jit(solution)/shard_map/dot_general | solution.py:147
  178.6 28.9 %shard_map.88 = f32[64,128]{1,0:T(8,128)} custom-call(s32[8192]{0:T(1024)} %bitcast.52, f32[4096,128]{1,0:T(8,128)} %convolution_subtract_fusion.1.table_ref, f32[8192,128]{1,0:T(8,128)} %bitcast.48), custom_call_target="tpu_custom_call" | custom-call | tf_op jit(solution)/shard_map/pallas_call | solution.py:91
  207.4 7.7 %all-to-all-start.3 = ((f32[32,1,256]{2,1,0:T(1,128)}), f32[32,1,256]{2,1,0:T(1,128)S(1)}, u32[]{:S(2)}, u32[]{:S(2)}) async-start(f32[32,1,256]{2,1,0:T(1,128)} %bitcast.56), calls=%async_computation.3 | async-start | bytes 65536 | tf_op jit(solution)/shard_map/all_to_all | solution.py:149
  216.6 5.8 %all-to-all-done.3 = f32[32,1,256]{2,1,0:T(1,128)S(1)} async-done(((f32[32,1,256]{2,1,0:T(1,128)}), f32[32,1,256]{2,1,0:T(1,128)S(1)}, u32[]{:S(2)}, u32[]{:S(2)}) %all-to-all-start.3) | async-done | bytes 32800 | tf_op jit(solution)/shard_map/all_to_all | solution.py:149
  225.2 11.0 %all_to_all.49 = f32[32,1,256]{2,1,0:T(1,128)} all-to-all(f32[32,1,256]{2,1,0:T(1,128)S(1)} %bitcast.67), channel_id=1, replica_groups=mesh['space'=32,'shell'=4] {'space'}, dimensions={0} | all-to-all | bytes 65536 | tf_op jit(solution)/shard_map/all_to_all | solution.py:130
  236.2 21.3 %shard_map.89 = f32[4096,128]{1,0:T(8,128)} custom-call(s32[8192]{0:T(1024)} %bitcast.53, f32[8192]{0:T(1024)} %bitcast.58, f32[8192,128]{1,0:T(8,128)} %bitcast.49, f32[4096,128]{1,0:T(8,128)} %broadcast_6_init_ref.2.init_ref), custom_call_target="tpu_custom_call" | custom-call | tf_op jit(solution)/shard_map/pallas_call | solution.py:56
  257.6 54.9 %all-reduce.7.cloned.1.call-done = f32[4096,128]{1,0:T(8,128)} async-done(((f32[4096,128]{1,0:T(8,128)}), f32[4096,128]{1,0:T(8,128)}) %all-reduce.7.cloned.1.call-update) | async-done | bytes 2097168 | tf_op jit(solution)/shard_map/psum | solution.py:142
  312.5 4.7 %convolution_subtract_fusion.table_ref = f32[4096,128]{1,0:T(8,128)} fusion(f32[4096,128]{1,0:T(8,128)S(1)} %copy-done.3, f32[4096,128]{1,0:T(8,128)} %all-reduce.7.cloned.1.call-done, f32[128,128]{1,0:T(8,128)S(1)} %copy-done.6), kind=kOutput, calls=%fused_computation.2 | convolution fusion | flops 805830656 | bytes 6356992 | tf_op jit(solution)/shard_map/dot_general | solution.py:147
  317.2 29.0 %shard_map.90 = f32[64,128]{1,0:T(8,128)} custom-call(s32[8192]{0:T(1024)} %bitcast.54, f32[4096,128]{1,0:T(8,128)} %convolution_subtract_fusion.table_ref, f32[8192,128]{1,0:T(8,128)} %bitcast.50), custom_call_target="tpu_custom_call" | custom-call | tf_op jit(solution)/shard_map/pallas_call | solution.py:91
  346.3 7.5 %all-to-all-start.5 = ((f32[32,1,256]{2,1,0:T(1,128)}), f32[32,1,256]{2,1,0:T(1,128)S(1)}, u32[]{:S(2)}, u32[]{:S(2)}) async-start(f32[32,1,256]{2,1,0:T(1,128)} %bitcast.57), calls=%async_computation.5 | async-start | bytes 65536 | tf_op jit(solution)/shard_map/all_to_all | solution.py:149
  353.8 3.4 fusion
  357.2 3.9 %all-to-all-done.5 = f32[32,1,256]{2,1,0:T(1,128)S(1)} async-done(((f32[32,1,256]{2,1,0:T(1,128)}), f32[32,1,256]{2,1,0:T(1,128)S(1)}, u32[]{:S(2)}, u32[]{:S(2)}) %all-to-all-start.5) | async-done | bytes 32800 | tf_op jit(solution)/shard_map/all_to_all | solution.py:149
  (49 shorter events, 19.4 us)
Async XLA Ops:
  7.2 26.5 %copy-start = (f32[128,64]{0,1:T(8,128)S(1)}, f32[128,64]{0,1:T(8,128)}, u32[]{:S(2)}) copy-start(f32[128,64]{0,1:T(8,128)} %param.12) | copy-start | bytes 98308
  7.2 12.0 %copy-start.9 = (s32[1,1,32]{2,1,0:T(1,128)S(1)}, s32[1,1,32]{2,1,0:T(1,128)}, u32[]{:S(2)}) copy-start(s32[1,1,32]{2,1,0:T(1,128)} %param.10) | copy-start | bytes 388
  10.6 15.8 %all-to-all-start = ((f32[32,1,256]{2,1,0:T(1,128)}), f32[32,1,256]{2,1,0:T(1,128)S(1)}, u32[]{:S(2)}, u32[]{:S(2)}) async-start(f32[32,1,256]{2,1,0:T(1,128)} %bitcast.4), calls=%async_computation | async-start | bytes 65536 | tf_op jit(solution)/shard_map/all_to_all | solution.py:130
  26.5 8.1 %copy-start.5 = (f32[64,4096]{1,0:T(8,128)S(1)}, f32[64,4096]{1,0:T(8,128)}, u32[]{:S(2)}) copy-start(f32[64,4096]{1,0:T(8,128)} %param.13) | copy-start | bytes 3145732
  26.5 35.0 %all-to-all-start.2 = ((f32[32,128,128]{2,1,0:T(8,128)}), f32[32,128,128]{2,1,0:T(8,128)S(1)}, u32[]{:S(2)}, u32[]{:S(2)}) async-start(f32[32,128,128]{2,1,0:T(8,128)} %get-tuple-element.12), calls=%async_computation.2 | async-start | bytes 4194304 | tf_op jit(solution)/shard_map/all_to_all | solution.py:114
  33.6 68.2 %all-reduce.9.cloned.1.call-start = ((), (), s32[]{:S(2)}) async-start(), calls=%async_computation.8 | async-start | bytes 4325376 | tf_op jit(solution)/shard_map/psum | solution.py:117
  61.5 1.3 copy-start.1
  61.5 8.3 %copy-start.7 = (s32[1,1,32,256]{3,2,1,0:T(8,128)S(1)}, s32[1,1,32,256]{3,2,1,0:T(8,128)}, u32[]{:S(2)}) copy-start(s32[1,1,32,256]{3,2,1,0:T(8,128)} %param.11) | copy-start | bytes 98308
  62.8 34.7 %all-to-all-start.1 = ((f32[32,128,128]{2,1,0:T(8,128)}), f32[32,128,128]{2,1,0:T(8,128)}, u32[]{:S(2)}, u32[]{:S(2)}) async-start(f32[32,128,128]{2,1,0:T(8,128)} %get-tuple-element.13), calls=%async_computation.1 | async-start | bytes 4194304 | tf_op jit(solution)/shard_map/all_to_all | solution.py:114
  69.5 103.6 %all-reduce.5.cloned.1.call-start = ((), (), s32[]{:S(2)}) async-start(), calls=%async_computation.6 | async-start | bytes 4194304 | tf_op jit(solution)/shard_map/psum | solution.py:142
  114.3 1.6 copy-start.2
  115.9 57.2 %copy-start.6 = (f32[128,128]{1,0:T(8,128)S(1)}, f32[128,128]{1,0:T(8,128)}, u32[]{:S(2)}) copy-start(f32[128,128]{1,0:T(8,128)} %get-tuple-element.6) | copy-start | bytes 196612
  207.4 16.4 %copy-start.8 = (f32[2048]{0:T(1024)S(1)}, f32[2048]{0:T(1024)}, u32[]{:S(2)}) copy-start(f32[2048]{0:T(1024)} %param.7) | copy-start | bytes 24580
  207.4 14.9 %all-to-all-start.3 = ((f32[32,1,256]{2,1,0:T(1,128)}), f32[32,1,256]{2,1,0:T(1,128)S(1)}, u32[]{:S(2)}, u32[]{:S(2)}) async-start(f32[32,1,256]{2,1,0:T(1,128)} %bitcast.56), calls=%async_computation.3 | async-start | bytes 65536 | tf_op jit(solution)/shard_map/all_to_all | solution.py:149
  215.1 97.4 %all-reduce.7.cloned.1.call-start = ((), (), s32[]{:S(2)}) async-start(), calls=%async_computation.7 | async-start | bytes 4194304 | tf_op jit(solution)/shard_map/psum | solution.py:142
  257.5 55.0 %copy-start.3 = (f32[4096,128]{1,0:T(8,128)S(1)}, f32[4096,128]{1,0:T(8,128)}, u32[]{:S(2)}) copy-start(f32[4096,128]{1,0:T(8,128)} %get-tuple-element.7) | copy-start | bytes 6291460
  317.2 36.6 %copy-start.4 = (f32[4096,128]{1,0:T(8,128)S(1)}, f32[4096,128]{1,0:T(8,128)}, u32[]{:S(2)}) copy-start(f32[4096,128]{1,0:T(8,128)} %all-reduce.7.cloned.1.call-done) | copy-start | bytes 6291460
  346.3 14.8 %all-to-all-start.5 = ((f32[32,1,256]{2,1,0:T(1,128)}), f32[32,1,256]{2,1,0:T(1,128)S(1)}, u32[]{:S(2)}, u32[]{:S(2)}) async-start(f32[32,1,256]{2,1,0:T(1,128)} %bitcast.57), calls=%async_computation.5 | async-start | bytes 65536 | tf_op jit(solution)/shard_map/all_to_all | solution.py:149
Sparse Core Ops, SparseCore 0:
  39.5 62.2 all-reduce.8
  114.5 58.6 all-reduce.4
  257.7 54.7 all-reduce.6

commit v7 on v5

v7 whole, which is shorter than its diff:
```python
import functools

import jax
import jax.numpy as jnp
from jax import lax
from jax.sharding import PartitionSpec as P
from jax.experimental import pallas as pl
from jax.experimental.pallas import tpu as pltpu

ITERS = 2
HI = lax.Precision.HIGHEST


def one_hot_pair(index, count):
    low_count = 64
    high_count = count // low_count
    flat = index.reshape(-1)
    high = (flat // low_count)[:, None] == lax.broadcasted_iota(jnp.int32, (1, high_count), 1)
    low = (flat % low_count)[:, None] == lax.broadcasted_iota(jnp.int32, (1, low_count), 1)
    return high.astype(jnp.float32), low.astype(jnp.float32)


def pick(table, high, low):
    rows = jnp.dot(high, table.reshape(high.shape[1], low.shape[1]), precision=HI)
    return jnp.sum(rows * low, axis=1)


def spread(values, high, low):
    return jnp.dot(high.T, values.reshape(-1)[:, None] * low, precision=HI).reshape(-1)


UNROLL = 8
ACCS = 4


def scatter_kernel(slots, pad, idx_ref, xs_ref, feat_ref, init_ref, out_ref, *accs):
    accs[0][...] = init_ref[...]
    for acc in accs[1:]:
        acc[...] = jnp.zeros(acc.shape, acc.dtype)

    def body(step, carry):
        for u in range(UNROLL):
            k = step * UNROLL + u
            acc = accs[u % ACCS]
            row = k + (k // slots) * pad
            acc[pl.ds(idx_ref[k], 1), :] += xs_ref[k] * feat_ref[pl.ds(row, 1), :]
        return carry

    lax.fori_loop(0, idx_ref.shape[0] // UNROLL, body, 0)
    total = accs[0][...]
    for acc in accs[1:]:
        total = total + acc[...]
    out_ref[...] = total


def row_scatter(idx, xs, feat, init, slots, pad):
    smem = pl.BlockSpec(memory_space=pltpu.SMEM)
    vmem = pl.BlockSpec(memory_space=pltpu.VMEM)
    return pl.pallas_call(
        functools.partial(scatter_kernel, slots, pad),
        out_shape=jax.ShapeDtypeStruct(init.shape, jnp.float32),
        in_specs=[smem, smem, vmem, vmem],
        out_specs=vmem,
        scratch_shapes=[pltpu.VMEM(init.shape, jnp.float32) for _ in range(ACCS)],
    )(idx, xs, feat, init)


def gather_kernel(slots, pad, idx_ref, table_ref, feat_ref, out_ref, rows_ref):
    def body(step, carry):
        for u in range(UNROLL):
            k = step * UNROLL + u
            rows_ref[pl.ds(k, 1), :] = table_ref[pl.ds(idx_ref[k], 1), :]
        return carry

    lax.fori_loop(0, idx_ref.shape[0] // UNROLL, body, 0)
    lanes = out_ref.shape[1]

    def reduce_block(block, carry):
        start = pl.multiple_of(block * lanes, lanes)
        frow = pl.multiple_of(start + (start // slots) * pad, 8)
        prod = rows_ref[pl.ds(start, lanes), :] * feat_ref[pl.ds(frow, lanes), :]
        out_ref[pl.ds(block, 1), :] = jnp.sum(prod.T, axis=0, keepdims=True)
        return carry

    lax.fori_loop(0, out_ref.shape[0], reduce_block, 0)


def row_gather_dot(idx, table, feat, slots, pad):
    smem = pl.BlockSpec(memory_space=pltpu.SMEM)
    vmem = pl.BlockSpec(memory_space=pltpu.VMEM)
    return pl.pallas_call(
        functools.partial(gather_kernel, slots, pad),
        out_shape=jax.ShapeDtypeStruct((idx.shape[0] // 128, 128), jnp.float32),
        in_specs=[smem, vmem, vmem],
        out_specs=vmem,
        scratch_shapes=[pltpu.VMEM((idx.shape[0], feat.shape[1]), jnp.float32)],
    )(idx, table, feat)


def on_device(weights, seg_streamline, seg_features, pair_counts, seg_voxel, dictionary, measured):
    blocks = seg_streamline.shape[2]
    slots = seg_streamline.shape[3]
    coeffs = seg_features.shape[4]
    streams = weights.shape[0]
    stream_index = seg_streamline.reshape(blocks, slots)
    voxel_index = seg_voxel.reshape(blocks * slots)
    counts = pair_counts.reshape(blocks)
    live_slot = lax.broadcasted_iota(jnp.int32, (blocks, slots), 1) < counts[:, None]
    masked = jnp.where(
        live_slot[:, :, None], seg_features.reshape(blocks, slots, coeffs), jnp.float32(0.0)
    )
    high, low = one_hot_pair(stream_index, streams)
    column_sq = spread(jnp.sum(masked * masked, axis=2), high, low)
    scaling = 0.5 / (0.5 + column_sq)
    pad = 8
    picked = pick(weights, high, low).reshape(blocks, slots // coeffs, coeffs)
    payload = jnp.concatenate(
        [masked, picked, jnp.zeros((blocks, pad - slots // coeffs, coeffs), jnp.float32)], axis=1
    )
    received = lax.all_to_all(payload, "space", 0, 0, tiled=True)
    gram = lax.psum(jnp.dot(dictionary, dictionary.T, precision=HI), "shell")
    data_proj = lax.psum(jnp.dot(measured.T, dictionary.T, precision=HI), "shell")
    received, gram, data_proj = lax.optimization_barrier((received, gram, data_proj))
    local_x = received[:, slots:slots + slots // coeffs].reshape(blocks, slots)
    local_feat = received.reshape(blocks * (slots + pad), coeffs)
    current = weights
    residual = jnp.zeros(measured.shape, jnp.float32)
    for iteration in range(ITERS):
        if iteration > 0:
            picked = pick(current, high, low).reshape(blocks, slots)
            local_x = lax.all_to_all(picked, "space", split_axis=0, concat_axis=0, tiled=True)
        partial_coeff = row_scatter(
            voxel_index, local_x.reshape(-1), local_feat,
            jnp.zeros((measured.shape[1], coeffs), jnp.float32), slots, pad,
        )
        coeff_sum = lax.psum(partial_coeff, "shell")
        if iteration == ITERS - 1:
            residual = (
                jnp.einsum("jg,vj->gv", dictionary, coeff_sum, precision=HI) - measured
            )
        adjoint = jnp.dot(coeff_sum, gram, precision=HI) - data_proj
        local_grad = row_gather_dot(voxel_index, adjoint, local_feat, slots, pad)
        grad_slot = lax.all_to_all(
            local_grad.reshape(blocks, slots), "space", split_axis=0, concat_axis=0, tiled=True
        )
        gradient = spread(grad_slot, high, low)
        current = jnp.maximum(current - scaling * gradient, 0.0)
    return (current, residual)


def solution(mesh):
    in_specs = (
        P(("space", "shell")),
        P("space", "shell", None, None),
        P("space", "shell", None, None, None),
        P("space", "shell", None),
        P("space", "shell", None, None),
        P(None, "shell"),
        P("shell", "space"),
    )
    out_specs = (P(("space", "shell")), P("shell", "space"))
    return jax.shard_map(
        on_device, mesh=mesh, in_specs=in_specs, out_specs=out_specs, check_vma=False
    )
```

time: 356 us -> 439 us (1.23)
  Pallas kernels: 90.2 us -> 165 us
  waiting for transfers between devices: 157 us -> 185 us
  starting transfers between devices: 38 us -> 24.3 us
    pallas_call x5 -> x4, Pallas kernels: 90.2 us -> 165 us  [the longest x2 121 us: row_scatter(): pl.pallas_call(functools.partial(scatter_kernel, slots, pad), out_shape=j...]
    psum x1, waiting for transfers between devices: 4.27 us -> 61.7 us  [on_device(): gram = lax.psum(jnp.dot(dictionary, dictionary.T, precision=HI), 'shell')]
    all_to_all x5 -> x3, waiting for transfers between devices: 44.5 us -> 9.44 us  [the longest x2 9.44 us: on_device(): lax.all_to_all(local_grad.reshape(blocks, slots), 'space', split_axis=0,...]
    all_to_all x5 -> x3, starting transfers between devices: 37.6 us -> 24 us  [the longest x2 15.2 us: on_device(): lax.all_to_all(local_grad.reshape(blocks, slots), 'space', split_axis=0,...]
    psum x2, waiting for transfers between devices: 108 us -> 114 us  [on_device(): coeff_sum = lax.psum(partial_coeff, 'shell')]
  transfers between devices with their start and end apart: 8 -> 6, of which waited for: 8 -> 5; matrix products, arithmetic and copies ran while one was open for 7% -> 3% of each run, Pallas kernels for 4% -> 0%
where the time goes in v7:
time: 439 us
  waiting for transfers between devices  185 us (42%)
  Pallas kernels  165 us (38%)
  matrix products  25.3 us (6%)
  starting transfers between devices  24.3 us (6%)
  between operations  13.9 us (3%)
  blocking collectives  11 us (3%)
  other arithmetic  8.29 us (2%)
  local copies, waits for them, and re-layouts  5.53 us (1%)
    pallas_call x2, Pallas kernels, row_scatter(): pl.pallas_call(functools.partial(scatter_kernel, slots, pad), out_shape=j...  121 us
    psum x2, waiting for transfers between devices, on_device(): coeff_sum = lax.psum(partial_coeff, 'shell')  114 us
    psum x1, waiting for transfers between devices, on_device(): gram = lax.psum(jnp.dot(dictionary, dictionary.T, precision=HI), 'shell')  61.7 us
    pallas_call x2, Pallas kernels, row_gather_dot(): pl.pallas_call(functools.partial(gather_kernel, slots, pad), out_shape=ja...  44 us
    all_to_all x2, starting transfers between devices, on_device(): lax.all_to_all(local_grad.reshape(blocks, slots), 'space', split_axis=0,...  15.2 us
    all_to_all x1, blocking collectives, on_device(): lax.all_to_all(picked, 'space', split_axis=0, concat_axis=0, tiled=True)  11 us
    dot_general x2, matrix products, on_device(): adjoint = jnp.dot(coeff_sum, gram, precision=HI) - data_proj  9.48 us
    all_to_all x2, waiting for transfers between devices, on_device(): lax.all_to_all(local_grad.reshape(blocks, slots), 'space', split_axis=0,...  9.44 us
  transfers between devices with their start and end apart: 6, of which 5 were waited for; matrix products, arithmetic and copies ran while one was open for 3% of the time, Pallas kernels for 0%

profile of v7, /device:TPU:1, one launch (start us, length us, event | category | flops | bytes accessed | tf_op | source)
XLA Modules:
  0.0 438.6 jit_solution(9045870872614525636)
XLA Ops:
  9.5 4.5 %multiply_reduce_fusion = (f32[32,256]{1,0:T(8,128)S(1)}, f32[32,256,128]{2,1,0:T(8,128)S(1)}) fusion(f32[1,1,32,256,128]{4,3,2,1,0:T(8,128)} %param.9, pred[32,256]{1,0:T(8,128)(4,1)S(1)} %iota_compare_fusion.10), kind=kLoop, calls=%fused_computation.8 | loop fusion | flops 3137536 | bytes 8429568 | tf_op jit(solution)/shard_map/reduce_sum | solution.py:113
  15.3 2.4 maximum_maximum_fusion
  17.7 8.8 %all-to-all-start = ((f32[32,264,128]{2,1,0:T(8,128)}), f32[32,264,128]{2,1,0:T(8,128)}, u32[]{:S(2)}, u32[]{:S(2)}) async-start(f32[32,264,128]{2,1,0:T(8,128)} %maximum_maximum_fusion), calls=%async_computation | async-start | bytes 8650752 | tf_op jit(solution)/shard_map/all_to_all | solution.py:120
  27.5 4.8 %fusion.41 = f32[4096,128]{1,0:T(8,128)} fusion(f32[64,4096]{1,0:T(8,128)S(1)} %copy-done.3, f32[128,64]{0,1:T(8,128)S(1)} %copy-done), kind=kOutput, calls=%fused_computation.52 | convolution fusion | flops 402653184 | bytes 3178496 | tf_op jit(solution)/shard_map/dot_general | solution.py:122
  33.0 61.7 %all-reduce.9.cloned.1.call-done = (f32[128,128]{1,0:T(8,128)}, f32[4096,128]{1,0:T(8,128)}) async-done(((f32[128,128]{1,0:T(8,128)}, f32[4096,128]{1,0:T(8,128)}), (f32[128,128]{1,0:T(8,128)}, f32[4096,128]{1,0:T(8,128)})) %all-reduce.9.cloned.1.call-update) | async-done | bytes 2162704 | tf_op jit(solution)/shard_map/psum | solution.py:121
  94.7 1.5 slice.3
  96.3 1.5 broadcast_6_init_ref.2.init_ref
  97.7 60.7 %shard_map.86 = f32[4096,128]{1,0:T(8,128)} custom-call(s32[8192]{0:T(1024)} %bitcast.35, f32[8192]{0:T(1024)} %bitcast.42, f32[8448,128]{1,0:T(8,128)} %bitcast.4.feat_ref, f32[4096,128]{1,0:T(8,128)} %broadcast_6_init_ref.2.init_ref), custom_call_target="tpu_custom_call" | custom-call | tf_op jit(solution)/shard_map/pallas_call | solution.py:59
  158.5 58.8 %all-reduce.5.cloned.1.call-done = f32[4096,128]{1,0:T(8,128)} async-done(((f32[4096,128]{1,0:T(8,128)}), f32[4096,128]{1,0:T(8,128)}) %all-reduce.5.cloned.1.call-update) | async-done | bytes 2097168 | tf_op jit(solution)/shard_map/psum | solution.py:136
  217.2 4.7 %convolution_subtract_fusion.1.table_ref = f32[4096,128]{1,0:T(8,128)} fusion(f32[4096,128]{1,0:T(8,128)S(1)} %copy-done.1, f32[4096,128]{1,0:T(8,128)} %all-reduce.5.cloned.1.call-done, f32[128,128]{1,0:T(8,128)S(1)} %copy-done.4), kind=kOutput, calls=%fused_computation.3 | convolution fusion | flops 805830656 | bytes 6356992 | tf_op jit(solution)/shard_map/dot_general | solution.py:141
  222.0 21.9 %shard_map.87 = f32[64,128]{1,0:T(8,128)} custom-call(s32[8192]{0:T(1024)} %bitcast.36, f32[4096,128]{1,0:T(8,128)} %convolution_subtract_fusion.1.table_ref, f32[8448,128]{1,0:T(8,128)} %bitcast.4.feat_ref), custom_call_target="tpu_custom_call" | custom-call | tf_op jit(solution)/shard_map/pallas_call | solution.py:91
  243.9 7.7 %all-to-all-start.1 = ((f32[32,1,256]{2,1,0:T(1,128)}), f32[32,1,256]{2,1,0:T(1,128)S(1)}, u32[]{:S(2)}, u32[]{:S(2)}) async-start(f32[32,1,256]{2,1,0:T(1,128)} %bitcast.40), calls=%async_computation.1 | async-start | bytes 65536 | tf_op jit(solution)/shard_map/all_to_all | solution.py:143
  251.8 1.4 fusion.12
  253.3 5.6 %all-to-all-done.1 = f32[32,1,256]{2,1,0:T(1,128)S(1)} async-done(((f32[32,1,256]{2,1,0:T(1,128)}), f32[32,1,256]{2,1,0:T(1,128)S(1)}, u32[]{:S(2)}, u32[]{:S(2)}) %all-to-all-start.1) | async-done | bytes 32800 | tf_op jit(solution)/shard_map/all_to_all | solution.py:143
  258.9 1.4 fusion.15
  261.7 11.0 %all_to_all.32 = f32[32,1,256]{2,1,0:T(1,128)} all-to-all(f32[32,1,256]{2,1,0:T(1,128)S(1)} %bitcast.51), channel_id=1, replica_groups=mesh['space'=32,'shell'=4] {'space'}, dimensions={0} | all-to-all | bytes 65536 | tf_op jit(solution)/shard_map/all_to_all | solution.py:131
  272.7 60.7 %shard_map.88 = f32[4096,128]{1,0:T(8,128)} custom-call(s32[8192]{0:T(1024)} %bitcast.37, f32[8192]{0:T(1024)} %bitcast.43, f32[8448,128]{1,0:T(8,128)} %bitcast.4.feat_ref, f32[4096,128]{1,0:T(8,128)} %broadcast_6_init_ref.2.init_ref), custom_call_target="tpu_custom_call" | custom-call | tf_op jit(solution)/shard_map/pallas_call | solution.py:59
  333.4 54.9 %all-reduce.7.cloned.1.call-done = f32[4096,128]{1,0:T(8,128)} async-done(((f32[4096,128]{1,0:T(8,128)}), f32[4096,128]{1,0:T(8,128)}) %all-reduce.7.cloned.1.call-update) | async-done | bytes 2097168 | tf_op jit(solution)/shard_map/psum | solution.py:136
  388.3 4.7 %convolution_subtract_fusion.table_ref = f32[4096,128]{1,0:T(8,128)} fusion(f32[4096,128]{1,0:T(8,128)S(1)} %copy-done.1, f32[4096,128]{1,0:T(8,128)} %all-reduce.7.cloned.1.call-done, f32[128,128]{1,0:T(8,128)S(1)} %copy-done.4), kind=kOutput, calls=%fused_computation.2 | convolution fusion | flops 805830656 | bytes 6356992 | tf_op jit(solution)/shard_map/dot_general | solution.py:141
  393.1 22.1 %shard_map.89 = f32[64,128]{1,0:T(8,128)} custom-call(s32[8192]{0:T(1024)} %bitcast.38, f32[4096,128]{1,0:T(8,128)} %convolution_subtract_fusion.table_ref, f32[8448,128]{1,0:T(8,128)} %bitcast.4.feat_ref), custom_call_target="tpu_custom_call" | custom-call | tf_op jit(solution)/shard_map/pallas_call | solution.py:91
  415.2 7.5 %all-to-all-start.3 = ((f32[32,1,256]{2,1,0:T(1,128)}), f32[32,1,256]{2,1,0:T(1,128)S(1)}, u32[]{:S(2)}, u32[]{:S(2)}) async-start(f32[32,1,256]{2,1,0:T(1,128)} %bitcast.41), calls=%async_computation.3 | async-start | bytes 65536 | tf_op jit(solution)/shard_map/all_to_all | solution.py:143
  422.7 3.4 fusion
  426.1 3.9 all-to-all-done.3
  430.0 1.4 fusion.18
  (37 shorter events, 7.7 us)
Async XLA Ops:
  7.2 19.4 %copy-start = (f32[128,64]{0,1:T(8,128)S(1)}, f32[128,64]{0,1:T(8,128)}, u32[]{:S(2)}) copy-start(f32[128,64]{0,1:T(8,128)} %param.12) | copy-start | bytes 98308
  17.7 9.8 %copy-start.3 = (f32[64,4096]{1,0:T(8,128)S(1)}, f32[64,4096]{1,0:T(8,128)}, u32[]{:S(2)}) copy-start(f32[64,4096]{1,0:T(8,128)} %param.13) | copy-start | bytes 3145732
  17.7 77.0 %all-to-all-start = ((f32[32,264,128]{2,1,0:T(8,128)}), f32[32,264,128]{2,1,0:T(8,128)}, u32[]{:S(2)}, u32[]{:S(2)}) async-start(f32[32,264,128]{2,1,0:T(8,128)} %maximum_maximum_fusion), calls=%async_computation | async-start | bytes 8650752 | tf_op jit(solution)/shard_map/all_to_all | solution.py:120
  26.5 68.2 %all-reduce.9.cloned.1.call-start = ((), (), s32[]{:S(2)}) async-start(), calls=%async_computation.6 | async-start | bytes 4325376 | tf_op jit(solution)/shard_map/psum | solution.py:121
  27.5 4.9 %copy-start.6 = (s32[1,1,32,256]{3,2,1,0:T(8,128)S(1)}, s32[1,1,32,256]{3,2,1,0:T(8,128)}, u32[]{:S(2)}) copy-start(s32[1,1,32,256]{3,2,1,0:T(8,128)} %param.11) | copy-start | bytes 98308
  32.3 184.9 %all-reduce.5.cloned.1.call-start = ((), (), s32[]{:S(2)}) async-start(), calls=%async_computation.4 | async-start | bytes 4194304 | tf_op jit(solution)/shard_map/psum | solution.py:136
  158.4 58.8 %copy-start.1 = (f32[4096,128]{1,0:T(8,128)S(1)}, f32[4096,128]{1,0:T(8,128)}, u32[]{:S(2)}) copy-start(f32[4096,128]{1,0:T(8,128)} %get-tuple-element.7) | copy-start | bytes 6291460
  158.4 58.8 %copy-start.4 = (f32[128,128]{1,0:T(8,128)S(1)}, f32[128,128]{1,0:T(8,128)}, u32[]{:S(2)}) copy-start(f32[128,128]{1,0:T(8,128)} %get-tuple-element.6) | copy-start | bytes 196612
  243.9 16.4 %copy-start.5 = (f32[2048]{0:T(1024)S(1)}, f32[2048]{0:T(1024)}, u32[]{:S(2)}) copy-start(f32[2048]{0:T(1024)} %param.7) | copy-start | bytes 24580
  243.9 14.9 %all-to-all-start.1 = ((f32[32,1,256]{2,1,0:T(1,128)}), f32[32,1,256]{2,1,0:T(1,128)S(1)}, u32[]{:S(2)}, u32[]{:S(2)}) async-start(f32[32,1,256]{2,1,0:T(1,128)} %bitcast.40), calls=%async_computation.1 | async-start | bytes 65536 | tf_op jit(solution)/shard_map/all_to_all | solution.py:143
  251.6 136.7 %all-reduce.7.cloned.1.call-start = ((), (), s32[]{:S(2)}) async-start(), calls=%async_computation.5 | async-start | bytes 4194304 | tf_op jit(solution)/shard_map/psum | solution.py:136
  393.1 29.6 %copy-start.2 = (f32[4096,128]{1,0:T(8,128)S(1)}, f32[4096,128]{1,0:T(8,128)}, u32[]{:S(2)}) copy-start(f32[4096,128]{1,0:T(8,128)} %all-reduce.7.cloned.1.call-done) | copy-start | bytes 6291460
  415.2 14.8 %all-to-all-start.3 = ((f32[32,1,256]{2,1,0:T(1,128)}), f32[32,1,256]{2,1,0:T(1,128)S(1)}, u32[]{:S(2)}, u32[]{:S(2)}) async-start(f32[32,1,256]{2,1,0:T(1,128)} %bitcast.41), calls=%async_computation.3 | async-start | bytes 65536 | tf_op jit(solution)/shard_map/all_to_all | solution.py:143
Sparse Core Ops, SparseCore 0:
  32.4 62.2 all-reduce.8
  158.6 58.6 all-reduce.4
  333.5 54.7 all-reduce.6

commit v8 on v5

--- a/solution.py
+++ b/solution.py
@@ -140,7 +140,7 @@
             residual = (
                 jnp.einsum("jg,vj->gv", dictionary, coeff_sum, precision=HI) - measured
             )
-        adjoint = jnp.dot(coeff_sum, gram, precision=HI) - data_proj
+        adjoint = jnp.dot(coeff_sum, gram, precision=lax.Precision.HIGH) - data_proj
         local_grad = row_gather_dot(voxel_index, adjoint, local_feat).reshape(blocks, slots)
         grad_slot = lax.all_to_all(local_grad, "space", split_axis=0, concat_axis=0, tiled=True)
         gradient = spread(grad_slot, high, low)

time: 356 us -> 355 us (level)
  no operation moved by 1% of the time
where the time goes in v8:
time: 355 us; the launch traced here: 354 us
  waiting for transfers between devices  157 us (44%)
  Pallas kernels  90.2 us (25%)
  starting transfers between devices  38 us (11%)
  matrix products  24.9 us (7%)
  between operations  13.9 us (4%)
  blocking collectives  11 us (3%)
  local copies, waits for them, and re-layouts  9.76 us (3%)
  other arithmetic  9.16 us (3%)
    psum x2, waiting for transfers between devices, on_device(): coeff_sum = lax.psum(partial_coeff, 'shell')  108 us
    pallas_call x3, Pallas kernels, row_scatter(): pl.pallas_call(scatter_kernel, out_shape=jax.ShapeDtypeStruct(init.shape,...  46.4 us
    pallas_call x2, Pallas kernels, row_gather_dot(): pl.pallas_call(gather_kernel, out_shape=jax.ShapeDtypeStruct((feat.shape[...  43.7 us
    all_to_all x2, waiting for transfers between devices, on_device(): lax.all_to_all(masked[:, h * half:(h + 1) * half], 'space', 0, 0, tiled=T...  34.7 us
    all_to_all x2, starting transfers between devices, on_device(): lax.all_to_all(local_grad, 'space', split_axis=0, concat_axis=0, tiled=True)  15.2 us
    all_to_all x2, starting transfers between devices, on_device(): lax.all_to_all(masked[:, h * half:(h + 1) * half], 'space', 0, 0, tiled=T...  13.9 us
    all_to_all x1, blocking collectives, on_device(): lax.all_to_all(picked, 'space', split_axis=0, concat_axis=0, tiled=True)  11 us
    all_to_all x2, waiting for transfers between devices, on_device(): lax.all_to_all(local_grad, 'space', split_axis=0, concat_axis=0, tiled=True)  9.43 us
  transfers between devices with their start and end apart: 8, of which 8 were waited for; matrix products, arithmetic and copies ran while one was open for 7% of the time, Pallas kernels for 4%

profile of v8, /device:TPU:1, one launch (start us, length us, event | category | flops | bytes accessed | tf_op | source)
XLA Modules:
  0.0 353.9 jit_solution(14576399029537045652)
XLA Ops:
  10.6 8.6 %all-to-all-start = ((f32[32,1,256]{2,1,0:T(1,128)}), f32[32,1,256]{2,1,0:T(1,128)S(1)}, u32[]{:S(2)}, u32[]{:S(2)}) async-start(f32[32,1,256]{2,1,0:T(1,128)} %bitcast.4), calls=%async_computation | async-start | bytes 65536 | tf_op jit(solution)/shard_map/all_to_all | solution.py:126
  19.3 4.5 %multiply_reduce_fusion = (f32[32,256]{1,0:T(8,128)S(1)}, f32[32,256,128]{2,1,0:T(8,128)S(1)}) fusion(f32[1,1,32,256,128]{4,3,2,1,0:T(8,128)} %param.9, pred[32,256]{1,0:T(8,128)(4,1)S(1)} %iota_compare_fusion.10), kind=kLoop, calls=%fused_computation.8 | loop fusion | flops 3137536 | bytes 8429568 | tf_op jit(solution)/shard_map/reduce_sum | solution.py:120
  26.5 7.1 %all-to-all-start.2 = ((f32[32,128,128]{2,1,0:T(8,128)}), f32[32,128,128]{2,1,0:T(8,128)S(1)}, u32[]{:S(2)}, u32[]{:S(2)}) async-start(f32[32,128,128]{2,1,0:T(8,128)} %get-tuple-element.12), calls=%async_computation.2 | async-start | bytes 4194304 | tf_op jit(solution)/shard_map/all_to_all | solution.py:110
  34.6 4.8 %fusion.42 = f32[4096,128]{1,0:T(8,128)} fusion(f32[64,4096]{1,0:T(8,128)S(1)} %copy-done.5, f32[128,64]{0,1:T(8,128)S(1)} %copy-done), kind=kOutput, calls=%fused_computation.58 | convolution fusion | flops 402653184 | bytes 3178496 | tf_op jit(solution)/shard_map/dot_general | solution.py:114
  39.4 22.1 %all-to-all-done.2 = f32[32,128,128]{2,1,0:T(8,128)S(1)} async-done(((f32[32,128,128]{2,1,0:T(8,128)}), f32[32,128,128]{2,1,0:T(8,128)S(1)}, u32[]{:S(2)}, u32[]{:S(2)}) %all-to-all-start.2) | async-done | bytes 2097184 | tf_op jit(solution)/shard_map/all_to_all | solution.py:110
  62.8 6.7 %all-to-all-start.1 = ((f32[32,128,128]{2,1,0:T(8,128)}), f32[32,128,128]{2,1,0:T(8,128)}, u32[]{:S(2)}, u32[]{:S(2)}) async-start(f32[32,128,128]{2,1,0:T(8,128)} %get-tuple-element.13), calls=%async_computation.1 | async-start | bytes 4194304 | tf_op jit(solution)/shard_map/all_to_all | solution.py:110
  72.3 12.6 %shard_map.86.init_ref = f32[4096,128]{1,0:T(8,128)} custom-call(s32[4096]{0:T(1024)} %get-tuple-element.16.idx_ref, f32[4096]{0:T(1024)} %get-tuple-element.14.xs_ref, f32[4096,128]{1,0:T(8,128)} %bitcast.51, f32[4096,128]{1,0:T(8,128)} %broadcast_6_init_ref.2.init_ref), custom_call_target="tpu_custom_call" | custom-call | tf_op jit(solution)/shard_map/pallas_call | solution.py:56
  84.9 12.6 %all-to-all-done.1 = f32[32,128,128]{2,1,0:T(8,128)} async-done(((f32[32,128,128]{2,1,0:T(8,128)}), f32[32,128,128]{2,1,0:T(8,128)}, u32[]{:S(2)}, u32[]{:S(2)}) %all-to-all-start.1) | async-done | bytes 2097184 | tf_op jit(solution)/shard_map/all_to_all | solution.py:110
  97.5 4.3 %all-reduce.9.cloned.1.call-done = (f32[128,128]{1,0:T(8,128)}, f32[4096,128]{1,0:T(8,128)}) async-done(((f32[128,128]{1,0:T(8,128)}, f32[4096,128]{1,0:T(8,128)}), (f32[128,128]{1,0:T(8,128)}, f32[4096,128]{1,0:T(8,128)})) %all-reduce.9.cloned.1.call-update) | async-done | bytes 2162704 | tf_op jit(solution)/shard_map/psum | solution.py:113
  101.8 12.5 %shard_map.87 = f32[4096,128]{1,0:T(8,128)} custom-call(s32[4096]{0:T(1024)} %get-tuple-element.17.idx_ref, f32[4096]{0:T(1024)} %get-tuple-element.15.xs_ref, f32[4096,128]{1,0:T(8,128)} %bitcast.6.feat_ref, f32[4096,128]{1,0:T(8,128)} %shard_map.86.init_ref), custom_call_target="tpu_custom_call" | custom-call | tf_op jit(solution)/shard_map/pallas_call | solution.py:56
  115.9 4.0 %pad_maximum_fusion = f32[32,256,128]{2,1,0:T(8,128)} fusion(f32[32,128,128]{2,1,0:T(8,128)} %all-to-all-done.1, f32[32,128,128]{2,1,0:T(8,128)S(1)} %copy-done.2), kind=kLoop, calls=%fused_computation.6 | loop fusion | flops 1048576 | bytes 8388608 | tf_op jit(solution)/shard_map/concatenate | solution.py:118
  119.9 53.3 %all-reduce.5.cloned.1.call-done = f32[4096,128]{1,0:T(8,128)} async-done(((f32[4096,128]{1,0:T(8,128)}), f32[4096,128]{1,0:T(8,128)}) %all-reduce.5.cloned.1.call-update) | async-done | bytes 2097168 | tf_op jit(solution)/shard_map/psum | solution.py:138
  173.2 4.6 %convolution_subtract_fusion.1.table_ref = f32[4096,128]{1,0:T(8,128)} fusion(f32[4096,128]{1,0:T(8,128)} %get-tuple-element.7, f32[4096,128]{1,0:T(8,128)} %all-reduce.5.cloned.1.call-done, f32[128,128]{1,0:T(8,128)S(1)} %copy-done.6), kind=kOutput, calls=%fused_computation.3 | convolution fusion | flops 403177472 | bytes 6356992 | tf_op jit(solution)/shard_map/dot_general | solution.py:143
  177.7 21.8 %shard_map.88 = f32[64,128]{1,0:T(8,128)} custom-call(s32[8192]{0:T(1024)} %bitcast.52, f32[4096,128]{1,0:T(8,128)} %convolution_subtract_fusion.1.table_ref, f32[8192,128]{1,0:T(8,128)} %bitcast.48), custom_call_target="tpu_custom_call" | custom-call | tf_op jit(solution)/shard_map/pallas_call | solution.py:87
  199.5 7.7 %all-to-all-start.3 = ((f32[32,1,256]{2,1,0:T(1,128)}), f32[32,1,256]{2,1,0:T(1,128)S(1)}, u32[]{:S(2)}, u32[]{:S(2)}) async-start(f32[32,1,256]{2,1,0:T(1,128)} %bitcast.56), calls=%async_computation.3 | async-start | bytes 65536 | tf_op jit(solution)/shard_map/all_to_all | solution.py:145
  208.9 5.6 %all-to-all-done.3 = f32[32,1,256]{2,1,0:T(1,128)S(1)} async-done(((f32[32,1,256]{2,1,0:T(1,128)}), f32[32,1,256]{2,1,0:T(1,128)S(1)}, u32[]{:S(2)}, u32[]{:S(2)}) %all-to-all-start.3) | async-done | bytes 32800 | tf_op jit(solution)/shard_map/all_to_all | solution.py:145
  217.3 11.0 %all_to_all.49 = f32[32,1,256]{2,1,0:T(1,128)} all-to-all(f32[32,1,256]{2,1,0:T(1,128)S(1)} %bitcast.67), channel_id=1, replica_groups=mesh['space'=32,'shell'=4] {'space'}, dimensions={0} | all-to-all | bytes 65536 | tf_op jit(solution)/shard_map/all_to_all | solution.py:126
  228.3 21.3 %shard_map.89 = f32[4096,128]{1,0:T(8,128)} custom-call(s32[8192]{0:T(1024)} %bitcast.53, f32[8192]{0:T(1024)} %bitcast.58, f32[8192,128]{1,0:T(8,128)} %bitcast.49, f32[4096,128]{1,0:T(8,128)} %broadcast_6_init_ref.2.init_ref), custom_call_target="tpu_custom_call" | custom-call | tf_op jit(solution)/shard_map/pallas_call | solution.py:56
  249.7 54.9 %all-reduce.7.cloned.1.call-done = f32[4096,128]{1,0:T(8,128)} async-done(((f32[4096,128]{1,0:T(8,128)}), f32[4096,128]{1,0:T(8,128)}) %all-reduce.7.cloned.1.call-update) | async-done | bytes 2097168 | tf_op jit(solution)/shard_map/psum | solution.py:138
  304.6 3.9 %convolution_subtract_fusion.table_ref = f32[4096,128]{1,0:T(8,128)} fusion(f32[4096,128]{1,0:T(8,128)S(1)} %copy-done.3, f32[4096,128]{1,0:T(8,128)} %all-reduce.7.cloned.1.call-done, f32[128,128]{1,0:T(8,128)S(1)} %copy-done.6), kind=kOutput, calls=%fused_computation.2 | convolution fusion | flops 403177472 | bytes 6356992 | tf_op jit(solution)/shard_map/dot_general | solution.py:143
  308.6 21.9 %shard_map.90 = f32[64,128]{1,0:T(8,128)} custom-call(s32[8192]{0:T(1024)} %bitcast.54, f32[4096,128]{1,0:T(8,128)} %convolution_subtract_fusion.table_ref, f32[8192,128]{1,0:T(8,128)} %bitcast.50), custom_call_target="tpu_custom_call" | custom-call | tf_op jit(solution)/shard_map/pallas_call | solution.py:87
  330.5 7.5 %all-to-all-start.5 = ((f32[32,1,256]{2,1,0:T(1,128)}), f32[32,1,256]{2,1,0:T(1,128)S(1)}, u32[]{:S(2)}, u32[]{:S(2)}) async-start(f32[32,1,256]{2,1,0:T(1,128)} %bitcast.57), calls=%async_computation.5 | async-start | bytes 65536 | tf_op jit(solution)/shard_map/all_to_all | solution.py:145
  338.1 3.4 fusion
  341.4 3.9 %all-to-all-done.5 = f32[32,1,256]{2,1,0:T(1,128)S(1)} async-done(((f32[32,1,256]{2,1,0:T(1,128)}), f32[32,1,256]{2,1,0:T(1,128)S(1)}, u32[]{:S(2)}, u32[]{:S(2)}) %all-to-all-start.5) | async-done | bytes 32800 | tf_op jit(solution)/shard_map/all_to_all | solution.py:145
  (49 shorter events, 19.4 us)
Async XLA Ops:
  7.2 26.5 %copy-start = (f32[128,64]{0,1:T(8,128)S(1)}, f32[128,64]{0,1:T(8,128)}, u32[]{:S(2)}) copy-start(f32[128,64]{0,1:T(8,128)} %param.12) | copy-start | bytes 98308
  7.2 12.0 %copy-start.9 = (s32[1,1,32]{2,1,0:T(1,128)S(1)}, s32[1,1,32]{2,1,0:T(1,128)}, u32[]{:S(2)}) copy-start(s32[1,1,32]{2,1,0:T(1,128)} %param.10) | copy-start | bytes 388
  10.6 15.8 %all-to-all-start = ((f32[32,1,256]{2,1,0:T(1,128)}), f32[32,1,256]{2,1,0:T(1,128)S(1)}, u32[]{:S(2)}, u32[]{:S(2)}) async-start(f32[32,1,256]{2,1,0:T(1,128)} %bitcast.4), calls=%async_computation | async-start | bytes 65536 | tf_op jit(solution)/shard_map/all_to_all | solution.py:126
  26.5 8.1 %copy-start.5 = (f32[64,4096]{1,0:T(8,128)S(1)}, f32[64,4096]{1,0:T(8,128)}, u32[]{:S(2)}) copy-start(f32[64,4096]{1,0:T(8,128)} %param.13) | copy-start | bytes 3145732
  26.5 35.0 %all-to-all-start.2 = ((f32[32,128,128]{2,1,0:T(8,128)}), f32[32,128,128]{2,1,0:T(8,128)S(1)}, u32[]{:S(2)}, u32[]{:S(2)}) async-start(f32[32,128,128]{2,1,0:T(8,128)} %get-tuple-element.12), calls=%async_computation.2 | async-start | bytes 4194304 | tf_op jit(solution)/shard_map/all_to_all | solution.py:110
  33.6 68.2 %all-reduce.9.cloned.1.call-start = ((), (), s32[]{:S(2)}) async-start(), calls=%async_computation.8 | async-start | bytes 4325376 | tf_op jit(solution)/shard_map/psum | solution.py:113
  61.5 1.3 copy-start.1
  61.5 8.1 %copy-start.7 = (s32[1,1,32,256]{3,2,1,0:T(8,128)S(1)}, s32[1,1,32,256]{3,2,1,0:T(8,128)}, u32[]{:S(2)}) copy-start(s32[1,1,32,256]{3,2,1,0:T(8,128)} %param.11) | copy-start | bytes 98308
  62.8 34.7 %all-to-all-start.1 = ((f32[32,128,128]{2,1,0:T(8,128)}), f32[32,128,128]{2,1,0:T(8,128)}, u32[]{:S(2)}, u32[]{:S(2)}) async-start(f32[32,128,128]{2,1,0:T(8,128)} %get-tuple-element.13), calls=%async_computation.1 | async-start | bytes 4194304 | tf_op jit(solution)/shard_map/all_to_all | solution.py:110
  69.5 103.6 %all-reduce.5.cloned.1.call-start = ((), (), s32[]{:S(2)}) async-start(), calls=%async_computation.6 | async-start | bytes 4194304 | tf_op jit(solution)/shard_map/psum | solution.py:138
  114.3 1.6 copy-start.2
  115.9 57.2 %copy-start.6 = (f32[128,128]{1,0:T(8,128)S(1)}, f32[128,128]{1,0:T(8,128)}, u32[]{:S(2)}) copy-start(f32[128,128]{1,0:T(8,128)} %get-tuple-element.6) | copy-start | bytes 196612
  199.5 16.4 %copy-start.8 = (f32[2048]{0:T(1024)S(1)}, f32[2048]{0:T(1024)}, u32[]{:S(2)}) copy-start(f32[2048]{0:T(1024)} %param.7) | copy-start | bytes 24580
  199.5 14.9 %all-to-all-start.3 = ((f32[32,1,256]{2,1,0:T(1,128)}), f32[32,1,256]{2,1,0:T(1,128)S(1)}, u32[]{:S(2)}, u32[]{:S(2)}) async-start(f32[32,1,256]{2,1,0:T(1,128)} %bitcast.56), calls=%async_computation.3 | async-start | bytes 65536 | tf_op jit(solution)/shard_map/all_to_all | solution.py:145
  207.2 97.4 %all-reduce.7.cloned.1.call-start = ((), (), s32[]{:S(2)}) async-start(), calls=%async_computation.7 | async-start | bytes 4194304 | tf_op jit(solution)/shard_map/psum | solution.py:138
  249.7 55.0 %copy-start.3 = (f32[4096,128]{1,0:T(8,128)S(1)}, f32[4096,128]{1,0:T(8,128)}, u32[]{:S(2)}) copy-start(f32[4096,128]{1,0:T(8,128)} %get-tuple-element.7) | copy-start | bytes 6291460
  308.6 29.5 %copy-start.4 = (f32[4096,128]{1,0:T(8,128)S(1)}, f32[4096,128]{1,0:T(8,128)}, u32[]{:S(2)}) copy-start(f32[4096,128]{1,0:T(8,128)} %all-reduce.7.cloned.1.call-done) | copy-start | bytes 6291460
  330.5 14.8 %all-to-all-start.5 = ((f32[32,1,256]{2,1,0:T(1,128)}), f32[32,1,256]{2,1,0:T(1,128)S(1)}, u32[]{:S(2)}, u32[]{:S(2)}) async-start(f32[32,1,256]{2,1,0:T(1,128)} %bitcast.57), calls=%async_computation.5 | async-start | bytes 65536 | tf_op jit(solution)/shard_map/all_to_all | solution.py:145
Sparse Core Ops, SparseCore 0:
  39.5 62.2 all-reduce.8
  114.5 58.6 all-reduce.4
  249.8 54.7 all-reduce.6

commit v9 on v5

--- a/solution.py
+++ b/solution.py
@@ -27,8 +27,8 @@
     return jnp.dot(high.T, values.reshape(-1)[:, None] * low, precision=HI).reshape(-1)
 
 
-UNROLL = 8
-ACCS = 4
+UNROLL = 64
+ACCS = 8
 
 
 def scatter_kernel(idx_ref, xs_ref, feat_ref, init_ref, out_ref, *accs):

time: 356 us -> 340 us (0.955)
  Pallas kernels: 90.2 us -> 70.9 us
    pallas_call x3, Pallas kernels: 46.4 us -> 35.7 us  [row_scatter(): pl.pallas_call(scatter_kernel, out_shape=jax.ShapeDtypeStruct(init.shape,...]
    pallas_call x2, Pallas kernels: 43.7 us -> 35.3 us  [row_gather_dot(): pl.pallas_call(gather_kernel, out_shape=jax.ShapeDtypeStruct((feat.shape[...]
  transfers between devices with their start and end apart: 8 -> 8, of which waited for: 8 -> 8; matrix products, arithmetic and copies ran while one was open for 7% -> 7% of each run, Pallas kernels for 4% -> 3%
where the time goes in v9:
time: 340 us; the launch traced here: 339 us
  waiting for transfers between devices  159 us (47%)
  Pallas kernels  70.9 us (21%)
  starting transfers between devices  38 us (11%)
  matrix products  26.5 us (8%)
  between operations  13.9 us (4%)
  blocking collectives  11 us (3%)
  local copies, waits for them, and re-layouts  9.76 us (3%)
  other arithmetic  9.16 us (3%)
    psum x2, waiting for transfers between devices, on_device(): coeff_sum = lax.psum(partial_coeff, 'shell')  108 us
    all_to_all x2, waiting for transfers between devices, on_device(): lax.all_to_all(masked[:, h * half:(h + 1) * half], 'space', 0, 0, tiled=T...  37 us
    pallas_call x3, Pallas kernels, row_scatter(): pl.pallas_call(scatter_kernel, out_shape=jax.ShapeDtypeStruct(init.shape,...  35.7 us
    pallas_call x2, Pallas kernels, row_gather_dot(): pl.pallas_call(gather_kernel, out_shape=jax.ShapeDtypeStruct((feat.shape[...  35.3 us
    all_to_all x2, starting transfers between devices, on_device(): lax.all_to_all(local_grad, 'space', split_axis=0, concat_axis=0, tiled=True)  15.2 us
    all_to_all x2, starting transfers between devices, on_device(): lax.all_to_all(masked[:, h * half:(h + 1) * half], 'space', 0, 0, tiled=T...  13.9 us
    all_to_all x1, blocking collectives, on_device(): lax.all_to_all(picked, 'space', split_axis=0, concat_axis=0, tiled=True)  11 us
    dot_general x2, matrix products, on_device(): adjoint = jnp.dot(coeff_sum, gram, precision=HI) - data_proj  10.1 us
  transfers between devices with their start and end apart: 8, of which 8 were waited for; matrix products, arithmetic and copies ran while one was open for 7% of the time, Pallas kernels for 3%

profile of v9, /device:TPU:1, one launch (start us, length us, event | category | flops | bytes accessed | tf_op | source)
XLA Modules:
  0.0 338.7 jit_solution(81237602311869813)
XLA Ops:
  10.6 8.6 %all-to-all-start = ((f32[32,1,256]{2,1,0:T(1,128)}), f32[32,1,256]{2,1,0:T(1,128)S(1)}, u32[]{:S(2)}, u32[]{:S(2)}) async-start(f32[32,1,256]{2,1,0:T(1,128)} %bitcast.4), calls=%async_computation | async-start | bytes 65536 | tf_op jit(solution)/shard_map/all_to_all | solution.py:126
  19.3 4.5 %multiply_reduce_fusion = (f32[32,256]{1,0:T(8,128)S(1)}, f32[32,256,128]{2,1,0:T(8,128)S(1)}) fusion(f32[1,1,32,256,128]{4,3,2,1,0:T(8,128)} %param.9, pred[32,256]{1,0:T(8,128)(4,1)S(1)} %iota_compare_fusion.10), kind=kLoop, calls=%fused_computation.8 | loop fusion | flops 3137536 | bytes 8429568 | tf_op jit(solution)/shard_map/reduce_sum | solution.py:120
  26.5 7.1 %all-to-all-start.2 = ((f32[32,128,128]{2,1,0:T(8,128)}), f32[32,128,128]{2,1,0:T(8,128)S(1)}, u32[]{:S(2)}, u32[]{:S(2)}) async-start(f32[32,128,128]{2,1,0:T(8,128)} %get-tuple-element.12), calls=%async_computation.2 | async-start | bytes 4194304 | tf_op jit(solution)/shard_map/all_to_all | solution.py:110
  34.6 4.8 %fusion.42 = f32[4096,128]{1,0:T(8,128)} fusion(f32[64,4096]{1,0:T(8,128)S(1)} %copy-done.5, f32[128,64]{0,1:T(8,128)S(1)} %copy-done), kind=kOutput, calls=%fused_computation.58 | convolution fusion | flops 402653184 | bytes 3178496 | tf_op jit(solution)/shard_map/dot_general | solution.py:114
  39.4 22.1 %all-to-all-done.2 = f32[32,128,128]{2,1,0:T(8,128)S(1)} async-done(((f32[32,128,128]{2,1,0:T(8,128)}), f32[32,128,128]{2,1,0:T(8,128)S(1)}, u32[]{:S(2)}, u32[]{:S(2)}) %all-to-all-start.2) | async-done | bytes 2097184 | tf_op jit(solution)/shard_map/all_to_all | solution.py:110
  62.8 6.7 %all-to-all-start.1 = ((f32[32,128,128]{2,1,0:T(8,128)}), f32[32,128,128]{2,1,0:T(8,128)}, u32[]{:S(2)}, u32[]{:S(2)}) async-start(f32[32,128,128]{2,1,0:T(8,128)} %get-tuple-element.13), calls=%async_computation.1 | async-start | bytes 4194304 | tf_op jit(solution)/shard_map/all_to_all | solution.py:110
  72.5 10.1 %shard_map.86.init_ref = f32[4096,128]{1,0:T(8,128)} custom-call(s32[4096]{0:T(1024)} %get-tuple-element.16.idx_ref, f32[4096]{0:T(1024)} %get-tuple-element.14.xs_ref, f32[4096,128]{1,0:T(8,128)} %bitcast.51, f32[4096,128]{1,0:T(8,128)} %broadcast_6_init_ref.2.init_ref), custom_call_target="tpu_custom_call" | custom-call | tf_op jit(solution)/shard_map/pallas_call | solution.py:56
  82.6 14.9 %all-to-all-done.1 = f32[32,128,128]{2,1,0:T(8,128)} async-done(((f32[32,128,128]{2,1,0:T(8,128)}), f32[32,128,128]{2,1,0:T(8,128)}, u32[]{:S(2)}, u32[]{:S(2)}) %all-to-all-start.1) | async-done | bytes 2097184 | tf_op jit(solution)/shard_map/all_to_all | solution.py:110
  97.5 4.3 %all-reduce.9.cloned.1.call-done = (f32[128,128]{1,0:T(8,128)}, f32[4096,128]{1,0:T(8,128)}) async-done(((f32[128,128]{1,0:T(8,128)}, f32[4096,128]{1,0:T(8,128)}), (f32[128,128]{1,0:T(8,128)}, f32[4096,128]{1,0:T(8,128)})) %all-reduce.9.cloned.1.call-update) | async-done | bytes 2162704 | tf_op jit(solution)/shard_map/psum | solution.py:113
  101.8 10.1 %shard_map.87 = f32[4096,128]{1,0:T(8,128)} custom-call(s32[4096]{0:T(1024)} %get-tuple-element.17.idx_ref, f32[4096]{0:T(1024)} %get-tuple-element.15.xs_ref, f32[4096,128]{1,0:T(8,128)} %bitcast.6.feat_ref, f32[4096,128]{1,0:T(8,128)} %shard_map.86.init_ref), custom_call_target="tpu_custom_call" | custom-call | tf_op jit(solution)/shard_map/pallas_call | solution.py:56
  113.5 4.0 %pad_maximum_fusion = f32[32,256,128]{2,1,0:T(8,128)} fusion(f32[32,128,128]{2,1,0:T(8,128)} %all-to-all-done.1, f32[32,128,128]{2,1,0:T(8,128)S(1)} %copy-done.2), kind=kLoop, calls=%fused_computation.6 | loop fusion | flops 1048576 | bytes 8388608 | tf_op jit(solution)/shard_map/concatenate | solution.py:118
  117.4 53.3 %all-reduce.5.cloned.1.call-done = f32[4096,128]{1,0:T(8,128)} async-done(((f32[4096,128]{1,0:T(8,128)}), f32[4096,128]{1,0:T(8,128)}) %all-reduce.5.cloned.1.call-update) | async-done | bytes 2097168 | tf_op jit(solution)/shard_map/psum | solution.py:138
  170.7 5.4 %convolution_subtract_fusion.1.table_ref = f32[4096,128]{1,0:T(8,128)} fusion(f32[4096,128]{1,0:T(8,128)} %get-tuple-element.7, f32[4096,128]{1,0:T(8,128)} %all-reduce.5.cloned.1.call-done, f32[128,128]{1,0:T(8,128)S(1)} %copy-done.6), kind=kOutput, calls=%fused_computation.3 | convolution fusion | flops 805830656 | bytes 6356992 | tf_op jit(solution)/shard_map/dot_general | solution.py:143
  176.1 17.6 %shard_map.88 = f32[64,128]{1,0:T(8,128)} custom-call(s32[8192]{0:T(1024)} %bitcast.52, f32[4096,128]{1,0:T(8,128)} %convolution_subtract_fusion.1.table_ref, f32[8192,128]{1,0:T(8,128)} %bitcast.48), custom_call_target="tpu_custom_call" | custom-call | tf_op jit(solution)/shard_map/pallas_call | solution.py:87
  193.6 7.7 %all-to-all-start.3 = ((f32[32,1,256]{2,1,0:T(1,128)}), f32[32,1,256]{2,1,0:T(1,128)S(1)}, u32[]{:S(2)}, u32[]{:S(2)}) async-start(f32[32,1,256]{2,1,0:T(1,128)} %bitcast.56), calls=%async_computation.3 | async-start | bytes 65536 | tf_op jit(solution)/shard_map/all_to_all | solution.py:145
  202.8 5.8 %all-to-all-done.3 = f32[32,1,256]{2,1,0:T(1,128)S(1)} async-done(((f32[32,1,256]{2,1,0:T(1,128)}), f32[32,1,256]{2,1,0:T(1,128)S(1)}, u32[]{:S(2)}, u32[]{:S(2)}) %all-to-all-start.3) | async-done | bytes 32800 | tf_op jit(solution)/shard_map/all_to_all | solution.py:145
  211.4 11.0 %all_to_all.49 = f32[32,1,256]{2,1,0:T(1,128)} all-to-all(f32[32,1,256]{2,1,0:T(1,128)S(1)} %bitcast.67), channel_id=1, replica_groups=mesh['space'=32,'shell'=4] {'space'}, dimensions={0} | all-to-all | bytes 65536 | tf_op jit(solution)/shard_map/all_to_all | solution.py:126
  222.4 15.5 %shard_map.89 = f32[4096,128]{1,0:T(8,128)} custom-call(s32[8192]{0:T(1024)} %bitcast.53, f32[8192]{0:T(1024)} %bitcast.58, f32[8192,128]{1,0:T(8,128)} %bitcast.49, f32[4096,128]{1,0:T(8,128)} %broadcast_6_init_ref.2.init_ref), custom_call_target="tpu_custom_call" | custom-call | tf_op jit(solution)/shard_map/pallas_call | solution.py:56
  237.9 54.9 %all-reduce.7.cloned.1.call-done = f32[4096,128]{1,0:T(8,128)} async-done(((f32[4096,128]{1,0:T(8,128)}), f32[4096,128]{1,0:T(8,128)}) %all-reduce.7.cloned.1.call-update) | async-done | bytes 2097168 | tf_op jit(solution)/shard_map/psum | solution.py:138
  292.9 4.7 %convolution_subtract_fusion.table_ref = f32[4096,128]{1,0:T(8,128)} fusion(f32[4096,128]{1,0:T(8,128)S(1)} %copy-done.3, f32[4096,128]{1,0:T(8,128)} %all-reduce.7.cloned.1.call-done, f32[128,128]{1,0:T(8,128)S(1)} %copy-done.6), kind=kOutput, calls=%fused_computation.2 | convolution fusion | flops 805830656 | bytes 6356992 | tf_op jit(solution)/shard_map/dot_general | solution.py:143
  297.6 17.7 %shard_map.90 = f32[64,128]{1,0:T(8,128)} custom-call(s32[8192]{0:T(1024)} %bitcast.54, f32[4096,128]{1,0:T(8,128)} %convolution_subtract_fusion.table_ref, f32[8192,128]{1,0:T(8,128)} %bitcast.50), custom_call_target="tpu_custom_call" | custom-call | tf_op jit(solution)/shard_map/pallas_call | solution.py:87
  315.3 7.5 %all-to-all-start.5 = ((f32[32,1,256]{2,1,0:T(1,128)}), f32[32,1,256]{2,1,0:T(1,128)S(1)}, u32[]{:S(2)}, u32[]{:S(2)}) async-start(f32[32,1,256]{2,1,0:T(1,128)} %bitcast.57), calls=%async_computation.5 | async-start | bytes 65536 | tf_op jit(solution)/shard_map/all_to_all | solution.py:145
  322.9 3.4 fusion
  326.3 3.9 %all-to-all-done.5 = f32[32,1,256]{2,1,0:T(1,128)S(1)} async-done(((f32[32,1,256]{2,1,0:T(1,128)}), f32[32,1,256]{2,1,0:T(1,128)S(1)}, u32[]{:S(2)}, u32[]{:S(2)}) %all-to-all-start.5) | async-done | bytes 32800 | tf_op jit(solution)/shard_map/all_to_all | solution.py:145
  (49 shorter events, 19.4 us)
Async XLA Ops:
  7.2 26.5 %copy-start = (f32[128,64]{0,1:T(8,128)S(1)}, f32[128,64]{0,1:T(8,128)}, u32[]{:S(2)}) copy-start(f32[128,64]{0,1:T(8,128)} %param.12) | copy-start | bytes 98308
  7.2 12.0 %copy-start.9 = (s32[1,1,32]{2,1,0:T(1,128)S(1)}, s32[1,1,32]{2,1,0:T(1,128)}, u32[]{:S(2)}) copy-start(s32[1,1,32]{2,1,0:T(1,128)} %param.10) | copy-start | bytes 388
  10.6 15.8 %all-to-all-start = ((f32[32,1,256]{2,1,0:T(1,128)}), f32[32,1,256]{2,1,0:T(1,128)S(1)}, u32[]{:S(2)}, u32[]{:S(2)}) async-start(f32[32,1,256]{2,1,0:T(1,128)} %bitcast.4), calls=%async_computation | async-start | bytes 65536 | tf_op jit(solution)/shard_map/all_to_all | solution.py:126
  26.5 8.1 %copy-start.5 = (f32[64,4096]{1,0:T(8,128)S(1)}, f32[64,4096]{1,0:T(8,128)}, u32[]{:S(2)}) copy-start(f32[64,4096]{1,0:T(8,128)} %param.13) | copy-start | bytes 3145732
  26.5 35.0 %all-to-all-start.2 = ((f32[32,128,128]{2,1,0:T(8,128)}), f32[32,128,128]{2,1,0:T(8,128)S(1)}, u32[]{:S(2)}, u32[]{:S(2)}) async-start(f32[32,128,128]{2,1,0:T(8,128)} %get-tuple-element.12), calls=%async_computation.2 | async-start | bytes 4194304 | tf_op jit(solution)/shard_map/all_to_all | solution.py:110
  33.6 68.2 %all-reduce.9.cloned.1.call-start = ((), (), s32[]{:S(2)}) async-start(), calls=%async_computation.8 | async-start | bytes 4325376 | tf_op jit(solution)/shard_map/psum | solution.py:113
  61.5 1.3 copy-start.1
  61.5 8.3 %copy-start.7 = (s32[1,1,32,256]{3,2,1,0:T(8,128)S(1)}, s32[1,1,32,256]{3,2,1,0:T(8,128)}, u32[]{:S(2)}) copy-start(s32[1,1,32,256]{3,2,1,0:T(8,128)} %param.11) | copy-start | bytes 98308
  62.8 34.7 %all-to-all-start.1 = ((f32[32,128,128]{2,1,0:T(8,128)}), f32[32,128,128]{2,1,0:T(8,128)}, u32[]{:S(2)}, u32[]{:S(2)}) async-start(f32[32,128,128]{2,1,0:T(8,128)} %get-tuple-element.13), calls=%async_computation.1 | async-start | bytes 4194304 | tf_op jit(solution)/shard_map/all_to_all | solution.py:110
  69.5 101.1 %all-reduce.5.cloned.1.call-start = ((), (), s32[]{:S(2)}) async-start(), calls=%async_computation.6 | async-start | bytes 4194304 | tf_op jit(solution)/shard_map/psum | solution.py:138
  111.9 1.6 copy-start.2
  113.5 57.2 %copy-start.6 = (f32[128,128]{1,0:T(8,128)S(1)}, f32[128,128]{1,0:T(8,128)}, u32[]{:S(2)}) copy-start(f32[128,128]{1,0:T(8,128)} %get-tuple-element.6) | copy-start | bytes 196612
  193.6 16.4 %copy-start.8 = (f32[2048]{0:T(1024)S(1)}, f32[2048]{0:T(1024)}, u32[]{:S(2)}) copy-start(f32[2048]{0:T(1024)} %param.7) | copy-start | bytes 24580
  193.6 14.9 %all-to-all-start.3 = ((f32[32,1,256]{2,1,0:T(1,128)}), f32[32,1,256]{2,1,0:T(1,128)S(1)}, u32[]{:S(2)}, u32[]{:S(2)}) async-start(f32[32,1,256]{2,1,0:T(1,128)} %bitcast.56), calls=%async_computation.3 | async-start | bytes 65536 | tf_op jit(solution)/shard_map/all_to_all | solution.py:145
  201.3 91.6 %all-reduce.7.cloned.1.call-start = ((), (), s32[]{:S(2)}) async-start(), calls=%async_computation.7 | async-start | bytes 4194304 | tf_op jit(solution)/shard_map/psum | solution.py:138
  237.9 55.0 %copy-start.3 = (f32[4096,128]{1,0:T(8,128)S(1)}, f32[4096,128]{1,0:T(8,128)}, u32[]{:S(2)}) copy-start(f32[4096,128]{1,0:T(8,128)} %get-tuple-element.7) | copy-start | bytes 6291460
  297.6 25.2 %copy-start.4 = (f32[4096,128]{1,0:T(8,128)S(1)}, f32[4096,128]{1,0:T(8,128)}, u32[]{:S(2)}) copy-start(f32[4096,128]{1,0:T(8,128)} %all-reduce.7.cloned.1.call-done) | copy-start | bytes 6291460
  315.3 14.8 %all-to-all-start.5 = ((f32[32,1,256]{2,1,0:T(1,128)}), f32[32,1,256]{2,1,0:T(1,128)S(1)}, u32[]{:S(2)}, u32[]{:S(2)}) async-start(f32[32,1,256]{2,1,0:T(1,128)} %bitcast.57), calls=%async_computation.5 | async-start | bytes 65536 | tf_op jit(solution)/shard_map/all_to_all | solution.py:145
Sparse Core Ops, SparseCore 0:
  39.5 62.2 all-reduce.8
  112.0 58.6 all-reduce.4
  238.1 54.7 all-reduce.6

commit v10 on v9

--- a/solution.py
+++ b/solution.py
@@ -70,15 +70,24 @@
         return carry
 
     lax.fori_loop(0, feat_ref.shape[0] // UNROLL, body, 0)
-    lanes = out_ref.shape[1]
+    lanes = feat_ref.shape[1]
+    chunk = out_ref.shape[1]
+    ones = jnp.ones((8, lanes), jnp.bfloat16)
 
-    def reduce_block(block, carry):
-        start = pl.multiple_of(block * lanes, lanes)
-        prod = rows_ref[pl.ds(start, lanes), :] * feat_ref[pl.ds(start, lanes), :]
-        out_ref[pl.ds(block, 1), :] = jnp.sum(prod.T, axis=0, keepdims=True)
+    def reduce_chunk(c, carry):
+        start = pl.multiple_of(c * chunk, chunk)
+        prod = rows_ref[pl.ds(start, chunk), :] * feat_ref[pl.ds(start, chunk), :]
+        sums = jnp.zeros((8, chunk), jnp.float32)
+        for _ in range(3):
+            part = prod.astype(jnp.bfloat16)
+            prod = prod - part.astype(jnp.float32)
+            sums = sums + lax.dot_general(
+                ones, part, (((1,), (1,)), ((), ())), preferred_element_type=jnp.float32
+            )
+        out_ref[pl.ds(c, 1), :] = sums[0:1, :]
         return carry
 
-    lax.fori_loop(0, out_ref.shape[0], reduce_block, 0)
+    lax.fori_loop(0, out_ref.shape[0], reduce_chunk, 0)
 
 
 def row_gather_dot(idx, table, feat):
@@ -86,7 +95,7 @@
     vmem = pl.BlockSpec(memory_space=pltpu.VMEM)
     return pl.pallas_call(
         gather_kernel,
-        out_shape=jax.ShapeDtypeStruct((feat.shape[0] // 128, 128), jnp.float32),
+        out_shape=jax.ShapeDtypeStruct((8, feat.shape[0] // 8), jnp.float32),
         in_specs=[smem, vmem, vmem],
         out_specs=vmem,
         scratch_shapes=[pltpu.VMEM(feat.shape, jnp.float32)],

time: 340 us -> 334 us (0.982)
  Pallas kernels: 70.9 us -> 62.4 us
    pallas_call x2, Pallas kernels: 35.3 us -> 26.7 us  [row_gather_dot(): pl.pallas_call(gather_kernel, out_shape=jax.ShapeDtypeStruct((8, feat.sha...]
where the time goes in v10:
time: 334 us; the launch traced here: 333 us
  waiting for transfers between devices  159 us (48%)
  Pallas kernels  62.4 us (19%)
  starting transfers between devices  37.8 us (11%)
  matrix products  26.5 us (8%)
  between operations  13.9 us (4%)
  local copies, waits for them, and re-layouts  12.6 us (4%)
  blocking collectives  11 us (3%)
  other arithmetic  9.16 us (3%)
    psum x2, waiting for transfers between devices, on_device(): coeff_sum = lax.psum(partial_coeff, 'shell')  108 us
    all_to_all x2, waiting for transfers between devices, on_device(): lax.all_to_all(masked[:, h * half:(h + 1) * half], 'space', 0, 0, tiled=T...  37 us
    pallas_call x3, Pallas kernels, row_scatter(): pl.pallas_call(scatter_kernel, out_shape=jax.ShapeDtypeStruct(init.shape,...  35.7 us
    pallas_call x2, Pallas kernels, row_gather_dot(): pl.pallas_call(gather_kernel, out_shape=jax.ShapeDtypeStruct((8, feat.sha...  26.7 us
    all_to_all x2, starting transfers between devices, on_device(): lax.all_to_all(local_grad, 'space', split_axis=0, concat_axis=0, tiled=True)  15.1 us
    all_to_all x2, starting transfers between devices, on_device(): lax.all_to_all(masked[:, h * half:(h + 1) * half], 'space', 0, 0, tiled=T...  13.9 us
    all_to_all x1, blocking collectives, on_device(): lax.all_to_all(picked, 'space', split_axis=0, concat_axis=0, tiled=True)  11 us
    dot_general x2, matrix products, on_device(): adjoint = jnp.dot(coeff_sum, gram, precision=HI) - data_proj  10.1 us
  transfers between devices with their start and end apart: 8, of which 8 were waited for; matrix products, arithmetic and copies ran while one was open for 7% of the time, Pallas kernels for 3%

profile of v10, /device:TPU:1, one launch (start us, length us, event | category | flops | bytes accessed | tf_op | source)
XLA Modules:
  0.0 332.9 jit_solution(6154999847841424314)
XLA Ops:
  10.6 8.6 %all-to-all-start = ((f32[32,1,256]{2,1,0:T(1,128)}), f32[32,1,256]{2,1,0:T(1,128)S(1)}, u32[]{:S(2)}, u32[]{:S(2)}) async-start(f32[32,1,256]{2,1,0:T(1,128)} %bitcast.4), calls=%async_computation | async-start | bytes 65536 | tf_op jit(solution)/shard_map/all_to_all | solution.py:135
  19.3 4.5 %multiply_reduce_fusion = (f32[32,256]{1,0:T(8,128)S(1)}, f32[32,256,128]{2,1,0:T(8,128)S(1)}) fusion(f32[1,1,32,256,128]{4,3,2,1,0:T(8,128)} %param.9, pred[32,256]{1,0:T(8,128)(4,1)S(1)} %iota_compare_fusion.10), kind=kLoop, calls=%fused_computation.8 | loop fusion | flops 3137536 | bytes 8429568 | tf_op jit(solution)/shard_map/reduce_sum | solution.py:129
  26.5 7.1 %all-to-all-start.2 = ((f32[32,128,128]{2,1,0:T(8,128)}), f32[32,128,128]{2,1,0:T(8,128)S(1)}, u32[]{:S(2)}, u32[]{:S(2)}) async-start(f32[32,128,128]{2,1,0:T(8,128)} %get-tuple-element.12), calls=%async_computation.2 | async-start | bytes 4194304 | tf_op jit(solution)/shard_map/all_to_all | solution.py:119
  34.6 4.8 %fusion.42 = f32[4096,128]{1,0:T(8,128)} fusion(f32[64,4096]{1,0:T(8,128)S(1)} %copy-done.5, f32[128,64]{0,1:T(8,128)S(1)} %copy-done), kind=kOutput, calls=%fused_computation.58 | convolution fusion | flops 402653184 | bytes 3178496 | tf_op jit(solution)/shard_map/dot_general | solution.py:123
  39.4 22.1 %all-to-all-done.2 = f32[32,128,128]{2,1,0:T(8,128)S(1)} async-done(((f32[32,128,128]{2,1,0:T(8,128)}), f32[32,128,128]{2,1,0:T(8,128)S(1)}, u32[]{:S(2)}, u32[]{:S(2)}) %all-to-all-start.2) | async-done | bytes 2097184 | tf_op jit(solution)/shard_map/all_to_all | solution.py:119
  62.8 6.7 %all-to-all-start.1 = ((f32[32,128,128]{2,1,0:T(8,128)}), f32[32,128,128]{2,1,0:T(8,128)}, u32[]{:S(2)}, u32[]{:S(2)}) async-start(f32[32,128,128]{2,1,0:T(8,128)} %get-tuple-element.13), calls=%async_computation.1 | async-start | bytes 4194304 | tf_op jit(solution)/shard_map/all_to_all | solution.py:119
  72.5 10.1 %shard_map.86.init_ref = f32[4096,128]{1,0:T(8,128)} custom-call(s32[4096]{0:T(1024)} %get-tuple-element.16.idx_ref, f32[4096]{0:T(1024)} %get-tuple-element.14.xs_ref, f32[4096,128]{1,0:T(8,128)} %bitcast.49, f32[4096,128]{1,0:T(8,128)} %broadcast_6_init_ref.2.init_ref), custom_call_target="tpu_custom_call" | custom-call | tf_op jit(solution)/shard_map/pallas_call | solution.py:56
  82.6 14.9 %all-to-all-done.1 = f32[32,128,128]{2,1,0:T(8,128)} async-done(((f32[32,128,128]{2,1,0:T(8,128)}), f32[32,128,128]{2,1,0:T(8,128)}, u32[]{:S(2)}, u32[]{:S(2)}) %all-to-all-start.1) | async-done | bytes 2097184 | tf_op jit(solution)/shard_map/all_to_all | solution.py:119
  97.5 4.3 %all-reduce.9.cloned.1.call-done = (f32[128,128]{1,0:T(8,128)}, f32[4096,128]{1,0:T(8,128)}) async-done(((f32[128,128]{1,0:T(8,128)}, f32[4096,128]{1,0:T(8,128)}), (f32[128,128]{1,0:T(8,128)}, f32[4096,128]{1,0:T(8,128)})) %all-reduce.9.cloned.1.call-update) | async-done | bytes 2162704 | tf_op jit(solution)/shard_map/psum | solution.py:122
  101.8 10.1 %shard_map.87 = f32[4096,128]{1,0:T(8,128)} custom-call(s32[4096]{0:T(1024)} %get-tuple-element.17.idx_ref, f32[4096]{0:T(1024)} %get-tuple-element.15.xs_ref, f32[4096,128]{1,0:T(8,128)} %bitcast.6.feat_ref, f32[4096,128]{1,0:T(8,128)} %shard_map.86.init_ref), custom_call_target="tpu_custom_call" | custom-call | tf_op jit(solution)/shard_map/pallas_call | solution.py:56
  113.5 4.0 %pad_maximum_fusion = f32[32,256,128]{2,1,0:T(8,128)} fusion(f32[32,128,128]{2,1,0:T(8,128)} %all-to-all-done.1, f32[32,128,128]{2,1,0:T(8,128)S(1)} %copy-done.2), kind=kLoop, calls=%fused_computation.6 | loop fusion | flops 1048576 | bytes 8388608 | tf_op jit(solution)/shard_map/concatenate | solution.py:127
  117.4 53.3 %all-reduce.5.cloned.1.call-done = f32[4096,128]{1,0:T(8,128)} async-done(((f32[4096,128]{1,0:T(8,128)}), f32[4096,128]{1,0:T(8,128)}) %all-reduce.5.cloned.1.call-update) | async-done | bytes 2097168 | tf_op jit(solution)/shard_map/psum | solution.py:147
  170.7 5.4 %convolution_subtract_fusion.1.table_ref = f32[4096,128]{1,0:T(8,128)} fusion(f32[4096,128]{1,0:T(8,128)} %get-tuple-element.7, f32[4096,128]{1,0:T(8,128)} %all-reduce.5.cloned.1.call-done, f32[128,128]{1,0:T(8,128)S(1)} %copy-done.6), kind=kOutput, calls=%fused_computation.3 | convolution fusion | flops 805830656 | bytes 6356992 | tf_op jit(solution)/shard_map/dot_general | solution.py:152
  176.1 13.3 %shard_map.88 = f32[8,1024]{1,0:T(8,128)} custom-call(s32[8192]{0:T(1024)} %bitcast.50, f32[4096,128]{1,0:T(8,128)} %convolution_subtract_fusion.1.table_ref, f32[8192,128]{1,0:T(8,128)} %bitcast.46), custom_call_target="tpu_custom_call" | custom-call | tf_op jit(solution)/shard_map/pallas_call | solution.py:96
  190.8 7.5 %all-to-all-start.3 = ((f32[32,1,256]{2,1,0:T(1,128)}), f32[32,1,256]{2,1,0:T(1,128)S(1)}, u32[]{:S(2)}, u32[]{:S(2)}) async-start(f32[32,1,256]{2,1,0:T(1,128)} %all_to_all.43), calls=%async_computation.3 | async-start | bytes 65536 | tf_op jit(solution)/shard_map/all_to_all | solution.py:154
  199.8 5.7 %all-to-all-done.3 = f32[32,1,256]{2,1,0:T(1,128)S(1)} async-done(((f32[32,1,256]{2,1,0:T(1,128)}), f32[32,1,256]{2,1,0:T(1,128)S(1)}, u32[]{:S(2)}, u32[]{:S(2)}) %all-to-all-start.3) | async-done | bytes 32800 | tf_op jit(solution)/shard_map/all_to_all | solution.py:154
  208.4 11.0 %all_to_all.51 = f32[32,1,256]{2,1,0:T(1,128)} all-to-all(f32[32,1,256]{2,1,0:T(1,128)S(1)} %bitcast.63), channel_id=1, replica_groups=mesh['space'=32,'shell'=4] {'space'}, dimensions={0} | all-to-all | bytes 65536 | tf_op jit(solution)/shard_map/all_to_all | solution.py:135
  219.4 15.5 %shard_map.89 = f32[4096,128]{1,0:T(8,128)} custom-call(s32[8192]{0:T(1024)} %bitcast.51, f32[8192]{0:T(1024)} %bitcast.54, f32[8192,128]{1,0:T(8,128)} %bitcast.47, f32[4096,128]{1,0:T(8,128)} %broadcast_6_init_ref.2.init_ref), custom_call_target="tpu_custom_call" | custom-call | tf_op jit(solution)/shard_map/pallas_call | solution.py:56
  235.0 54.9 %all-reduce.7.cloned.1.call-done = f32[4096,128]{1,0:T(8,128)} async-done(((f32[4096,128]{1,0:T(8,128)}), f32[4096,128]{1,0:T(8,128)}) %all-reduce.7.cloned.1.call-update) | async-done | bytes 2097168 | tf_op jit(solution)/shard_map/psum | solution.py:147
  289.9 4.7 %convolution_subtract_fusion.table_ref = f32[4096,128]{1,0:T(8,128)} fusion(f32[4096,128]{1,0:T(8,128)S(1)} %copy-done.3, f32[4096,128]{1,0:T(8,128)} %all-reduce.7.cloned.1.call-done, f32[128,128]{1,0:T(8,128)S(1)} %copy-done.6), kind=kOutput, calls=%fused_computation.2 | convolution fusion | flops 805830656 | bytes 6356992 | tf_op jit(solution)/shard_map/dot_general | solution.py:152
  294.7 13.4 %shard_map.90 = f32[8,1024]{1,0:T(8,128)} custom-call(s32[8192]{0:T(1024)} %bitcast.52, f32[4096,128]{1,0:T(8,128)} %convolution_subtract_fusion.table_ref, f32[8192,128]{1,0:T(8,128)} %bitcast.48), custom_call_target="tpu_custom_call" | custom-call | tf_op jit(solution)/shard_map/pallas_call | solution.py:96
  309.5 7.5 %all-to-all-start.5 = ((f32[32,1,256]{2,1,0:T(1,128)}), f32[32,1,256]{2,1,0:T(1,128)S(1)}, u32[]{:S(2)}, u32[]{:S(2)}) async-start(f32[32,1,256]{2,1,0:T(1,128)} %all_to_all.44), calls=%async_computation.5 | async-start | bytes 65536 | tf_op jit(solution)/shard_map/all_to_all | solution.py:154
  317.1 3.4 %fusion = f32[64,4096]{1,0:T(8,128)} fusion(f32[64,4096]{1,0:T(8,128)S(1)} %copy-done.5, f32[4096,128]{1,0:T(8,128)S(1)} %copy-done.4, f32[128,64]{0,1:T(8,128)S(1)} %copy-done), kind=kOutput, calls=%fused_computation.5 | convolution fusion | flops 402915328 | bytes 4227072 | tf_op jit(solution)/shard_map/jg,vj->gv/dot_general | solution.py:150
  320.4 3.9 %all-to-all-done.5 = f32[32,1,256]{2,1,0:T(1,128)S(1)} async-done(((f32[32,1,256]{2,1,0:T(1,128)}), f32[32,1,256]{2,1,0:T(1,128)S(1)}, u32[]{:S(2)}, u32[]{:S(2)}) %all-to-all-start.5) | async-done | bytes 32800 | tf_op jit(solution)/shard_map/all_to_all | solution.py:154
  (51 shorter events, 22.3 us)
Async XLA Ops:
  7.2 26.5 %copy-start = (f32[128,64]{0,1:T(8,128)S(1)}, f32[128,64]{0,1:T(8,128)}, u32[]{:S(2)}) copy-start(f32[128,64]{0,1:T(8,128)} %param.12) | copy-start | bytes 98308
  7.2 12.0 %copy-start.9 = (s32[1,1,32]{2,1,0:T(1,128)S(1)}, s32[1,1,32]{2,1,0:T(1,128)}, u32[]{:S(2)}) copy-start(s32[1,1,32]{2,1,0:T(1,128)} %param.10) | copy-start | bytes 388
  10.6 15.8 %all-to-all-start = ((f32[32,1,256]{2,1,0:T(1,128)}), f32[32,1,256]{2,1,0:T(1,128)S(1)}, u32[]{:S(2)}, u32[]{:S(2)}) async-start(f32[32,1,256]{2,1,0:T(1,128)} %bitcast.4), calls=%async_computation | async-start | bytes 65536 | tf_op jit(solution)/shard_map/all_to_all | solution.py:135
  26.5 8.1 %copy-start.5 = (f32[64,4096]{1,0:T(8,128)S(1)}, f32[64,4096]{1,0:T(8,128)}, u32[]{:S(2)}) copy-start(f32[64,4096]{1,0:T(8,128)} %param.13) | copy-start | bytes 3145732
  26.5 35.0 %all-to-all-start.2 = ((f32[32,128,128]{2,1,0:T(8,128)}), f32[32,128,128]{2,1,0:T(8,128)S(1)}, u32[]{:S(2)}, u32[]{:S(2)}) async-start(f32[32,128,128]{2,1,0:T(8,128)} %get-tuple-element.12), calls=%async_computation.2 | async-start | bytes 4194304 | tf_op jit(solution)/shard_map/all_to_all | solution.py:119
  33.6 68.2 %all-reduce.9.cloned.1.call-start = ((), (), s32[]{:S(2)}) async-start(), calls=%async_computation.8 | async-start | bytes 4325376 | tf_op jit(solution)/shard_map/psum | solution.py:122
  61.5 1.3 copy-start.1
  61.5 8.3 %copy-start.7 = (s32[1,1,32,256]{3,2,1,0:T(8,128)S(1)}, s32[1,1,32,256]{3,2,1,0:T(8,128)}, u32[]{:S(2)}) copy-start(s32[1,1,32,256]{3,2,1,0:T(8,128)} %param.11) | copy-start | bytes 98308
  62.8 34.7 %all-to-all-start.1 = ((f32[32,128,128]{2,1,0:T(8,128)}), f32[32,128,128]{2,1,0:T(8,128)}, u32[]{:S(2)}, u32[]{:S(2)}) async-start(f32[32,128,128]{2,1,0:T(8,128)} %get-tuple-element.13), calls=%async_computation.1 | async-start | bytes 4194304 | tf_op jit(solution)/shard_map/all_to_all | solution.py:119
  69.5 101.1 %all-reduce.5.cloned.1.call-start = ((), (), s32[]{:S(2)}) async-start(), calls=%async_computation.6 | async-start | bytes 4194304 | tf_op jit(solution)/shard_map/psum | solution.py:147
  111.9 1.6 copy-start.2
  113.5 57.2 %copy-start.6 = (f32[128,128]{1,0:T(8,128)S(1)}, f32[128,128]{1,0:T(8,128)}, u32[]{:S(2)}) copy-start(f32[128,128]{1,0:T(8,128)} %get-tuple-element.6) | copy-start | bytes 196612
  189.4 17.7 %copy-start.8 = (f32[2048]{0:T(1024)S(1)}, f32[2048]{0:T(1024)}, u32[]{:S(2)}) copy-start(f32[2048]{0:T(1024)} %param.7) | copy-start | bytes 24580
  190.8 14.8 %all-to-all-start.3 = ((f32[32,1,256]{2,1,0:T(1,128)}), f32[32,1,256]{2,1,0:T(1,128)S(1)}, u32[]{:S(2)}, u32[]{:S(2)}) async-start(f32[32,1,256]{2,1,0:T(1,128)} %all_to_all.43), calls=%async_computation.3 | async-start | bytes 65536 | tf_op jit(solution)/shard_map/all_to_all | solution.py:154
  198.3 91.6 %all-reduce.7.cloned.1.call-start = ((), (), s32[]{:S(2)}) async-start(), calls=%async_computation.7 | async-start | bytes 4194304 | tf_op jit(solution)/shard_map/psum | solution.py:147
  234.9 55.0 %copy-start.3 = (f32[4096,128]{1,0:T(8,128)S(1)}, f32[4096,128]{1,0:T(8,128)}, u32[]{:S(2)}) copy-start(f32[4096,128]{1,0:T(8,128)} %get-tuple-element.7) | copy-start | bytes 6291460
  294.6 22.4 %copy-start.4 = (f32[4096,128]{1,0:T(8,128)S(1)}, f32[4096,128]{1,0:T(8,128)}, u32[]{:S(2)}) copy-start(f32[4096,128]{1,0:T(8,128)} %all-reduce.7.cloned.1.call-done) | copy-start | bytes 6291460
  309.5 14.8 %all-to-all-start.5 = ((f32[32,1,256]{2,1,0:T(1,128)}), f32[32,1,256]{2,1,0:T(1,128)S(1)}, u32[]{:S(2)}, u32[]{:S(2)}) async-start(f32[32,1,256]{2,1,0:T(1,128)} %all_to_all.44), calls=%async_computation.5 | async-start | bytes 65536 | tf_op jit(solution)/shard_map/all_to_all | solution.py:154
Sparse Core Ops, SparseCore 0:
  39.5 62.2 all-reduce.8
  112.0 58.6 all-reduce.4
  235.1 54.7 all-reduce.6

commit v11 on v10

--- a/solution.py
+++ b/solution.py
@@ -1,3 +1,5 @@
+import functools
+
 import jax
 import jax.numpy as jnp
 from jax import lax
@@ -31,30 +33,33 @@
 ACCS = 8
 
 
-def scatter_kernel(idx_ref, xs_ref, feat_ref, init_ref, out_ref, *accs):
+def scatter_kernel(slots, pad, idx_ref, xs_ref, feat_ref, init_ref, out_ref, *accs):
     accs[0][...] = init_ref[...]
     for acc in accs[1:]:
         acc[...] = jnp.zeros(acc.shape, acc.dtype)
 
     def body(step, carry):
+        row = step * UNROLL
+        if pad:
+            row = row + (row // slots) * pad
         for u in range(UNROLL):
             k = step * UNROLL + u
             acc = accs[u % ACCS]
-            acc[pl.ds(idx_ref[k], 1), :] += xs_ref[k] * feat_ref[pl.ds(k, 1), :]
+            acc[pl.ds(idx_ref[k], 1), :] += xs_ref[k] * feat_ref[pl.ds(row + u, 1), :]
         return carry
 
-    lax.fori_loop(0, feat_ref.shape[0] // UNROLL, body, 0)
+    lax.fori_loop(0, idx_ref.shape[0] // UNROLL, body, 0)
     total = accs[0][...]
     for acc in accs[1:]:
         total = total + acc[...]
     out_ref[...] = total
 
 
-def row_scatter(idx, xs, feat, init):
+def row_scatter(idx, xs, feat, init, slots=128, pad=0):
     smem = pl.BlockSpec(memory_space=pltpu.SMEM)
     vmem = pl.BlockSpec(memory_space=pltpu.VMEM)
     return pl.pallas_call(
-        scatter_kernel,
+        functools.partial(scatter_kernel, slots, pad),
         out_shape=jax.ShapeDtypeStruct(init.shape, jnp.float32),
         in_specs=[smem, smem, vmem, vmem],
         out_specs=vmem,
@@ -114,33 +119,41 @@
     masked = jnp.where(
         live_slot[:, :, None], seg_features.reshape(blocks, slots, coeffs), jnp.float32(0.0)
     )
-    half = slots // 2
-    feat_parts = [
-        lax.all_to_all(masked[:, h * half:(h + 1) * half], "space", 0, 0, tiled=True)
-        for h in range(2)
-    ]
-    gram = lax.psum(jnp.dot(dictionary, dictionary.T, precision=HI), "shell")
-    data_proj = lax.psum(jnp.dot(measured.T, dictionary.T, precision=HI), "shell")
-    feat_parts[1], gram, data_proj = lax.optimization_barrier((feat_parts[1], gram, data_proj))
-    vox_parts = [voxel_index.reshape(blocks, slots)[:, h * half:(h + 1) * half].reshape(-1)
-                 for h in range(2)]
-    local_feat = jnp.concatenate(feat_parts, axis=1).reshape(blocks * slots, coeffs)
     high, low = one_hot_pair(stream_index, streams)
     column_sq = spread(jnp.sum(masked * masked, axis=2), high, low)
     scaling = 0.5 / (0.5 + column_sq)
+    half = slots // 2
+    pad = 8
+    picked = pick(weights, high, low).reshape(blocks, slots // coeffs, coeffs)
+    first = jnp.concatenate(
+        [masked[:, :half], picked, jnp.zeros((blocks, pad - slots // coeffs, coeffs), jnp.float32)],
+        axis=1,
+    )
+    first = lax.all_to_all(first, "space", 0, 0, tiled=True)
+    second = lax.all_to_all(masked[:, half:], "space", 0, 0, tiled=True)
+    gram = lax.psum(jnp.dot(dictionary, dictionary.T, precision=HI), "shell")
+    data_proj = lax.psum(jnp.dot(measured.T, dictionary.T, precision=HI), "shell")
+    second, gram, data_proj = lax.optimization_barrier((second, gram, data_proj))
+    first_x = first[:, half:half + slots // coeffs].reshape(blocks, slots)
+    vox_parts = [voxel_index.reshape(blocks, slots)[:, h * half:(h + 1) * half].reshape(-1)
+                 for h in range(2)]
+    local_feat = jnp.concatenate([first[:, :half], second], axis=1).reshape(blocks * slots, coeffs)
     current = weights
     residual = jnp.zeros(measured.shape, jnp.float32)
     for iteration in range(ITERS):
-        picked = pick(current, high, low).reshape(blocks, slots)
-        local_x = lax.all_to_all(picked, "space", split_axis=0, concat_axis=0, tiled=True)
         partial_coeff = jnp.zeros((measured.shape[1], coeffs), jnp.float32)
         if iteration == 0:
-            for h in range(2):
-                part_x = local_x[:, h * half:(h + 1) * half].reshape(-1)
-                partial_coeff = row_scatter(
-                    vox_parts[h], part_x, feat_parts[h].reshape(-1, coeffs), partial_coeff
-                )
+            partial_coeff = row_scatter(
+                vox_parts[0], first_x[:, :half].reshape(-1),
+                first.reshape(-1, coeffs), partial_coeff, half, pad,
+            )
+            partial_coeff = row_scatter(
+                vox_parts[1], first_x[:, half:].reshape(-1),
+                second.reshape(-1, coeffs), partial_coeff,
+            )
         else:
+            picked = pick(current, high, low).reshape(blocks, slots)
+            local_x = lax.all_to_all(picked, "space", split_axis=0, concat_axis=0, tiled=True)
             partial_coeff = row_scatter(
                 voxel_index, local_x.reshape(-1), local_feat, partial_coeff
             )

time: 334 us -> 327 us (0.979)
  starting transfers between devices: 37.8 us -> 31.1 us
    all_to_all x3 -> x2, starting transfers between devices: 22.5 us -> 15.7 us  [the longest x1 8.72 us: on_device(): first = lax.all_to_all(first, 'space', 0, 0, tiled=True)]
    all_to_all x3 -> x2, waiting for transfers between devices: 37.4 us -> 38.1 us  [the longest x1 23.5 us: on_device(): first = lax.all_to_all(first, 'space', 0, 0, tiled=True)]
  transfers between devices with their start and end apart: 8 -> 7, of which waited for: 8 -> 7; matrix products, arithmetic and copies ran while one was open for 7% -> 6% of each run, Pallas kernels for 3% -> 3%
where the time goes in v11:
time: 327 us; the launch traced here: 326 us
  waiting for transfers between devices  159 us (49%)
  Pallas kernels  62.6 us (19%)
  starting transfers between devices  31.1 us (10%)
  matrix products  25.2 us (8%)
  between operations  13.9 us (4%)
  other arithmetic  11.6 us (4%)
  local copies, waits for them, and re-layouts  11 us (3%)
  blocking collectives  11 us (3%)
    psum x2, waiting for transfers between devices, on_device(): coeff_sum = lax.psum(partial_coeff, 'shell')  108 us
    pallas_call x3, Pallas kernels, row_scatter(): pl.pallas_call(functools.partial(scatter_kernel, slots, pad), out_shape=j...  35.9 us
    pallas_call x2, Pallas kernels, row_gather_dot(): pl.pallas_call(gather_kernel, out_shape=jax.ShapeDtypeStruct((8, feat.sha...  26.7 us
    all_to_all x1, waiting for transfers between devices, on_device(): first = lax.all_to_all(first, 'space', 0, 0, tiled=True)  23.5 us
    all_to_all x2, starting transfers between devices, on_device(): lax.all_to_all(local_grad, 'space', split_axis=0, concat_axis=0, tiled=True)  15.1 us
    all_to_all x1, waiting for transfers between devices, on_device(): second = lax.all_to_all(masked[:, half:], 'space', 0, 0, tiled=True)  14.6 us
    all_to_all x1, blocking collectives, on_device(): lax.all_to_all(picked, 'space', split_axis=0, concat_axis=0, tiled=True)  11 us
    all_to_all x2, waiting for transfers between devices, on_device(): lax.all_to_all(local_grad, 'space', split_axis=0, concat_axis=0, tiled=True)  9.62 us
  transfers between devices with their start and end apart: 7, of which 7 were waited for; matrix products, arithmetic and copies ran while one was open for 6% of the time, Pallas kernels for 3%

profile of v11, /device:TPU:1, one launch (start us, length us, event | category | flops | bytes accessed | tf_op | source)
XLA Modules:
  0.0 325.8 jit_solution(12635276124940923230)
XLA Ops:
  9.5 4.5 %multiply_reduce_fusion = (f32[32,256]{1,0:T(8,128)S(1)}, f32[32,256,128]{2,1,0:T(8,128)S(1)}) fusion(f32[1,1,32,256,128]{4,3,2,1,0:T(8,128)} %param.9, pred[32,256]{1,0:T(8,128)(4,1)S(1)} %iota_compare_fusion.10), kind=kLoop, calls=%fused_computation.8 | loop fusion | flops 3137536 | bytes 8429568 | tf_op jit(solution)/shard_map/reduce_sum | solution.py:123
  14.0 1.7 fusion.40
  18.6 8.7 %all-to-all-start = ((f32[32,136,128]{2,1,0:T(8,128)}), f32[32,136,128]{2,1,0:T(8,128)S(1)}, u32[]{:S(2)}, u32[]{:S(2)}) async-start(f32[32,136,128]{2,1,0:T(8,128)} %maximum_maximum_fusion), calls=%async_computation | async-start | bytes 4456448 | tf_op jit(solution)/shard_map/all_to_all | solution.py:132
  28.3 4.8 %fusion.42 = f32[4096,128]{1,0:T(8,128)} fusion(f32[64,4096]{1,0:T(8,128)S(1)} %copy-done.5, f32[128,64]{0,1:T(8,128)S(1)} %copy-done), kind=kOutput, calls=%fused_computation.59 | convolution fusion | flops 402653184 | bytes 3178496 | tf_op jit(solution)/shard_map/dot_general | solution.py:135
  33.1 23.5 %all-to-all-done = f32[32,136,128]{2,1,0:T(8,128)S(1)} async-done(((f32[32,136,128]{2,1,0:T(8,128)}), f32[32,136,128]{2,1,0:T(8,128)S(1)}, u32[]{:S(2)}, u32[]{:S(2)}) %all-to-all-start) | async-done | bytes 2228256 | tf_op jit(solution)/shard_map/all_to_all | solution.py:132
  56.6 7.0 %all-to-all-start.1 = ((f32[32,128,128]{2,1,0:T(8,128)}), f32[32,128,128]{2,1,0:T(8,128)}, u32[]{:S(2)}, u32[]{:S(2)}) async-start(f32[32,128,128]{2,1,0:T(8,128)} %get-tuple-element.13), calls=%async_computation.1 | async-start | bytes 4194304 | tf_op jit(solution)/shard_map/all_to_all | solution.py:133
  66.6 10.4 %shard_map.86.init_ref = f32[4096,128]{1,0:T(8,128)} custom-call(s32[4096]{0:T(1024)} %get-tuple-element.16.idx_ref, f32[4096]{0:T(1024)} %get-tuple-element.14.xs_ref, f32[4352,128]{1,0:T(8,128)} %bitcast.50, f32[4096,128]{1,0:T(8,128)} %broadcast_6_init_ref.2.init_ref), custom_call_target="tpu_custom_call" | custom-call | tf_op jit(solution)/shard_map/pallas_call | solution.py:61
  77.0 14.6 %all-to-all-done.1 = f32[32,128,128]{2,1,0:T(8,128)} async-done(((f32[32,128,128]{2,1,0:T(8,128)}), f32[32,128,128]{2,1,0:T(8,128)}, u32[]{:S(2)}, u32[]{:S(2)}) %all-to-all-start.1) | async-done | bytes 2097184 | tf_op jit(solution)/shard_map/all_to_all | solution.py:133
  91.6 3.9 %all-reduce.9.cloned.1.call-done = (f32[128,128]{1,0:T(8,128)}, f32[4096,128]{1,0:T(8,128)}) async-done(((f32[128,128]{1,0:T(8,128)}, f32[4096,128]{1,0:T(8,128)}), (f32[128,128]{1,0:T(8,128)}, f32[4096,128]{1,0:T(8,128)})) %all-reduce.9.cloned.1.call-update) | async-done | bytes 2162704 | tf_op jit(solution)/shard_map/psum | solution.py:134
  95.5 10.1 %shard_map.87 = f32[4096,128]{1,0:T(8,128)} custom-call(s32[4096]{0:T(1024)} %get-tuple-element.17.idx_ref, f32[4096]{0:T(1024)} %get-tuple-element.15.xs_ref, f32[4096,128]{1,0:T(8,128)} %bitcast.6.feat_ref, f32[4096,128]{1,0:T(8,128)} %shard_map.86.init_ref), custom_call_target="tpu_custom_call" | custom-call | tf_op jit(solution)/shard_map/pallas_call | solution.py:61
  107.5 4.2 %pad_maximum_fusion = f32[32,256,128]{2,1,0:T(8,128)} fusion(f32[32,128,128]{2,1,0:T(8,128)} %all-to-all-done.1, f32[32,128,128]{2,1,0:T(8,128)S(1)} %slice.39), kind=kLoop, calls=%fused_computation.6 | loop fusion | flops 1048576 | bytes 8388608 | tf_op jit(solution)/shard_map/concatenate | solution.py:140
  111.7 52.7 %all-reduce.5.cloned.1.call-done = f32[4096,128]{1,0:T(8,128)} async-done(((f32[4096,128]{1,0:T(8,128)}), f32[4096,128]{1,0:T(8,128)}) %all-reduce.5.cloned.1.call-update) | async-done | bytes 2097168 | tf_op jit(solution)/shard_map/psum | solution.py:160
  164.4 4.7 %convolution_subtract_fusion.1.table_ref = f32[4096,128]{1,0:T(8,128)} fusion(f32[4096,128]{1,0:T(8,128)S(1)} %copy-done.3, f32[4096,128]{1,0:T(8,128)} %all-reduce.5.cloned.1.call-done, f32[128,128]{1,0:T(8,128)S(1)} %copy-done.6), kind=kOutput, calls=%fused_computation.3 | convolution fusion | flops 805830656 | bytes 6356992 | tf_op jit(solution)/shard_map/dot_general | solution.py:165
  169.2 13.3 %shard_map.88 = f32[8,1024]{1,0:T(8,128)} custom-call(s32[8192]{0:T(1024)} %bitcast.51, f32[4096,128]{1,0:T(8,128)} %convolution_subtract_fusion.1.table_ref, f32[8192,128]{1,0:T(8,128)} %bitcast.47), custom_call_target="tpu_custom_call" | custom-call | tf_op jit(solution)/shard_map/pallas_call | solution.py:101
  183.8 7.5 %all-to-all-start.2 = ((f32[32,1,256]{2,1,0:T(1,128)}), f32[32,1,256]{2,1,0:T(1,128)S(1)}, u32[]{:S(2)}, u32[]{:S(2)}) async-start(f32[32,1,256]{2,1,0:T(1,128)} %all_to_all.32), calls=%async_computation.2 | async-start | bytes 65536 | tf_op jit(solution)/shard_map/all_to_all | solution.py:167
  192.9 5.8 %all-to-all-done.2 = f32[32,1,256]{2,1,0:T(1,128)S(1)} async-done(((f32[32,1,256]{2,1,0:T(1,128)}), f32[32,1,256]{2,1,0:T(1,128)S(1)}, u32[]{:S(2)}, u32[]{:S(2)}) %all-to-all-start.2) | async-done | bytes 32800 | tf_op jit(solution)/shard_map/all_to_all | solution.py:167
  201.5 11.0 %all_to_all.39 = f32[32,1,256]{2,1,0:T(1,128)} all-to-all(f32[32,1,256]{2,1,0:T(1,128)S(1)} %bitcast.66), channel_id=1, replica_groups=mesh['space'=32,'shell'=4] {'space'}, dimensions={0} | all-to-all | bytes 65536 | tf_op jit(solution)/shard_map/all_to_all | solution.py:156
  212.5 15.4 %shard_map.89 = f32[4096,128]{1,0:T(8,128)} custom-call(s32[8192]{0:T(1024)} %bitcast.52, f32[8192]{0:T(1024)} %bitcast.55, f32[8192,128]{1,0:T(8,128)} %bitcast.48, f32[4096,128]{1,0:T(8,128)} %broadcast_6_init_ref.2.init_ref), custom_call_target="tpu_custom_call" | custom-call | tf_op jit(solution)/shard_map/pallas_call | solution.py:61
  227.9 54.9 %all-reduce.7.cloned.1.call-done = f32[4096,128]{1,0:T(8,128)} async-done(((f32[4096,128]{1,0:T(8,128)}), f32[4096,128]{1,0:T(8,128)}) %all-reduce.7.cloned.1.call-update) | async-done | bytes 2097168 | tf_op jit(solution)/shard_map/psum | solution.py:160
  282.9 4.7 %convolution_subtract_fusion.table_ref = f32[4096,128]{1,0:T(8,128)} fusion(f32[4096,128]{1,0:T(8,128)S(1)} %copy-done.3, f32[4096,128]{1,0:T(8,128)} %all-reduce.7.cloned.1.call-done, f32[128,128]{1,0:T(8,128)S(1)} %copy-done.6), kind=kOutput, calls=%fused_computation.2 | convolution fusion | flops 805830656 | bytes 6356992 | tf_op jit(solution)/shard_map/dot_general | solution.py:165
  287.6 13.4 %shard_map.90 = f32[8,1024]{1,0:T(8,128)} custom-call(s32[8192]{0:T(1024)} %bitcast.53, f32[4096,128]{1,0:T(8,128)} %convolution_subtract_fusion.table_ref, f32[8192,128]{1,0:T(8,128)} %bitcast.49), custom_call_target="tpu_custom_call" | custom-call | tf_op jit(solution)/shard_map/pallas_call | solution.py:101
  302.4 7.5 %all-to-all-start.4 = ((f32[32,1,256]{2,1,0:T(1,128)}), f32[32,1,256]{2,1,0:T(1,128)S(1)}, u32[]{:S(2)}, u32[]{:S(2)}) async-start(f32[32,1,256]{2,1,0:T(1,128)} %all_to_all.33), calls=%async_computation.4 | async-start | bytes 65536 | tf_op jit(solution)/shard_map/all_to_all | solution.py:167
  310.0 3.4 %fusion = f32[64,4096]{1,0:T(8,128)} fusion(f32[64,4096]{1,0:T(8,128)S(1)} %copy-done.5, f32[4096,128]{1,0:T(8,128)S(1)} %copy-done.4, f32[128,64]{0,1:T(8,128)S(1)} %copy-done), kind=kOutput, calls=%fused_computation.5 | convolution fusion | flops 402915328 | bytes 4227072 | tf_op jit(solution)/shard_map/jg,vj->gv/dot_general | solution.py:163
  313.3 3.9 %all-to-all-done.4 = f32[32,1,256]{2,1,0:T(1,128)S(1)} async-done(((f32[32,1,256]{2,1,0:T(1,128)}), f32[32,1,256]{2,1,0:T(1,128)S(1)}, u32[]{:S(2)}, u32[]{:S(2)}) %all-to-all-start.4) | async-done | bytes 32800 | tf_op jit(solution)/shard_map/all_to_all | solution.py:167
  (52 shorter events, 20.2 us)
Async XLA Ops:
  7.2 20.2 %copy-start = (f32[128,64]{0,1:T(8,128)S(1)}, f32[128,64]{0,1:T(8,128)}, u32[]{:S(2)}) copy-start(f32[128,64]{0,1:T(8,128)} %param.12) | copy-start | bytes 98308
  18.6 9.7 %copy-start.5 = (f32[64,4096]{1,0:T(8,128)S(1)}, f32[64,4096]{1,0:T(8,128)}, u32[]{:S(2)}) copy-start(f32[64,4096]{1,0:T(8,128)} %param.13) | copy-start | bytes 3145732
  18.6 38.0 %all-to-all-start = ((f32[32,136,128]{2,1,0:T(8,128)}), f32[32,136,128]{2,1,0:T(8,128)S(1)}, u32[]{:S(2)}, u32[]{:S(2)}) async-start(f32[32,136,128]{2,1,0:T(8,128)} %maximum_maximum_fusion), calls=%async_computation | async-start | bytes 4456448 | tf_op jit(solution)/shard_map/all_to_all | solution.py:132
  27.3 68.2 %all-reduce.9.cloned.1.call-start = ((), (), s32[]{:S(2)}) async-start(), calls=%async_computation.7 | async-start | bytes 4325376 | tf_op jit(solution)/shard_map/psum | solution.py:134
  56.6 7.9 %copy-start.1 = (f32[32,136,128]{2,1,0:T(8,128)}, f32[32,136,128]{2,1,0:T(8,128)S(1)}, u32[]{:S(2)}) copy-start(f32[32,136,128]{2,1,0:T(8,128)S(1)} %all-to-all-done) | copy-start | bytes 6684676
  56.6 7.2 %copy-start.7 = (s32[1,1,32,256]{3,2,1,0:T(8,128)S(1)}, s32[1,1,32,256]{3,2,1,0:T(8,128)}, u32[]{:S(2)}) copy-start(s32[1,1,32,256]{3,2,1,0:T(8,128)} %param.11) | copy-start | bytes 98308
  56.6 35.0 %all-to-all-start.1 = ((f32[32,128,128]{2,1,0:T(8,128)}), f32[32,128,128]{2,1,0:T(8,128)}, u32[]{:S(2)}, u32[]{:S(2)}) async-start(f32[32,128,128]{2,1,0:T(8,128)} %get-tuple-element.13), calls=%async_computation.1 | async-start | bytes 4194304 | tf_op jit(solution)/shard_map/all_to_all | solution.py:133
  63.6 100.8 %all-reduce.5.cloned.1.call-start = ((), (), s32[]{:S(2)}) async-start(), calls=%async_computation.5 | async-start | bytes 4194304 | tf_op jit(solution)/shard_map/psum | solution.py:160
  105.6 1.6 copy-start.2
  107.5 56.9 %copy-start.3 = (f32[4096,128]{1,0:T(8,128)S(1)}, f32[4096,128]{1,0:T(8,128)}, u32[]{:S(2)}) copy-start(f32[4096,128]{1,0:T(8,128)} %get-tuple-element.7) | copy-start | bytes 6291460
  107.5 56.9 %copy-start.6 = (f32[128,128]{1,0:T(8,128)S(1)}, f32[128,128]{1,0:T(8,128)}, u32[]{:S(2)}) copy-start(f32[128,128]{1,0:T(8,128)} %get-tuple-element.6) | copy-start | bytes 196612
  182.4 17.7 %copy-start.8 = (f32[2048]{0:T(1024)S(1)}, f32[2048]{0:T(1024)}, u32[]{:S(2)}) copy-start(f32[2048]{0:T(1024)} %param.7) | copy-start | bytes 24580
  183.8 14.8 %all-to-all-start.2 = ((f32[32,1,256]{2,1,0:T(1,128)}), f32[32,1,256]{2,1,0:T(1,128)S(1)}, u32[]{:S(2)}, u32[]{:S(2)}) async-start(f32[32,1,256]{2,1,0:T(1,128)} %all_to_all.32), calls=%async_computation.2 | async-start | bytes 65536 | tf_op jit(solution)/shard_map/all_to_all | solution.py:167
  191.4 91.5 %all-reduce.7.cloned.1.call-start = ((), (), s32[]{:S(2)}) async-start(), calls=%async_computation.6 | async-start | bytes 4194304 | tf_op jit(solution)/shard_map/psum | solution.py:160
  287.6 22.4 %copy-start.4 = (f32[4096,128]{1,0:T(8,128)S(1)}, f32[4096,128]{1,0:T(8,128)}, u32[]{:S(2)}) copy-start(f32[4096,128]{1,0:T(8,128)} %all-reduce.7.cloned.1.call-done) | copy-start | bytes 6291460
  302.4 14.8 %all-to-all-start.4 = ((f32[32,1,256]{2,1,0:T(1,128)}), f32[32,1,256]{2,1,0:T(1,128)S(1)}, u32[]{:S(2)}, u32[]{:S(2)}) async-start(f32[32,1,256]{2,1,0:T(1,128)} %all_to_all.33), calls=%async_computation.4 | async-start | bytes 65536 | tf_op jit(solution)/shard_map/all_to_all | solution.py:167
Sparse Core Ops, SparseCore 0:
  33.3 62.2 all-reduce.8
  105.8 58.6 all-reduce.4
  228.1 54.7 all-reduce.6

commit v12 on v11

--- a/solution.py
+++ b/solution.py
@@ -120,8 +120,6 @@
         live_slot[:, :, None], seg_features.reshape(blocks, slots, coeffs), jnp.float32(0.0)
     )
     high, low = one_hot_pair(stream_index, streams)
-    column_sq = spread(jnp.sum(masked * masked, axis=2), high, low)
-    scaling = 0.5 / (0.5 + column_sq)
     half = slots // 2
     pad = 8
     picked = pick(weights, high, low).reshape(blocks, slots // coeffs, coeffs)
@@ -130,6 +128,9 @@
         axis=1,
     )
     first = lax.all_to_all(first, "space", 0, 0, tiled=True)
+    first, own_feat = lax.optimization_barrier((first, masked))
+    column_sq = spread(jnp.sum(own_feat * own_feat, axis=2), high, low)
+    scaling = 0.5 / (0.5 + column_sq)
     second = lax.all_to_all(masked[:, half:], "space", 0, 0, tiled=True)
     gram = lax.psum(jnp.dot(dictionary, dictionary.T, precision=HI), "shell")
     data_proj = lax.psum(jnp.dot(measured.T, dictionary.T, precision=HI), "shell")

time: 327 us -> 327 us (level)
    select_n x0 -> x1, other arithmetic: none -> 3.58 us  [on_device(): jnp.where(live_slot[:, :, None], seg_features.reshape(blocks, slots, coef...]
    reduce_sum x1, other arithmetic: 4.48 us -> 1.15 us  [on_device(): column_sq = spread(jnp.sum(own_feat * own_feat, axis=2), high, low)]
where the time goes in v12:
time: 327 us; the launch traced here: 326 us
  waiting for transfers between devices  157 us (48%)
  Pallas kernels  62.9 us (19%)
  starting transfers between devices  31.3 us (10%)
  matrix products  25.2 us (8%)
  between operations  13.9 us (4%)
  local copies, waits for them, and re-layouts  12.9 us (4%)
  other arithmetic  11.9 us (4%)
  blocking collectives  11.1 us (3%)
    psum x2, waiting for transfers between devices, on_device(): coeff_sum = lax.psum(partial_coeff, 'shell')  106 us
    pallas_call x3, Pallas kernels, row_scatter(): pl.pallas_call(functools.partial(scatter_kernel, slots, pad), out_shape=j...  36.1 us
    pallas_call x2, Pallas kernels, row_gather_dot(): pl.pallas_call(gather_kernel, out_shape=jax.ShapeDtypeStruct((8, feat.sha...  26.7 us
    all_to_all x1, waiting for transfers between devices, on_device(): first = lax.all_to_all(first, 'space', 0, 0, tiled=True)  23.5 us
    all_to_all x2, starting transfers between devices, on_device(): lax.all_to_all(local_grad, 'space', split_axis=0, concat_axis=0, tiled=True)  15.1 us
    all_to_all x1, waiting for transfers between devices, on_device(): second = lax.all_to_all(masked[:, half:], 'space', 0, 0, tiled=True)  14.5 us
    all_to_all x1, blocking collectives, on_device(): lax.all_to_all(picked, 'space', split_axis=0, concat_axis=0, tiled=True)  11.1 us
    dot_general x2, matrix products, on_device(): adjoint = jnp.dot(coeff_sum, gram, precision=HI) - data_proj  9.47 us
  transfers between devices with their start and end apart: 7, of which 7 were waited for; matrix products, arithmetic and copies ran while one was open for 6% of the time, Pallas kernels for 3%

profile of v12, /device:TPU:1, one launch (start us, length us, event | category | flops | bytes accessed | tf_op | source)
XLA Modules:
  0.0 326.1 jit_solution(5680468433566951567)
XLA Ops:
  9.5 3.6 %bitcast_select_fusion = f32[32,256,128]{2,1,0:T(8,128)S(1)} fusion(f32[1,1,32,256,128]{4,3,2,1,0:T(8,128)} %param.9, pred[32,256]{1,0:T(8,128)(4,1)S(1)} %iota_compare_fusion.10), kind=kLoop, calls=%fused_computation.7 | loop fusion | flops 1048576 | bytes 8396800 | tf_op jit(solution)/shard_map/jit(_where)/select_n | solution.py:119
  13.1 2.0 fusion.40
  18.6 8.7 %all-to-all-start = ((f32[32,136,128]{2,1,0:T(8,128)}), f32[32,136,128]{2,1,0:T(8,128)S(1)}, u32[]{:S(2)}, u32[]{:S(2)}) async-start(f32[32,136,128]{2,1,0:T(8,128)} %maximum_maximum_fusion), calls=%async_computation | async-start | bytes 4456448 | tf_op jit(solution)/shard_map/all_to_all | solution.py:130
  28.4 4.8 %fusion.42 = f32[4096,128]{1,0:T(8,128)} fusion(f32[64,4096]{1,0:T(8,128)S(1)} %copy-done.7, f32[128,64]{0,1:T(8,128)S(1)} %copy-done), kind=kOutput, calls=%fused_computation.59 | convolution fusion | flops 402653184 | bytes 3178496 | tf_op jit(solution)/shard_map/dot_general | solution.py:136
  33.1 23.5 %all-to-all-done = f32[32,136,128]{2,1,0:T(8,128)S(1)} async-done(((f32[32,136,128]{2,1,0:T(8,128)}), f32[32,136,128]{2,1,0:T(8,128)S(1)}, u32[]{:S(2)}, u32[]{:S(2)}) %all-to-all-start) | async-done | bytes 2228256 | tf_op jit(solution)/shard_map/all_to_all | solution.py:130
  56.6 7.0 %all-to-all-start.1 = ((f32[32,128,128]{2,1,0:T(8,128)}), f32[32,128,128]{2,1,0:T(8,128)}, u32[]{:S(2)}, u32[]{:S(2)}) async-start(f32[32,128,128]{2,1,0:T(8,128)} %get-tuple-element.14), calls=%async_computation.1 | async-start | bytes 4194304 | tf_op jit(solution)/shard_map/all_to_all | solution.py:134
  66.7 10.4 %shard_map.86.init_ref = f32[4096,128]{1,0:T(8,128)} custom-call(s32[4096]{0:T(1024)} %get-tuple-element.18.idx_ref, f32[4096]{0:T(1024)} %get-tuple-element.16.xs_ref, f32[4352,128]{1,0:T(8,128)} %bitcast.49, f32[4096,128]{1,0:T(8,128)} %broadcast_6_init_ref.2.init_ref), custom_call_target="tpu_custom_call" | custom-call | tf_op jit(solution)/shard_map/pallas_call | solution.py:61
  77.1 14.5 %all-to-all-done.1 = f32[32,128,128]{2,1,0:T(8,128)} async-done(((f32[32,128,128]{2,1,0:T(8,128)}), f32[32,128,128]{2,1,0:T(8,128)}, u32[]{:S(2)}, u32[]{:S(2)}) %all-to-all-start.1) | async-done | bytes 2097184 | tf_op jit(solution)/shard_map/all_to_all | solution.py:134
  91.6 3.9 %all-reduce.9.cloned.1.call-done = (f32[128,128]{1,0:T(8,128)}, f32[4096,128]{1,0:T(8,128)}) async-done(((f32[128,128]{1,0:T(8,128)}, f32[4096,128]{1,0:T(8,128)}), (f32[128,128]{1,0:T(8,128)}, f32[4096,128]{1,0:T(8,128)})) %all-reduce.9.cloned.1.call-update) | async-done | bytes 2162704 | tf_op jit(solution)/shard_map/psum | solution.py:135
  95.5 10.2 %shard_map.87 = f32[4096,128]{1,0:T(8,128)} custom-call(s32[4096]{0:T(1024)} %get-tuple-element.19.idx_ref, f32[4096]{0:T(1024)} %get-tuple-element.17.xs_ref, f32[4096,128]{1,0:T(8,128)} %bitcast.6.feat_ref, f32[4096,128]{1,0:T(8,128)} %shard_map.86.init_ref), custom_call_target="tpu_custom_call" | custom-call | tf_op jit(solution)/shard_map/pallas_call | solution.py:61
  109.8 4.2 %pad_maximum_fusion = f32[32,256,128]{2,1,0:T(8,128)} fusion(f32[32,128,128]{2,1,0:T(8,128)} %all-to-all-done.1, f32[32,128,128]{2,1,0:T(8,128)S(1)} %slice.31), kind=kLoop, calls=%fused_computation.6 | loop fusion | flops 1048576 | bytes 8388608 | tf_op jit(solution)/shard_map/concatenate | solution.py:141
  114.0 50.6 %all-reduce.5.cloned.1.call-done = f32[4096,128]{1,0:T(8,128)} async-done(((f32[4096,128]{1,0:T(8,128)}), f32[4096,128]{1,0:T(8,128)}) %all-reduce.5.cloned.1.call-update) | async-done | bytes 2097168 | tf_op jit(solution)/shard_map/psum | solution.py:161
  164.6 4.7 %convolution_subtract_fusion.1.table_ref = f32[4096,128]{1,0:T(8,128)} fusion(f32[4096,128]{1,0:T(8,128)S(1)} %copy-done.5, f32[4096,128]{1,0:T(8,128)} %all-reduce.5.cloned.1.call-done, f32[128,128]{1,0:T(8,128)S(1)} %copy-done.8), kind=kOutput, calls=%fused_computation.3 | convolution fusion | flops 805830656 | bytes 6356992 | tf_op jit(solution)/shard_map/dot_general | solution.py:166
  169.3 13.3 %shard_map.88 = f32[8,1024]{1,0:T(8,128)} custom-call(s32[8192]{0:T(1024)} %bitcast.50, f32[4096,128]{1,0:T(8,128)} %convolution_subtract_fusion.1.table_ref, f32[8192,128]{1,0:T(8,128)} %bitcast.46), custom_call_target="tpu_custom_call" | custom-call | tf_op jit(solution)/shard_map/pallas_call | solution.py:101
  184.0 7.5 %all-to-all-start.2 = ((f32[32,1,256]{2,1,0:T(1,128)}), f32[32,1,256]{2,1,0:T(1,128)S(1)}, u32[]{:S(2)}, u32[]{:S(2)}) async-start(f32[32,1,256]{2,1,0:T(1,128)} %all_to_all.32), calls=%async_computation.2 | async-start | bytes 65536 | tf_op jit(solution)/shard_map/all_to_all | solution.py:168
  193.3 5.5 %all-to-all-done.2 = f32[32,1,256]{2,1,0:T(1,128)S(1)} async-done(((f32[32,1,256]{2,1,0:T(1,128)}), f32[32,1,256]{2,1,0:T(1,128)S(1)}, u32[]{:S(2)}, u32[]{:S(2)}) %all-to-all-start.2) | async-done | bytes 32800 | tf_op jit(solution)/shard_map/all_to_all | solution.py:168
  201.6 11.1 %all_to_all.39 = f32[32,1,256]{2,1,0:T(1,128)} all-to-all(f32[32,1,256]{2,1,0:T(1,128)S(1)} %bitcast.65), channel_id=1, replica_groups=mesh['space'=32,'shell'=4] {'space'}, dimensions={0} | all-to-all | bytes 65536 | tf_op jit(solution)/shard_map/all_to_all | solution.py:157
  212.7 15.5 %shard_map.89 = f32[4096,128]{1,0:T(8,128)} custom-call(s32[8192]{0:T(1024)} %bitcast.51, f32[8192]{0:T(1024)} %bitcast.53, f32[8192,128]{1,0:T(8,128)} %bitcast.47, f32[4096,128]{1,0:T(8,128)} %broadcast_6_init_ref.2.init_ref), custom_call_target="tpu_custom_call" | custom-call | tf_op jit(solution)/shard_map/pallas_call | solution.py:61
  228.2 54.9 %all-reduce.7.cloned.1.call-done = f32[4096,128]{1,0:T(8,128)} async-done(((f32[4096,128]{1,0:T(8,128)}), f32[4096,128]{1,0:T(8,128)}) %all-reduce.7.cloned.1.call-update) | async-done | bytes 2097168 | tf_op jit(solution)/shard_map/psum | solution.py:161
  283.2 4.7 %convolution_subtract_fusion.table_ref = f32[4096,128]{1,0:T(8,128)} fusion(f32[4096,128]{1,0:T(8,128)S(1)} %copy-done.5, f32[4096,128]{1,0:T(8,128)} %all-reduce.7.cloned.1.call-done, f32[128,128]{1,0:T(8,128)S(1)} %copy-done.8), kind=kOutput, calls=%fused_computation.2 | convolution fusion | flops 805830656 | bytes 6356992 | tf_op jit(solution)/shard_map/dot_general | solution.py:166
  287.9 13.4 %shard_map.90 = f32[8,1024]{1,0:T(8,128)} custom-call(s32[8192]{0:T(1024)} %bitcast.52, f32[4096,128]{1,0:T(8,128)} %convolution_subtract_fusion.table_ref, f32[8192,128]{1,0:T(8,128)} %bitcast.48), custom_call_target="tpu_custom_call" | custom-call | tf_op jit(solution)/shard_map/pallas_call | solution.py:101
  302.7 7.5 %all-to-all-start.4 = ((f32[32,1,256]{2,1,0:T(1,128)}), f32[32,1,256]{2,1,0:T(1,128)S(1)}, u32[]{:S(2)}, u32[]{:S(2)}) async-start(f32[32,1,256]{2,1,0:T(1,128)} %all_to_all.33), calls=%async_computation.4 | async-start | bytes 65536 | tf_op jit(solution)/shard_map/all_to_all | solution.py:168
  310.3 3.4 %fusion = f32[64,4096]{1,0:T(8,128)} fusion(f32[64,4096]{1,0:T(8,128)S(1)} %copy-done.7, f32[4096,128]{1,0:T(8,128)S(1)} %copy-done.6, f32[128,64]{0,1:T(8,128)S(1)} %copy-done), kind=kOutput, calls=%fused_computation.5 | convolution fusion | flops 402915328 | bytes 4227072 | tf_op jit(solution)/shard_map/jg,vj->gv/dot_general | solution.py:164
  313.7 3.9 %all-to-all-done.4 = f32[32,1,256]{2,1,0:T(1,128)S(1)} async-done(((f32[32,1,256]{2,1,0:T(1,128)}), f32[32,1,256]{2,1,0:T(1,128)S(1)}, u32[]{:S(2)}, u32[]{:S(2)}) %all-to-all-start.4) | async-done | bytes 32800 | tf_op jit(solution)/shard_map/all_to_all | solution.py:168
  (57 shorter events, 23.2 us)
Async XLA Ops:
  7.2 20.3 %copy-start = (f32[128,64]{0,1:T(8,128)S(1)}, f32[128,64]{0,1:T(8,128)}, u32[]{:S(2)}) copy-start(f32[128,64]{0,1:T(8,128)} %param.12) | copy-start | bytes 98308
  13.1 2.6 copy-start.1
  18.6 9.7 %copy-start.7 = (f32[64,4096]{1,0:T(8,128)S(1)}, f32[64,4096]{1,0:T(8,128)}, u32[]{:S(2)}) copy-start(f32[64,4096]{1,0:T(8,128)} %param.13) | copy-start | bytes 3145732
  18.6 38.0 %all-to-all-start = ((f32[32,136,128]{2,1,0:T(8,128)}), f32[32,136,128]{2,1,0:T(8,128)S(1)}, u32[]{:S(2)}, u32[]{:S(2)}) async-start(f32[32,136,128]{2,1,0:T(8,128)} %maximum_maximum_fusion), calls=%async_computation | async-start | bytes 4456448 | tf_op jit(solution)/shard_map/all_to_all | solution.py:130
  27.4 68.2 %all-reduce.9.cloned.1.call-start = ((), (), s32[]{:S(2)}) async-start(), calls=%async_computation.7 | async-start | bytes 4325376 | tf_op jit(solution)/shard_map/psum | solution.py:135
  56.6 7.9 %copy-start.3 = (f32[32,136,128]{2,1,0:T(8,128)}, f32[32,136,128]{2,1,0:T(8,128)S(1)}, u32[]{:S(2)}) copy-start(f32[32,136,128]{2,1,0:T(8,128)S(1)} %all-to-all-done) | copy-start | bytes 6684676
  56.6 7.3 %copy-start.9 = (s32[1,1,32,256]{3,2,1,0:T(8,128)S(1)}, s32[1,1,32,256]{3,2,1,0:T(8,128)}, u32[]{:S(2)}) copy-start(s32[1,1,32,256]{3,2,1,0:T(8,128)} %param.11) | copy-start | bytes 98308
  56.6 35.0 %all-to-all-start.1 = ((f32[32,128,128]{2,1,0:T(8,128)}), f32[32,128,128]{2,1,0:T(8,128)}, u32[]{:S(2)}, u32[]{:S(2)}) async-start(f32[32,128,128]{2,1,0:T(8,128)} %get-tuple-element.14), calls=%async_computation.1 | async-start | bytes 4194304 | tf_op jit(solution)/shard_map/all_to_all | solution.py:134
  63.7 100.9 %all-reduce.5.cloned.1.call-start = ((), (), s32[]{:S(2)}) async-start(), calls=%async_computation.5 | async-start | bytes 4194304 | tf_op jit(solution)/shard_map/psum | solution.py:161
  95.5 10.9 %copy-start.4 = (f32[32,136,128]{2,1,0:T(8,128)S(1)}, f32[32,136,128]{2,1,0:T(8,128)}, u32[]{:S(2)}) copy-start(f32[32,136,128]{2,1,0:T(8,128)} %copy-done.3) | copy-start | bytes 6684676
  106.4 2.2 copy-start.2
  109.8 54.8 %copy-start.5 = (f32[4096,128]{1,0:T(8,128)S(1)}, f32[4096,128]{1,0:T(8,128)}, u32[]{:S(2)}) copy-start(f32[4096,128]{1,0:T(8,128)} %get-tuple-element.11) | copy-start | bytes 6291460
  109.8 54.8 %copy-start.8 = (f32[128,128]{1,0:T(8,128)S(1)}, f32[128,128]{1,0:T(8,128)}, u32[]{:S(2)}) copy-start(f32[128,128]{1,0:T(8,128)} %get-tuple-element.10) | copy-start | bytes 196612
  182.6 17.7 %copy-start.10 = (f32[2048]{0:T(1024)S(1)}, f32[2048]{0:T(1024)}, u32[]{:S(2)}) copy-start(f32[2048]{0:T(1024)} %param.7) | copy-start | bytes 24580
  184.0 14.8 %all-to-all-start.2 = ((f32[32,1,256]{2,1,0:T(1,128)}), f32[32,1,256]{2,1,0:T(1,128)S(1)}, u32[]{:S(2)}, u32[]{:S(2)}) async-start(f32[32,1,256]{2,1,0:T(1,128)} %all_to_all.32), calls=%async_computation.2 | async-start | bytes 65536 | tf_op jit(solution)/shard_map/all_to_all | solution.py:168
  191.6 91.6 %all-reduce.7.cloned.1.call-start = ((), (), s32[]{:S(2)}) async-start(), calls=%async_computation.6 | async-start | bytes 4194304 | tf_op jit(solution)/shard_map/psum | solution.py:161
  287.9 22.4 %copy-start.6 = (f32[4096,128]{1,0:T(8,128)S(1)}, f32[4096,128]{1,0:T(8,128)}, u32[]{:S(2)}) copy-start(f32[4096,128]{1,0:T(8,128)} %all-reduce.7.cloned.1.call-done) | copy-start | bytes 6291460
  302.7 14.8 %all-to-all-start.4 = ((f32[32,1,256]{2,1,0:T(1,128)}), f32[32,1,256]{2,1,0:T(1,128)S(1)}, u32[]{:S(2)}, u32[]{:S(2)}) async-start(f32[32,1,256]{2,1,0:T(1,128)} %all_to_all.33), calls=%async_computation.4 | async-start | bytes 65536 | tf_op jit(solution)/shard_map/all_to_all | solution.py:168
Sparse Core Ops, SparseCore 0:
  33.3 62.2 all-reduce.8
  105.9 58.6 all-reduce.4
  228.3 54.7 all-reduce.6

commit v13 on v12

--- a/solution.py
+++ b/solution.py
@@ -116,26 +116,33 @@
     voxel_index = seg_voxel.reshape(blocks * slots)
     counts = pair_counts.reshape(blocks)
     live_slot = lax.broadcasted_iota(jnp.int32, (blocks, slots), 1) < counts[:, None]
-    masked = jnp.where(
-        live_slot[:, :, None], seg_features.reshape(blocks, slots, coeffs), jnp.float32(0.0)
-    )
+    raw = seg_features.reshape(blocks, slots, coeffs)
     high, low = one_hot_pair(stream_index, streams)
     half = slots // 2
     pad = 8
-    picked = pick(weights, high, low).reshape(blocks, slots // coeffs, coeffs)
+    x_rows = slots // coeffs
+    picked = pick(weights, high, low).reshape(blocks, x_rows, coeffs)
+    count_row = jnp.broadcast_to(counts.astype(jnp.float32)[:, None, None], (blocks, 1, coeffs))
     first = jnp.concatenate(
-        [masked[:, :half], picked, jnp.zeros((blocks, pad - slots // coeffs, coeffs), jnp.float32)],
+        [raw[:, :half], picked, count_row,
+         jnp.zeros((blocks, pad - x_rows - 1, coeffs), jnp.float32)],
         axis=1,
     )
     first = lax.all_to_all(first, "space", 0, 0, tiled=True)
-    first, own_feat = lax.optimization_barrier((first, masked))
-    column_sq = spread(jnp.sum(own_feat * own_feat, axis=2), high, low)
+    first, own_feat = lax.optimization_barrier((first, raw))
+    masked_sq = jnp.where(live_slot, jnp.sum(own_feat * own_feat, axis=2), jnp.float32(0.0))
+    column_sq = spread(masked_sq, high, low)
     scaling = 0.5 / (0.5 + column_sq)
-    second = lax.all_to_all(masked[:, half:], "space", 0, 0, tiled=True)
+    second = lax.all_to_all(raw[:, half:], "space", 0, 0, tiled=True)
     gram = lax.psum(jnp.dot(dictionary, dictionary.T, precision=HI), "shell")
     data_proj = lax.psum(jnp.dot(measured.T, dictionary.T, precision=HI), "shell")
     second, gram, data_proj = lax.optimization_barrier((second, gram, data_proj))
-    first_x = first[:, half:half + slots // coeffs].reshape(blocks, slots)
+    source_count = first[:, half + x_rows, 0]
+    live_here = (
+        lax.broadcasted_iota(jnp.int32, (blocks, slots), 1).astype(jnp.float32)
+        < source_count[:, None]
+    )
+    first_x = jnp.where(live_here, first[:, half:half + x_rows].reshape(blocks, slots), 0.0)
     vox_parts = [voxel_index.reshape(blocks, slots)[:, h * half:(h + 1) * half].reshape(-1)
                  for h in range(2)]
     local_feat = jnp.concatenate([first[:, :half], second], axis=1).reshape(blocks * slots, coeffs)
@@ -155,6 +162,7 @@
         else:
             picked = pick(current, high, low).reshape(blocks, slots)
             local_x = lax.all_to_all(picked, "space", split_axis=0, concat_axis=0, tiled=True)
+            local_x = jnp.where(live_here, local_x, 0.0)
             partial_coeff = row_scatter(
                 voxel_index, local_x.reshape(-1), local_feat, partial_coeff
             )
@@ -165,6 +173,7 @@
             )
         adjoint = jnp.dot(coeff_sum, gram, precision=HI) - data_proj
         local_grad = row_gather_dot(voxel_index, adjoint, local_feat).reshape(blocks, slots)
+        local_grad = jnp.where(live_here, local_grad, 0.0)
         grad_slot = lax.all_to_all(local_grad, "space", split_axis=0, concat_axis=0, tiled=True)
         gradient = spread(grad_slot, high, low)
         current = jnp.maximum(current - scaling * gradient, 0.0)

time: 327 us -> 326 us (level)
  blocking collectives: 11.1 us -> 0 us
  waiting for transfers between devices: 157 us -> 164 us
  starting transfers between devices: 31.3 us -> 35 us
    all_to_all x1 -> x0, blocking collectives: 11.1 us -> none  [on_device(): lax.all_to_all(picked, 'space', split_axis=0, concat_axis=0, tiled=True)]
    all_to_all x1 -> x2, waiting for transfers between devices: 14.5 us -> 21.4 us  [the longest x1 14.2 us: on_device(): second = lax.all_to_all(raw[:, half:], 'space', 0, 0, tiled=True)]
    all_to_all x1 -> x2, starting transfers between devices: 7.01 us -> 10.9 us  [the longest x1 7 us: on_device(): second = lax.all_to_all(raw[:, half:], 'space', 0, 0, tiled=True)]
  transfers between devices with their start and end apart: 7 -> 8, of which waited for: 7 -> 8; matrix products, arithmetic and copies ran while one was open for 6% -> 6% of each run, Pallas kernels for 3% -> 3%
where the time goes in v13:
time: 326 us; the launch traced here: 325 us
  waiting for transfers between devices  164 us (50%)
  Pallas kernels  62.8 us (19%)
  starting transfers between devices  35 us (11%)
  matrix products  25.8 us (8%)
  between operations  14 us (4%)
  local copies, waits for them, and re-layouts  13.4 us (4%)
  other arithmetic  9.82 us (3%)
    psum x2, waiting for transfers between devices, on_device(): coeff_sum = lax.psum(partial_coeff, 'shell')  105 us
    pallas_call x3, Pallas kernels, row_scatter(): pl.pallas_call(functools.partial(scatter_kernel, slots, pad), out_shape=j...  36.1 us
    pallas_call x2, Pallas kernels, row_gather_dot(): pl.pallas_call(gather_kernel, out_shape=jax.ShapeDtypeStruct((8, feat.sha...  26.7 us
    all_to_all x1, waiting for transfers between devices, on_device(): first = lax.all_to_all(first, 'space', 0, 0, tiled=True)  23.5 us
    all_to_all x2, starting transfers between devices, on_device(): lax.all_to_all(local_grad, 'space', split_axis=0, concat_axis=0, tiled=True)  15.1 us
    all_to_all x1, waiting for transfers between devices, on_device(): second = lax.all_to_all(raw[:, half:], 'space', 0, 0, tiled=True)  14.2 us
    all_to_all x2, waiting for transfers between devices, on_device(): lax.all_to_all(local_grad, 'space', split_axis=0, concat_axis=0, tiled=True)  9.66 us
    dot_general x2, matrix products, on_device(): adjoint = jnp.dot(coeff_sum, gram, precision=HI) - data_proj  9.43 us
  transfers between devices with their start and end apart: 8, of which 8 were waited for; matrix products, arithmetic and copies ran while one was open for 6% of the time, Pallas kernels for 3%

profile of v13, /device:TPU:1, one launch (start us, length us, event | category | flops | bytes accessed | tf_op | source)
XLA Modules:
  0.0 324.7 jit_solution(16338330784776942891)
XLA Ops:
  8.8 3.9 %fusion.40 = (f32[32,128,128]{2,1,0:T(8,128)}, f32[32,128,128]{2,1,0:T(8,128)S(1)}) fusion(f32[32,256,128]{2,1,0:T(8,128)} %bitcast.50), kind=kLoop, calls=%fused_computation.64 | loop fusion | bytes 8388608 | tf_op jit(solution)/shard_map/slice | solution.py:136
  15.8 8.7 %all-to-all-start = ((f32[32,136,128]{2,1,0:T(8,128)}), f32[32,136,128]{2,1,0:T(8,128)S(1)}, u32[]{:S(2)}, u32[]{:S(2)}) async-start(f32[32,136,128]{2,1,0:T(8,128)} %maximum_maximum_fusion), calls=%async_computation | async-start | bytes 4456448 | tf_op jit(solution)/shard_map/all_to_all | solution.py:131
  25.5 4.8 %fusion.42 = f32[4096,128]{1,0:T(8,128)} fusion(f32[64,4096]{1,0:T(8,128)S(1)} %copy-done.6, f32[128,64]{0,1:T(8,128)S(1)} %copy-done), kind=kOutput, calls=%fused_computation.66 | convolution fusion | flops 402653184 | bytes 3178496 | tf_op jit(solution)/shard_map/dot_general | solution.py:138
  30.3 23.5 %all-to-all-done = f32[32,136,128]{2,1,0:T(8,128)S(1)} async-done(((f32[32,136,128]{2,1,0:T(8,128)}), f32[32,136,128]{2,1,0:T(8,128)S(1)}, u32[]{:S(2)}, u32[]{:S(2)}) %all-to-all-start) | async-done | bytes 2228256 | tf_op jit(solution)/shard_map/all_to_all | solution.py:131
  53.8 7.0 %all-to-all-start.1 = ((f32[32,128,128]{2,1,0:T(8,128)}), f32[32,128,128]{2,1,0:T(8,128)}, u32[]{:S(2)}, u32[]{:S(2)}) async-start(f32[32,128,128]{2,1,0:T(8,128)} %get-tuple-element.14), calls=%async_computation.1 | async-start | bytes 4194304 | tf_op jit(solution)/shard_map/all_to_all | solution.py:136
  64.2 10.4 %shard_map.86.init_ref = f32[4096,128]{1,0:T(8,128)} custom-call(s32[4096]{0:T(1024)} %get-tuple-element.18.idx_ref, f32[4096]{0:T(1024)} %get-tuple-element.16.xs_ref, f32[4352,128]{1,0:T(8,128)} %bitcast.49, f32[4096,128]{1,0:T(8,128)} %broadcast_6_init_ref.2.init_ref), custom_call_target="tpu_custom_call" | custom-call | tf_op jit(solution)/shard_map/pallas_call | solution.py:61
  74.5 14.2 %all-to-all-done.1 = f32[32,128,128]{2,1,0:T(8,128)} async-done(((f32[32,128,128]{2,1,0:T(8,128)}), f32[32,128,128]{2,1,0:T(8,128)}, u32[]{:S(2)}, u32[]{:S(2)}) %all-to-all-start.1) | async-done | bytes 2097184 | tf_op jit(solution)/shard_map/all_to_all | solution.py:136
  88.8 3.9 %all-reduce.9.cloned.1.call-done = (f32[128,128]{1,0:T(8,128)}, f32[4096,128]{1,0:T(8,128)}) async-done(((f32[128,128]{1,0:T(8,128)}, f32[4096,128]{1,0:T(8,128)}), (f32[128,128]{1,0:T(8,128)}, f32[4096,128]{1,0:T(8,128)})) %all-reduce.9.cloned.1.call-update) | async-done | bytes 2162704 | tf_op jit(solution)/shard_map/psum | solution.py:137
  92.7 10.2 %shard_map.87 = f32[4096,128]{1,0:T(8,128)} custom-call(s32[4096]{0:T(1024)} %get-tuple-element.19.idx_ref, f32[4096]{0:T(1024)} %get-tuple-element.17.xs_ref, f32[4096,128]{1,0:T(8,128)} %bitcast.6.feat_ref, f32[4096,128]{1,0:T(8,128)} %shard_map.86.init_ref), custom_call_target="tpu_custom_call" | custom-call | tf_op jit(solution)/shard_map/pallas_call | solution.py:61
  107.0 4.2 %pad_maximum_fusion = f32[32,256,128]{2,1,0:T(8,128)} fusion(f32[32,128,128]{2,1,0:T(8,128)} %all-to-all-done.1, f32[32,128,128]{2,1,0:T(8,128)S(1)} %slice.35), kind=kLoop, calls=%fused_computation.6 | loop fusion | flops 1048576 | bytes 8388608 | tf_op jit(solution)/shard_map/concatenate | solution.py:148
  111.2 50.5 %all-reduce.5.cloned.1.call-done = f32[4096,128]{1,0:T(8,128)} async-done(((f32[4096,128]{1,0:T(8,128)}), f32[4096,128]{1,0:T(8,128)}) %all-reduce.5.cloned.1.call-update) | async-done | bytes 2097168 | tf_op jit(solution)/shard_map/psum | solution.py:169
  161.7 4.7 %convolution_subtract_fusion.1.table_ref = f32[4096,128]{1,0:T(8,128)} fusion(f32[4096,128]{1,0:T(8,128)S(1)} %copy-done.4, f32[4096,128]{1,0:T(8,128)} %all-reduce.5.cloned.1.call-done, f32[128,128]{1,0:T(8,128)S(1)} %copy-done.7), kind=kOutput, calls=%fused_computation.3 | convolution fusion | flops 805830656 | bytes 6356992 | tf_op jit(solution)/shard_map/dot_general | solution.py:174
  166.4 13.3 %shard_map.88 = f32[8,1024]{1,0:T(8,128)} custom-call(s32[8192]{0:T(1024)} %bitcast.52, f32[4096,128]{1,0:T(8,128)} %convolution_subtract_fusion.1.table_ref, f32[8192,128]{1,0:T(8,128)} %bitcast.46), custom_call_target="tpu_custom_call" | custom-call | tf_op jit(solution)/shard_map/pallas_call | solution.py:101
  181.2 7.5 %all-to-all-start.2 = ((f32[32,1,256]{2,1,0:T(1,128)}), f32[32,1,256]{2,1,0:T(1,128)S(1)}, u32[]{:S(2)}, u32[]{:S(2)}) async-start(f32[32,1,256]{2,1,0:T(1,128)} %compare_select_fusion.1), calls=%async_computation.2 | async-start | bytes 65536 | tf_op jit(solution)/shard_map/all_to_all | solution.py:177
  190.2 5.8 %all-to-all-done.2 = f32[32,1,256]{2,1,0:T(1,128)S(1)} async-done(((f32[32,1,256]{2,1,0:T(1,128)}), f32[32,1,256]{2,1,0:T(1,128)S(1)}, u32[]{:S(2)}, u32[]{:S(2)}) %all-to-all-start.2) | async-done | bytes 32800 | tf_op jit(solution)/shard_map/all_to_all | solution.py:177
  199.4 3.9 %all-to-all-start.3 = ((f32[32,1,256]{2,1,0:T(1,128)}), f32[32,1,256]{2,1,0:T(1,128)S(1)}, u32[]{:S(2)}, u32[]{:S(2)}) async-start(f32[32,1,256]{2,1,0:T(1,128)} %bitcast.12), calls=%async_computation.3 | async-start | bytes 65536 | tf_op jit(solution)/shard_map/all_to_all | solution.py:164
  203.5 7.2 %all-to-all-done.3 = f32[32,1,256]{2,1,0:T(1,128)S(1)} async-done(((f32[32,1,256]{2,1,0:T(1,128)}), f32[32,1,256]{2,1,0:T(1,128)S(1)}, u32[]{:S(2)}, u32[]{:S(2)}) %all-to-all-start.3) | async-done | bytes 32800 | tf_op jit(solution)/shard_map/all_to_all | solution.py:164
  211.3 15.4 %shard_map.89 = f32[4096,128]{1,0:T(8,128)} custom-call(s32[8192]{0:T(1024)} %bitcast.53, f32[8192]{0:T(1024)} %broadcast_select_fusion.xs_ref, f32[8192,128]{1,0:T(8,128)} %bitcast.47, f32[4096,128]{1,0:T(8,128)} %broadcast_6_init_ref.2.init_ref), custom_call_target="tpu_custom_call" | custom-call | tf_op jit(solution)/shard_map/pallas_call | solution.py:61
  226.8 54.9 %all-reduce.7.cloned.1.call-done = f32[4096,128]{1,0:T(8,128)} async-done(((f32[4096,128]{1,0:T(8,128)}), f32[4096,128]{1,0:T(8,128)}) %all-reduce.7.cloned.1.call-update) | async-done | bytes 2097168 | tf_op jit(solution)/shard_map/psum | solution.py:169
  281.7 4.7 %convolution_subtract_fusion.table_ref = f32[4096,128]{1,0:T(8,128)} fusion(f32[4096,128]{1,0:T(8,128)S(1)} %copy-done.4, f32[4096,128]{1,0:T(8,128)} %all-reduce.7.cloned.1.call-done, f32[128,128]{1,0:T(8,128)S(1)} %copy-done.7), kind=kOutput, calls=%fused_computation.2 | convolution fusion | flops 805830656 | bytes 6356992 | tf_op jit(solution)/shard_map/dot_general | solution.py:174
  286.4 13.4 %shard_map.90 = f32[8,1024]{1,0:T(8,128)} custom-call(s32[8192]{0:T(1024)} %bitcast.54, f32[4096,128]{1,0:T(8,128)} %convolution_subtract_fusion.table_ref, f32[8192,128]{1,0:T(8,128)} %bitcast.48), custom_call_target="tpu_custom_call" | custom-call | tf_op jit(solution)/shard_map/pallas_call | solution.py:101
  301.3 7.5 %all-to-all-start.4 = ((f32[32,1,256]{2,1,0:T(1,128)}), f32[32,1,256]{2,1,0:T(1,128)S(1)}, u32[]{:S(2)}, u32[]{:S(2)}) async-start(f32[32,1,256]{2,1,0:T(1,128)} %compare_select_fusion), calls=%async_computation.4 | async-start | bytes 65536 | tf_op jit(solution)/shard_map/all_to_all | solution.py:177
  308.9 3.4 %fusion = f32[64,4096]{1,0:T(8,128)} fusion(f32[64,4096]{1,0:T(8,128)S(1)} %copy-done.6, f32[4096,128]{1,0:T(8,128)S(1)} %copy-done.5, f32[128,64]{0,1:T(8,128)S(1)} %copy-done), kind=kOutput, calls=%fused_computation.5 | convolution fusion | flops 402915328 | bytes 4227072 | tf_op jit(solution)/shard_map/jg,vj->gv/dot_general | solution.py:172
  312.3 3.9 %all-to-all-done.4 = f32[32,1,256]{2,1,0:T(1,128)S(1)} async-done(((f32[32,1,256]{2,1,0:T(1,128)}), f32[32,1,256]{2,1,0:T(1,128)S(1)}, u32[]{:S(2)}, u32[]{:S(2)}) %all-to-all-start.4) | async-done | bytes 32800 | tf_op jit(solution)/shard_map/all_to_all | solution.py:177
  (66 shorter events, 23.7 us)
Async XLA Ops:
  7.2 17.4 %copy-start = (f32[128,64]{0,1:T(8,128)S(1)}, f32[128,64]{0,1:T(8,128)}, u32[]{:S(2)}) copy-start(f32[128,64]{0,1:T(8,128)} %param.12) | copy-start | bytes 98308
  8.8 4.0 %copy-start.10 = (s32[1,1,32]{2,1,0:T(1,128)S(1)}, s32[1,1,32]{2,1,0:T(1,128)}, u32[]{:S(2)}) copy-start(s32[1,1,32]{2,1,0:T(1,128)} %param.10) | copy-start | bytes 388
  15.8 9.7 %copy-start.6 = (f32[64,4096]{1,0:T(8,128)S(1)}, f32[64,4096]{1,0:T(8,128)}, u32[]{:S(2)}) copy-start(f32[64,4096]{1,0:T(8,128)} %param.13) | copy-start | bytes 3145732
  15.8 38.0 %all-to-all-start = ((f32[32,136,128]{2,1,0:T(8,128)}), f32[32,136,128]{2,1,0:T(8,128)S(1)}, u32[]{:S(2)}, u32[]{:S(2)}) async-start(f32[32,136,128]{2,1,0:T(8,128)} %maximum_maximum_fusion), calls=%async_computation | async-start | bytes 4456448 | tf_op jit(solution)/shard_map/all_to_all | solution.py:131
  24.5 68.2 %all-reduce.9.cloned.1.call-start = ((), (), s32[]{:S(2)}) async-start(), calls=%async_computation.7 | async-start | bytes 4325376 | tf_op jit(solution)/shard_map/psum | solution.py:137
  53.8 7.9 %copy-start.1 = (f32[32,136,128]{2,1,0:T(8,128)}, f32[32,136,128]{2,1,0:T(8,128)S(1)}, u32[]{:S(2)}) copy-start(f32[32,136,128]{2,1,0:T(8,128)S(1)} %all-to-all-done) | copy-start | bytes 6684676
  53.8 7.3 %copy-start.8 = (s32[1,1,32,256]{3,2,1,0:T(8,128)S(1)}, s32[1,1,32,256]{3,2,1,0:T(8,128)}, u32[]{:S(2)}) copy-start(s32[1,1,32,256]{3,2,1,0:T(8,128)} %param.11) | copy-start | bytes 98308
  53.8 35.0 %all-to-all-start.1 = ((f32[32,128,128]{2,1,0:T(8,128)}), f32[32,128,128]{2,1,0:T(8,128)}, u32[]{:S(2)}, u32[]{:S(2)}) async-start(f32[32,128,128]{2,1,0:T(8,128)} %get-tuple-element.14), calls=%async_computation.1 | async-start | bytes 4194304 | tf_op jit(solution)/shard_map/all_to_all | solution.py:136
  60.8 100.9 %all-reduce.5.cloned.1.call-start = ((), (), s32[]{:S(2)}) async-start(), calls=%async_computation.5 | async-start | bytes 4194304 | tf_op jit(solution)/shard_map/psum | solution.py:169
  92.7 10.9 %copy-start.2 = (f32[32,136,128]{2,1,0:T(8,128)S(1)}, f32[32,136,128]{2,1,0:T(8,128)}, u32[]{:S(2)}) copy-start(f32[32,136,128]{2,1,0:T(8,128)} %copy-done.1) | copy-start | bytes 6684676
  103.6 2.2 copy-start.3
  107.0 54.7 %copy-start.4 = (f32[4096,128]{1,0:T(8,128)S(1)}, f32[4096,128]{1,0:T(8,128)}, u32[]{:S(2)}) copy-start(f32[4096,128]{1,0:T(8,128)} %get-tuple-element.11) | copy-start | bytes 6291460
  107.0 54.7 %copy-start.7 = (f32[128,128]{1,0:T(8,128)S(1)}, f32[128,128]{1,0:T(8,128)}, u32[]{:S(2)}) copy-start(f32[128,128]{1,0:T(8,128)} %get-tuple-element.10) | copy-start | bytes 196612
  180.5 17.0 %copy-start.9 = (f32[2048]{0:T(1024)S(1)}, f32[2048]{0:T(1024)}, u32[]{:S(2)}) copy-start(f32[2048]{0:T(1024)} %param.7) | copy-start | bytes 24580
  181.2 14.8 %all-to-all-start.2 = ((f32[32,1,256]{2,1,0:T(1,128)}), f32[32,1,256]{2,1,0:T(1,128)S(1)}, u32[]{:S(2)}, u32[]{:S(2)}) async-start(f32[32,1,256]{2,1,0:T(1,128)} %compare_select_fusion.1), calls=%async_computation.2 | async-start | bytes 65536 | tf_op jit(solution)/shard_map/all_to_all | solution.py:177
  199.4 11.3 %all-to-all-start.3 = ((f32[32,1,256]{2,1,0:T(1,128)}), f32[32,1,256]{2,1,0:T(1,128)S(1)}, u32[]{:S(2)}, u32[]{:S(2)}) async-start(f32[32,1,256]{2,1,0:T(1,128)} %bitcast.12), calls=%async_computation.3 | async-start | bytes 65536 | tf_op jit(solution)/shard_map/all_to_all | solution.py:164
  203.3 78.4 %all-reduce.7.cloned.1.call-start = ((), (), s32[]{:S(2)}) async-start(), calls=%async_computation.6 | async-start | bytes 4194304 | tf_op jit(solution)/shard_map/psum | solution.py:169
  286.4 22.5 %copy-start.5 = (f32[4096,128]{1,0:T(8,128)S(1)}, f32[4096,128]{1,0:T(8,128)}, u32[]{:S(2)}) copy-start(f32[4096,128]{1,0:T(8,128)} %all-reduce.7.cloned.1.call-done) | copy-start | bytes 6291460
  301.3 14.8 %all-to-all-start.4 = ((f32[32,1,256]{2,1,0:T(1,128)}), f32[32,1,256]{2,1,0:T(1,128)S(1)}, u32[]{:S(2)}, u32[]{:S(2)}) async-start(f32[32,1,256]{2,1,0:T(1,128)} %compare_select_fusion), calls=%async_computation.4 | async-start | bytes 65536 | tf_op jit(solution)/shard_map/all_to_all | solution.py:177
Sparse Core Ops, SparseCore 0:
  30.4 62.2 all-reduce.8
  103.1 58.6 all-reduce.4
  226.9 54.7 all-reduce.6

commit v14 on v13

--- a/solution.py
+++ b/solution.py
@@ -133,7 +133,7 @@
     masked_sq = jnp.where(live_slot, jnp.sum(own_feat * own_feat, axis=2), jnp.float32(0.0))
     column_sq = spread(masked_sq, high, low)
     scaling = 0.5 / (0.5 + column_sq)
-    second = lax.all_to_all(raw[:, half:], "space", 0, 0, tiled=True)
+    second = lax.all_to_all(own_feat[:, half:], "space", 0, 0, tiled=True)
     gram = lax.psum(jnp.dot(dictionary, dictionary.T, precision=HI), "shell")
     data_proj = lax.psum(jnp.dot(measured.T, dictionary.T, precision=HI), "shell")
     second, gram, data_proj = lax.optimization_barrier((second, gram, data_proj))

time: 326 us -> 324 us (level)
  waiting for transfers between devices: 164 us -> 160 us
    all_to_all x1, waiting for transfers between devices: 14.2 us -> 0.05 us  [on_device(): second = lax.all_to_all(own_feat[:, half:], 'space', 0, 0, tiled=True)]
    psum x1, waiting for transfers between devices: 3.92 us -> 14.1 us  [on_device(): gram = lax.psum(jnp.dot(dictionary, dictionary.T, precision=HI), 'shell')]
  transfers between devices with their start and end apart: 8 -> 8, of which waited for: 8 -> 7; matrix products, arithmetic and copies ran while one was open for 6% -> 7% of each run, Pallas kernels for 3% -> 3%
where the time goes in v14:
time: 324 us; the launch traced here: 323 us
  waiting for transfers between devices  160 us (49%)
  Pallas kernels  62.8 us (19%)
  starting transfers between devices  35 us (11%)
  matrix products  25.8 us (8%)
  local copies, waits for them, and re-layouts  15.2 us (5%)
  between operations  14 us (4%)
  other arithmetic  9.85 us (3%)
    psum x2, waiting for transfers between devices, on_device(): coeff_sum = lax.psum(partial_coeff, 'shell')  106 us
    pallas_call x3, Pallas kernels, row_scatter(): pl.pallas_call(functools.partial(scatter_kernel, slots, pad), out_shape=j...  36.1 us
    pallas_call x2, Pallas kernels, row_gather_dot(): pl.pallas_call(gather_kernel, out_shape=jax.ShapeDtypeStruct((8, feat.sha...  26.7 us
    all_to_all x1, waiting for transfers between devices, on_device(): first = lax.all_to_all(first, 'space', 0, 0, tiled=True)  23.5 us
    all_to_all x2, starting transfers between devices, on_device(): lax.all_to_all(local_grad, 'space', split_axis=0, concat_axis=0, tiled=True)  15.1 us
    psum x1, waiting for transfers between devices, on_device(): gram = lax.psum(jnp.dot(dictionary, dictionary.T, precision=HI), 'shell')  14.1 us
    all_to_all x2, waiting for transfers between devices, on_device(): lax.all_to_all(local_grad, 'space', split_axis=0, concat_axis=0, tiled=True)  9.65 us
    dot_general x2, matrix products, on_device(): adjoint = jnp.dot(coeff_sum, gram, precision=HI) - data_proj  9.44 us
  transfers between devices with their start and end apart: 8, of which 7 were waited for; matrix products, arithmetic and copies ran while one was open for 7% of the time, Pallas kernels for 3%

profile of v14, /device:TPU:1, one launch (start us, length us, event | category | flops | bytes accessed | tf_op | source)
XLA Modules:
  0.0 322.8 jit_solution(11366032442749703410)
XLA Ops:
  13.6 8.7 %all-to-all-start = ((f32[32,136,128]{2,1,0:T(8,128)}), f32[32,136,128]{2,1,0:T(8,128)S(1)}, u32[]{:S(2)}, u32[]{:S(2)}) async-start(f32[32,136,128]{2,1,0:T(8,128)} %maximum_maximum_fusion), calls=%async_computation | async-start | bytes 4456448 | tf_op jit(solution)/shard_map/all_to_all | solution.py:131
  23.3 4.8 %fusion.41 = f32[4096,128]{1,0:T(8,128)} fusion(f32[64,4096]{1,0:T(8,128)S(1)} %copy-done.6, f32[128,64]{0,1:T(8,128)S(1)} %copy-done), kind=kOutput, calls=%fused_computation.65 | convolution fusion | flops 402653184 | bytes 3178496 | tf_op jit(solution)/shard_map/dot_general | solution.py:138
  28.1 23.5 %all-to-all-done = f32[32,136,128]{2,1,0:T(8,128)S(1)} async-done(((f32[32,136,128]{2,1,0:T(8,128)}), f32[32,136,128]{2,1,0:T(8,128)S(1)}, u32[]{:S(2)}, u32[]{:S(2)}) %all-to-all-start) | async-done | bytes 2228256 | tf_op jit(solution)/shard_map/all_to_all | solution.py:131
  51.6 4.0 %slice.32 = f32[32,128,128]{2,1,0:T(8,128)} slice(f32[32,256,128]{2,1,0:T(8,128)} %bitcast.51), slice={[0:32], [128:256], [0:128]} | slice | bytes 4194304 | tf_op jit(solution)/shard_map/slice | solution.py:136
  55.6 7.0 %all-to-all-start.1 = ((f32[32,128,128]{2,1,0:T(8,128)}), f32[32,128,128]{2,1,0:T(8,128)}, u32[]{:S(2)}, u32[]{:S(2)}) async-start(f32[32,128,128]{2,1,0:T(8,128)} %slice.32), calls=%async_computation.1 | async-start | bytes 4194304 | tf_op jit(solution)/shard_map/all_to_all | solution.py:136
  65.9 10.4 %shard_map.86.init_ref = f32[4096,128]{1,0:T(8,128)} custom-call(s32[4096]{0:T(1024)} %get-tuple-element.16.idx_ref, f32[4096]{0:T(1024)} %get-tuple-element.14.xs_ref, f32[4352,128]{1,0:T(8,128)} %bitcast.49, f32[4096,128]{1,0:T(8,128)} %broadcast_6_init_ref.2.init_ref), custom_call_target="tpu_custom_call" | custom-call | tf_op jit(solution)/shard_map/pallas_call | solution.py:61
  76.4 14.1 %all-reduce.9.cloned.1.call-done = (f32[128,128]{1,0:T(8,128)}, f32[4096,128]{1,0:T(8,128)}) async-done(((f32[128,128]{1,0:T(8,128)}, f32[4096,128]{1,0:T(8,128)}), (f32[128,128]{1,0:T(8,128)}, f32[4096,128]{1,0:T(8,128)})) %all-reduce.9.cloned.1.call-update) | async-done | bytes 2162704 | tf_op jit(solution)/shard_map/psum | solution.py:137
  90.5 10.2 %shard_map.87 = f32[4096,128]{1,0:T(8,128)} custom-call(s32[4096]{0:T(1024)} %get-tuple-element.17.idx_ref, f32[4096]{0:T(1024)} %get-tuple-element.15.xs_ref, f32[4096,128]{1,0:T(8,128)} %bitcast.6.feat_ref, f32[4096,128]{1,0:T(8,128)} %shard_map.86.init_ref), custom_call_target="tpu_custom_call" | custom-call | tf_op jit(solution)/shard_map/pallas_call | solution.py:61
  101.7 1.9 copy-done.3
  104.9 4.2 %pad_maximum_fusion = f32[32,256,128]{2,1,0:T(8,128)} fusion(f32[32,128,128]{2,1,0:T(8,128)} %all-to-all-done.1, f32[32,128,128]{2,1,0:T(8,128)S(1)} %slice.35), kind=kLoop, calls=%fused_computation.6 | loop fusion | flops 1048576 | bytes 8388608 | tf_op jit(solution)/shard_map/concatenate | solution.py:148
  109.0 50.6 %all-reduce.5.cloned.1.call-done = f32[4096,128]{1,0:T(8,128)} async-done(((f32[4096,128]{1,0:T(8,128)}), f32[4096,128]{1,0:T(8,128)}) %all-reduce.5.cloned.1.call-update) | async-done | bytes 2097168 | tf_op jit(solution)/shard_map/psum | solution.py:169
  159.6 4.7 %convolution_subtract_fusion.1.table_ref = f32[4096,128]{1,0:T(8,128)} fusion(f32[4096,128]{1,0:T(8,128)S(1)} %copy-done.4, f32[4096,128]{1,0:T(8,128)} %all-reduce.5.cloned.1.call-done, f32[128,128]{1,0:T(8,128)S(1)} %copy-done.7), kind=kOutput, calls=%fused_computation.3 | convolution fusion | flops 805830656 | bytes 6356992 | tf_op jit(solution)/shard_map/dot_general | solution.py:174
  164.4 13.3 %shard_map.88 = f32[8,1024]{1,0:T(8,128)} custom-call(s32[8192]{0:T(1024)} %bitcast.53, f32[4096,128]{1,0:T(8,128)} %convolution_subtract_fusion.1.table_ref, f32[8192,128]{1,0:T(8,128)} %bitcast.46), custom_call_target="tpu_custom_call" | custom-call | tf_op jit(solution)/shard_map/pallas_call | solution.py:101
  179.2 7.5 %all-to-all-start.2 = ((f32[32,1,256]{2,1,0:T(1,128)}), f32[32,1,256]{2,1,0:T(1,128)S(1)}, u32[]{:S(2)}, u32[]{:S(2)}) async-start(f32[32,1,256]{2,1,0:T(1,128)} %compare_select_fusion.1), calls=%async_computation.2 | async-start | bytes 65536 | tf_op jit(solution)/shard_map/all_to_all | solution.py:177
  188.2 5.8 %all-to-all-done.2 = f32[32,1,256]{2,1,0:T(1,128)S(1)} async-done(((f32[32,1,256]{2,1,0:T(1,128)}), f32[32,1,256]{2,1,0:T(1,128)S(1)}, u32[]{:S(2)}, u32[]{:S(2)}) %all-to-all-start.2) | async-done | bytes 32800 | tf_op jit(solution)/shard_map/all_to_all | solution.py:177
  197.4 3.9 %all-to-all-start.3 = ((f32[32,1,256]{2,1,0:T(1,128)}), f32[32,1,256]{2,1,0:T(1,128)S(1)}, u32[]{:S(2)}, u32[]{:S(2)}) async-start(f32[32,1,256]{2,1,0:T(1,128)} %bitcast.12), calls=%async_computation.3 | async-start | bytes 65536 | tf_op jit(solution)/shard_map/all_to_all | solution.py:164
  201.4 7.2 %all-to-all-done.3 = f32[32,1,256]{2,1,0:T(1,128)S(1)} async-done(((f32[32,1,256]{2,1,0:T(1,128)}), f32[32,1,256]{2,1,0:T(1,128)S(1)}, u32[]{:S(2)}, u32[]{:S(2)}) %all-to-all-start.3) | async-done | bytes 32800 | tf_op jit(solution)/shard_map/all_to_all | solution.py:164
  209.3 15.5 %shard_map.89 = f32[4096,128]{1,0:T(8,128)} custom-call(s32[8192]{0:T(1024)} %bitcast.54, f32[8192]{0:T(1024)} %broadcast_select_fusion.xs_ref, f32[8192,128]{1,0:T(8,128)} %bitcast.47, f32[4096,128]{1,0:T(8,128)} %broadcast_6_init_ref.2.init_ref), custom_call_target="tpu_custom_call" | custom-call | tf_op jit(solution)/shard_map/pallas_call | solution.py:61
  224.7 54.9 %all-reduce.7.cloned.1.call-done = f32[4096,128]{1,0:T(8,128)} async-done(((f32[4096,128]{1,0:T(8,128)}), f32[4096,128]{1,0:T(8,128)}) %all-reduce.7.cloned.1.call-update) | async-done | bytes 2097168 | tf_op jit(solution)/shard_map/psum | solution.py:169
  279.7 4.7 %convolution_subtract_fusion.table_ref = f32[4096,128]{1,0:T(8,128)} fusion(f32[4096,128]{1,0:T(8,128)S(1)} %copy-done.4, f32[4096,128]{1,0:T(8,128)} %all-reduce.7.cloned.1.call-done, f32[128,128]{1,0:T(8,128)S(1)} %copy-done.7), kind=kOutput, calls=%fused_computation.2 | convolution fusion | flops 805830656 | bytes 6356992 | tf_op jit(solution)/shard_map/dot_general | solution.py:174
  284.4 13.4 %shard_map.90 = f32[8,1024]{1,0:T(8,128)} custom-call(s32[8192]{0:T(1024)} %bitcast.55, f32[4096,128]{1,0:T(8,128)} %convolution_subtract_fusion.table_ref, f32[8192,128]{1,0:T(8,128)} %bitcast.48), custom_call_target="tpu_custom_call" | custom-call | tf_op jit(solution)/shard_map/pallas_call | solution.py:101
  299.4 7.5 %all-to-all-start.4 = ((f32[32,1,256]{2,1,0:T(1,128)}), f32[32,1,256]{2,1,0:T(1,128)S(1)}, u32[]{:S(2)}, u32[]{:S(2)}) async-start(f32[32,1,256]{2,1,0:T(1,128)} %compare_select_fusion), calls=%async_computation.4 | async-start | bytes 65536 | tf_op jit(solution)/shard_map/all_to_all | solution.py:177
  306.9 3.4 %fusion = f32[64,4096]{1,0:T(8,128)} fusion(f32[64,4096]{1,0:T(8,128)S(1)} %copy-done.6, f32[4096,128]{1,0:T(8,128)S(1)} %copy-done.5, f32[128,64]{0,1:T(8,128)S(1)} %copy-done), kind=kOutput, calls=%fused_computation.5 | convolution fusion | flops 402915328 | bytes 4227072 | tf_op jit(solution)/shard_map/jg,vj->gv/dot_general | solution.py:172
  310.3 3.9 %all-to-all-done.4 = f32[32,1,256]{2,1,0:T(1,128)S(1)} async-done(((f32[32,1,256]{2,1,0:T(1,128)}), f32[32,1,256]{2,1,0:T(1,128)S(1)}, u32[]{:S(2)}, u32[]{:S(2)}) %all-to-all-start.4) | async-done | bytes 32800 | tf_op jit(solution)/shard_map/all_to_all | solution.py:177
  (67 shorter events, 23.6 us)
Async XLA Ops:
  7.2 15.2 %copy-start = (f32[128,64]{0,1:T(8,128)S(1)}, f32[128,64]{0,1:T(8,128)}, u32[]{:S(2)}) copy-start(f32[128,64]{0,1:T(8,128)} %param.12) | copy-start | bytes 98308
  8.8 1.8 copy-start.10
  13.6 9.7 %copy-start.6 = (f32[64,4096]{1,0:T(8,128)S(1)}, f32[64,4096]{1,0:T(8,128)}, u32[]{:S(2)}) copy-start(f32[64,4096]{1,0:T(8,128)} %param.13) | copy-start | bytes 3145732
  13.6 38.0 %all-to-all-start = ((f32[32,136,128]{2,1,0:T(8,128)}), f32[32,136,128]{2,1,0:T(8,128)S(1)}, u32[]{:S(2)}, u32[]{:S(2)}) async-start(f32[32,136,128]{2,1,0:T(8,128)} %maximum_maximum_fusion), calls=%async_computation | async-start | bytes 4456448 | tf_op jit(solution)/shard_map/all_to_all | solution.py:131
  22.3 68.2 %all-reduce.9.cloned.1.call-start = ((), (), s32[]{:S(2)}) async-start(), calls=%async_computation.7 | async-start | bytes 4325376 | tf_op jit(solution)/shard_map/psum | solution.py:137
  51.6 11.8 %copy-start.1 = (f32[32,136,128]{2,1,0:T(8,128)}, f32[32,136,128]{2,1,0:T(8,128)S(1)}, u32[]{:S(2)}) copy-start(f32[32,136,128]{2,1,0:T(8,128)S(1)} %all-to-all-done) | copy-start | bytes 6684676
  55.6 7.2 %copy-start.8 = (s32[1,1,32,256]{3,2,1,0:T(8,128)S(1)}, s32[1,1,32,256]{3,2,1,0:T(8,128)}, u32[]{:S(2)}) copy-start(s32[1,1,32,256]{3,2,1,0:T(8,128)} %param.11) | copy-start | bytes 98308
  55.6 35.0 %all-to-all-start.1 = ((f32[32,128,128]{2,1,0:T(8,128)}), f32[32,128,128]{2,1,0:T(8,128)}, u32[]{:S(2)}, u32[]{:S(2)}) async-start(f32[32,128,128]{2,1,0:T(8,128)} %slice.32), calls=%async_computation.1 | async-start | bytes 4194304 | tf_op jit(solution)/shard_map/all_to_all | solution.py:136
  62.6 97.1 %all-reduce.5.cloned.1.call-start = ((), (), s32[]{:S(2)}) async-start(), calls=%async_computation.5 | async-start | bytes 4194304 | tf_op jit(solution)/shard_map/psum | solution.py:169
  90.5 10.9 %copy-start.2 = (f32[32,136,128]{2,1,0:T(8,128)S(1)}, f32[32,136,128]{2,1,0:T(8,128)}, u32[]{:S(2)}) copy-start(f32[32,136,128]{2,1,0:T(8,128)} %copy-done.1) | copy-start | bytes 6684676
  101.4 2.2 copy-start.3
  104.9 54.8 %copy-start.4 = (f32[4096,128]{1,0:T(8,128)S(1)}, f32[4096,128]{1,0:T(8,128)}, u32[]{:S(2)}) copy-start(f32[4096,128]{1,0:T(8,128)} %get-tuple-element.11) | copy-start | bytes 6291460
  104.9 54.8 %copy-start.7 = (f32[128,128]{1,0:T(8,128)S(1)}, f32[128,128]{1,0:T(8,128)}, u32[]{:S(2)}) copy-start(f32[128,128]{1,0:T(8,128)} %get-tuple-element.10) | copy-start | bytes 196612
  178.5 17.0 %copy-start.9 = (f32[2048]{0:T(1024)S(1)}, f32[2048]{0:T(1024)}, u32[]{:S(2)}) copy-start(f32[2048]{0:T(1024)} %param.7) | copy-start | bytes 24580
  179.2 14.8 %all-to-all-start.2 = ((f32[32,1,256]{2,1,0:T(1,128)}), f32[32,1,256]{2,1,0:T(1,128)S(1)}, u32[]{:S(2)}, u32[]{:S(2)}) async-start(f32[32,1,256]{2,1,0:T(1,128)} %compare_select_fusion.1), calls=%async_computation.2 | async-start | bytes 65536 | tf_op jit(solution)/shard_map/all_to_all | solution.py:177
  197.4 11.2 %all-to-all-start.3 = ((f32[32,1,256]{2,1,0:T(1,128)}), f32[32,1,256]{2,1,0:T(1,128)S(1)}, u32[]{:S(2)}, u32[]{:S(2)}) async-start(f32[32,1,256]{2,1,0:T(1,128)} %bitcast.12), calls=%async_computation.3 | async-start | bytes 65536 | tf_op jit(solution)/shard_map/all_to_all | solution.py:164
  201.3 78.4 %all-reduce.7.cloned.1.call-start = ((), (), s32[]{:S(2)}) async-start(), calls=%async_computation.6 | async-start | bytes 4194304 | tf_op jit(solution)/shard_map/psum | solution.py:169
  284.4 22.5 %copy-start.5 = (f32[4096,128]{1,0:T(8,128)S(1)}, f32[4096,128]{1,0:T(8,128)}, u32[]{:S(2)}) copy-start(f32[4096,128]{1,0:T(8,128)} %all-reduce.7.cloned.1.call-done) | copy-start | bytes 6291460
  299.4 14.8 %all-to-all-start.4 = ((f32[32,1,256]{2,1,0:T(1,128)}), f32[32,1,256]{2,1,0:T(1,128)S(1)}, u32[]{:S(2)}, u32[]{:S(2)}) async-start(f32[32,1,256]{2,1,0:T(1,128)} %compare_select_fusion), calls=%async_computation.4 | async-start | bytes 65536 | tf_op jit(solution)/shard_map/all_to_all | solution.py:177
Sparse Core Ops, SparseCore 0:
  28.2 62.2 all-reduce.8
  100.9 58.6 all-reduce.4
  224.9 54.7 all-reduce.6

commit v15 on v14

--- a/solution.py
+++ b/solution.py
@@ -133,9 +133,11 @@
     masked_sq = jnp.where(live_slot, jnp.sum(own_feat * own_feat, axis=2), jnp.float32(0.0))
     column_sq = spread(masked_sq, high, low)
     scaling = 0.5 / (0.5 + column_sq)
-    second = lax.all_to_all(own_feat[:, half:], "space", 0, 0, tiled=True)
+    shell_proj = jnp.dot(measured.T, dictionary.T, precision=HI)
+    shell_proj, later_feat = lax.optimization_barrier((shell_proj, raw))
+    second = lax.all_to_all(later_feat[:, half:], "space", 0, 0, tiled=True)
     gram = lax.psum(jnp.dot(dictionary, dictionary.T, precision=HI), "shell")
-    data_proj = lax.psum(jnp.dot(measured.T, dictionary.T, precision=HI), "shell")
+    data_proj = lax.psum(shell_proj, "shell")
     second, gram, data_proj = lax.optimization_barrier((second, gram, data_proj))
     source_count = first[:, half + x_rows, 0]
     live_here = (

time: 324 us -> 324 us (level)
    all_to_all x1, waiting for transfers between devices: 0.05 us -> 14.2 us  [on_device(): second = lax.all_to_all(later_feat[:, half:], 'space', 0, 0, tiled=True)]
    psum x1, waiting for transfers between devices: 14.1 us -> 4.04 us  [on_device(): gram = lax.psum(jnp.dot(dictionary, dictionary.T, precision=HI), 'shell')]
  transfers between devices with their start and end apart: 8 -> 8, of which waited for: 7 -> 8; matrix products, arithmetic and copies ran while one was open for 7% -> 7% of each run, Pallas kernels for 3% -> 3%
where the time goes in v15:
time: 324 us; the launch traced here: 323 us
  waiting for transfers between devices  161 us (50%)
  Pallas kernels  62.8 us (19%)
  starting transfers between devices  34.9 us (11%)
  matrix products  25.8 us (8%)
  local copies, waits for them, and re-layouts  14.4 us (4%)
  between operations  14 us (4%)
  other arithmetic  9.85 us (3%)
    psum x2, waiting for transfers between devices, on_device(): coeff_sum = lax.psum(partial_coeff, 'shell')  105 us
    pallas_call x3, Pallas kernels, row_scatter(): pl.pallas_call(functools.partial(scatter_kernel, slots, pad), out_shape=j...  36.1 us
    pallas_call x2, Pallas kernels, row_gather_dot(): pl.pallas_call(gather_kernel, out_shape=jax.ShapeDtypeStruct((8, feat.sha...  26.7 us
    all_to_all x1, waiting for transfers between devices, on_device(): first = lax.all_to_all(first, 'space', 0, 0, tiled=True)  20.3 us
    all_to_all x2, starting transfers between devices, on_device(): lax.all_to_all(local_grad, 'space', split_axis=0, concat_axis=0, tiled=True)  15.1 us
    all_to_all x1, waiting for transfers between devices, on_device(): second = lax.all_to_all(later_feat[:, half:], 'space', 0, 0, tiled=True)  14.2 us
    all_to_all x2, waiting for transfers between devices, on_device(): lax.all_to_all(local_grad, 'space', split_axis=0, concat_axis=0, tiled=True)  9.66 us
    dot_general x2, matrix products, on_device(): adjoint = jnp.dot(coeff_sum, gram, precision=HI) - data_proj  9.44 us
  transfers between devices with their start and end apart: 8, of which 8 were waited for; matrix products, arithmetic and copies ran while one was open for 7% of the time, Pallas kernels for 3%

profile of v15, /device:TPU:1, one launch (start us, length us, event | category | flops | bytes accessed | tf_op | source)
XLA Modules:
  0.0 322.7 jit_solution(6782599862875819008)
XLA Ops:
  13.6 8.7 %all-to-all-start = ((f32[32,136,128]{2,1,0:T(8,128)}), f32[32,136,128]{2,1,0:T(8,128)S(1)}, u32[]{:S(2)}, u32[]{:S(2)}) async-start(f32[32,136,128]{2,1,0:T(8,128)} %maximum_maximum_fusion), calls=%async_computation | async-start | bytes 4456448 | tf_op jit(solution)/shard_map/all_to_all | solution.py:131
  22.4 4.8 %fusion.40 = f32[4096,128]{1,0:T(8,128)} fusion(f32[64,4096]{1,0:T(8,128)S(1)} %copy-done.6, f32[128,64]{0,1:T(8,128)S(1)} %copy-done), kind=kOutput, calls=%fused_computation.64 | convolution fusion | flops 402653184 | bytes 3178496 | tf_op jit(solution)/shard_map/dot_general | solution.py:136
  28.1 3.2 slice.32
  31.3 20.3 %all-to-all-done = f32[32,136,128]{2,1,0:T(8,128)S(1)} async-done(((f32[32,136,128]{2,1,0:T(8,128)}), f32[32,136,128]{2,1,0:T(8,128)S(1)}, u32[]{:S(2)}, u32[]{:S(2)}) %all-to-all-start) | async-done | bytes 2228256 | tf_op jit(solution)/shard_map/all_to_all | solution.py:131
  51.6 6.9 %all-to-all-start.1 = ((f32[32,128,128]{2,1,0:T(8,128)}), f32[32,128,128]{2,1,0:T(8,128)}, u32[]{:S(2)}, u32[]{:S(2)}) async-start(f32[32,128,128]{2,1,0:T(8,128)} %slice.32), calls=%async_computation.1 | async-start | bytes 4194304 | tf_op jit(solution)/shard_map/all_to_all | solution.py:138
  61.9 10.4 %shard_map.86.init_ref = f32[4096,128]{1,0:T(8,128)} custom-call(s32[4096]{0:T(1024)} %get-tuple-element.20.idx_ref, f32[4096]{0:T(1024)} %get-tuple-element.18.xs_ref, f32[4352,128]{1,0:T(8,128)} %bitcast.49, f32[4096,128]{1,0:T(8,128)} %broadcast_6_init_ref.2.init_ref), custom_call_target="tpu_custom_call" | custom-call | tf_op jit(solution)/shard_map/pallas_call | solution.py:61
  72.3 14.2 %all-to-all-done.1 = f32[32,128,128]{2,1,0:T(8,128)} async-done(((f32[32,128,128]{2,1,0:T(8,128)}), f32[32,128,128]{2,1,0:T(8,128)}, u32[]{:S(2)}, u32[]{:S(2)}) %all-to-all-start.1) | async-done | bytes 2097184 | tf_op jit(solution)/shard_map/all_to_all | solution.py:138
  86.5 4.0 %all-reduce.9.cloned.1.call-done = (f32[128,128]{1,0:T(8,128)}, f32[4096,128]{1,0:T(8,128)}) async-done(((f32[128,128]{1,0:T(8,128)}, f32[4096,128]{1,0:T(8,128)}), (f32[128,128]{1,0:T(8,128)}, f32[4096,128]{1,0:T(8,128)})) %all-reduce.9.cloned.1.call-update) | async-done | bytes 2162704 | tf_op jit(solution)/shard_map/psum | solution.py:139
  90.5 10.2 %shard_map.87 = f32[4096,128]{1,0:T(8,128)} custom-call(s32[4096]{0:T(1024)} %get-tuple-element.21.idx_ref, f32[4096]{0:T(1024)} %get-tuple-element.19.xs_ref, f32[4096,128]{1,0:T(8,128)} %bitcast.6.feat_ref, f32[4096,128]{1,0:T(8,128)} %shard_map.86.init_ref), custom_call_target="tpu_custom_call" | custom-call | tf_op jit(solution)/shard_map/pallas_call | solution.py:61
  104.9 4.2 %pad_maximum_fusion = f32[32,256,128]{2,1,0:T(8,128)} fusion(f32[32,128,128]{2,1,0:T(8,128)} %all-to-all-done.1, f32[32,128,128]{2,1,0:T(8,128)S(1)} %slice.35), kind=kLoop, calls=%fused_computation.6 | loop fusion | flops 1048576 | bytes 8388608 | tf_op jit(solution)/shard_map/concatenate | solution.py:150
  109.0 50.5 %all-reduce.5.cloned.1.call-done = f32[4096,128]{1,0:T(8,128)} async-done(((f32[4096,128]{1,0:T(8,128)}), f32[4096,128]{1,0:T(8,128)}) %all-reduce.5.cloned.1.call-update) | async-done | bytes 2097168 | tf_op jit(solution)/shard_map/psum | solution.py:171
  159.5 4.7 %convolution_subtract_fusion.1.table_ref = f32[4096,128]{1,0:T(8,128)} fusion(f32[4096,128]{1,0:T(8,128)S(1)} %copy-done.4, f32[4096,128]{1,0:T(8,128)} %all-reduce.5.cloned.1.call-done, f32[128,128]{1,0:T(8,128)S(1)} %copy-done.7), kind=kOutput, calls=%fused_computation.3 | convolution fusion | flops 805830656 | bytes 6356992 | tf_op jit(solution)/shard_map/dot_general | solution.py:176
  164.3 13.3 %shard_map.88 = f32[8,1024]{1,0:T(8,128)} custom-call(s32[8192]{0:T(1024)} %bitcast.53, f32[4096,128]{1,0:T(8,128)} %convolution_subtract_fusion.1.table_ref, f32[8192,128]{1,0:T(8,128)} %bitcast.46), custom_call_target="tpu_custom_call" | custom-call | tf_op jit(solution)/shard_map/pallas_call | solution.py:101
  179.1 7.5 %all-to-all-start.2 = ((f32[32,1,256]{2,1,0:T(1,128)}), f32[32,1,256]{2,1,0:T(1,128)S(1)}, u32[]{:S(2)}, u32[]{:S(2)}) async-start(f32[32,1,256]{2,1,0:T(1,128)} %compare_select_fusion.1), calls=%async_computation.2 | async-start | bytes 65536 | tf_op jit(solution)/shard_map/all_to_all | solution.py:179
  188.1 5.8 %all-to-all-done.2 = f32[32,1,256]{2,1,0:T(1,128)S(1)} async-done(((f32[32,1,256]{2,1,0:T(1,128)}), f32[32,1,256]{2,1,0:T(1,128)S(1)}, u32[]{:S(2)}, u32[]{:S(2)}) %all-to-all-start.2) | async-done | bytes 32800 | tf_op jit(solution)/shard_map/all_to_all | solution.py:179
  197.3 3.9 %all-to-all-start.3 = ((f32[32,1,256]{2,1,0:T(1,128)}), f32[32,1,256]{2,1,0:T(1,128)S(1)}, u32[]{:S(2)}, u32[]{:S(2)}) async-start(f32[32,1,256]{2,1,0:T(1,128)} %bitcast.12), calls=%async_computation.3 | async-start | bytes 65536 | tf_op jit(solution)/shard_map/all_to_all | solution.py:166
  201.3 7.2 %all-to-all-done.3 = f32[32,1,256]{2,1,0:T(1,128)S(1)} async-done(((f32[32,1,256]{2,1,0:T(1,128)}), f32[32,1,256]{2,1,0:T(1,128)S(1)}, u32[]{:S(2)}, u32[]{:S(2)}) %all-to-all-start.3) | async-done | bytes 32800 | tf_op jit(solution)/shard_map/all_to_all | solution.py:166
  209.2 15.5 %shard_map.89 = f32[4096,128]{1,0:T(8,128)} custom-call(s32[8192]{0:T(1024)} %bitcast.54, f32[8192]{0:T(1024)} %broadcast_select_fusion.xs_ref, f32[8192,128]{1,0:T(8,128)} %bitcast.47, f32[4096,128]{1,0:T(8,128)} %broadcast_6_init_ref.2.init_ref), custom_call_target="tpu_custom_call" | custom-call | tf_op jit(solution)/shard_map/pallas_call | solution.py:61
  224.6 54.9 %all-reduce.7.cloned.1.call-done = f32[4096,128]{1,0:T(8,128)} async-done(((f32[4096,128]{1,0:T(8,128)}), f32[4096,128]{1,0:T(8,128)}) %all-reduce.7.cloned.1.call-update) | async-done | bytes 2097168 | tf_op jit(solution)/shard_map/psum | solution.py:171
  279.6 4.7 %convolution_subtract_fusion.table_ref = f32[4096,128]{1,0:T(8,128)} fusion(f32[4096,128]{1,0:T(8,128)S(1)} %copy-done.4, f32[4096,128]{1,0:T(8,128)} %all-reduce.7.cloned.1.call-done, f32[128,128]{1,0:T(8,128)S(1)} %copy-done.7), kind=kOutput, calls=%fused_computation.2 | convolution fusion | flops 805830656 | bytes 6356992 | tf_op jit(solution)/shard_map/dot_general | solution.py:176
  284.3 13.4 %shard_map.90 = f32[8,1024]{1,0:T(8,128)} custom-call(s32[8192]{0:T(1024)} %bitcast.55, f32[4096,128]{1,0:T(8,128)} %convolution_subtract_fusion.table_ref, f32[8192,128]{1,0:T(8,128)} %bitcast.48), custom_call_target="tpu_custom_call" | custom-call | tf_op jit(solution)/shard_map/pallas_call | solution.py:101
  299.3 7.5 %all-to-all-start.4 = ((f32[32,1,256]{2,1,0:T(1,128)}), f32[32,1,256]{2,1,0:T(1,128)S(1)}, u32[]{:S(2)}, u32[]{:S(2)}) async-start(f32[32,1,256]{2,1,0:T(1,128)} %compare_select_fusion), calls=%async_computation.4 | async-start | bytes 65536 | tf_op jit(solution)/shard_map/all_to_all | solution.py:179
  306.8 3.4 %fusion = f32[64,4096]{1,0:T(8,128)} fusion(f32[64,4096]{1,0:T(8,128)S(1)} %copy-done.6, f32[4096,128]{1,0:T(8,128)S(1)} %copy-done.5, f32[128,64]{0,1:T(8,128)S(1)} %copy-done), kind=kOutput, calls=%fused_computation.5 | convolution fusion | flops 402915328 | bytes 4227072 | tf_op jit(solution)/shard_map/jg,vj->gv/dot_general | solution.py:174
  310.2 3.9 %all-to-all-done.4 = f32[32,1,256]{2,1,0:T(1,128)S(1)} async-done(((f32[32,1,256]{2,1,0:T(1,128)}), f32[32,1,256]{2,1,0:T(1,128)S(1)}, u32[]{:S(2)}, u32[]{:S(2)}) %all-to-all-start.4) | async-done | bytes 32800 | tf_op jit(solution)/shard_map/all_to_all | solution.py:179
  (67 shorter events, 25.5 us)
Async XLA Ops:
  7.2 15.2 %copy-start = (f32[128,64]{0,1:T(8,128)S(1)}, f32[128,64]{0,1:T(8,128)}, u32[]{:S(2)}) copy-start(f32[128,64]{0,1:T(8,128)} %param.12) | copy-start | bytes 98308
  8.8 1.8 copy-start.10
  13.6 8.8 %copy-start.6 = (f32[64,4096]{1,0:T(8,128)S(1)}, f32[64,4096]{1,0:T(8,128)}, u32[]{:S(2)}) copy-start(f32[64,4096]{1,0:T(8,128)} %param.13) | copy-start | bytes 3145732
  13.6 38.0 %all-to-all-start = ((f32[32,136,128]{2,1,0:T(8,128)}), f32[32,136,128]{2,1,0:T(8,128)S(1)}, u32[]{:S(2)}, u32[]{:S(2)}) async-start(f32[32,136,128]{2,1,0:T(8,128)} %maximum_maximum_fusion), calls=%async_computation | async-start | bytes 4456448 | tf_op jit(solution)/shard_map/all_to_all | solution.py:131
  22.3 68.2 %all-reduce.9.cloned.1.call-start = ((), (), s32[]{:S(2)}) async-start(), calls=%async_computation.7 | async-start | bytes 4325376 | tf_op jit(solution)/shard_map/psum | solution.py:139
  31.3 27.5 %copy-start.8 = (s32[1,1,32,256]{3,2,1,0:T(8,128)S(1)}, s32[1,1,32,256]{3,2,1,0:T(8,128)}, u32[]{:S(2)}) copy-start(s32[1,1,32,256]{3,2,1,0:T(8,128)} %param.11) | copy-start | bytes 98308
  51.6 7.8 %copy-start.1 = (f32[32,136,128]{2,1,0:T(8,128)}, f32[32,136,128]{2,1,0:T(8,128)S(1)}, u32[]{:S(2)}) copy-start(f32[32,136,128]{2,1,0:T(8,128)S(1)} %all-to-all-done) | copy-start | bytes 6684676
  51.6 34.9 %all-to-all-start.1 = ((f32[32,128,128]{2,1,0:T(8,128)}), f32[32,128,128]{2,1,0:T(8,128)}, u32[]{:S(2)}, u32[]{:S(2)}) async-start(f32[32,128,128]{2,1,0:T(8,128)} %slice.32), calls=%async_computation.1 | async-start | bytes 4194304 | tf_op jit(solution)/shard_map/all_to_all | solution.py:138
  58.5 101.1 %all-reduce.5.cloned.1.call-start = ((), (), s32[]{:S(2)}) async-start(), calls=%async_computation.5 | async-start | bytes 4194304 | tf_op jit(solution)/shard_map/psum | solution.py:171
  90.5 10.9 %copy-start.2 = (f32[32,136,128]{2,1,0:T(8,128)S(1)}, f32[32,136,128]{2,1,0:T(8,128)}, u32[]{:S(2)}) copy-start(f32[32,136,128]{2,1,0:T(8,128)} %copy-done.1) | copy-start | bytes 6684676
  101.4 2.2 copy-start.3
  104.8 54.7 %copy-start.4 = (f32[4096,128]{1,0:T(8,128)S(1)}, f32[4096,128]{1,0:T(8,128)}, u32[]{:S(2)}) copy-start(f32[4096,128]{1,0:T(8,128)} %get-tuple-element.15) | copy-start | bytes 6291460
  104.8 54.7 %copy-start.7 = (f32[128,128]{1,0:T(8,128)S(1)}, f32[128,128]{1,0:T(8,128)}, u32[]{:S(2)}) copy-start(f32[128,128]{1,0:T(8,128)} %get-tuple-element.14) | copy-start | bytes 196612
  178.4 17.0 %copy-start.9 = (f32[2048]{0:T(1024)S(1)}, f32[2048]{0:T(1024)}, u32[]{:S(2)}) copy-start(f32[2048]{0:T(1024)} %param.7) | copy-start | bytes 24580
  179.1 14.8 %all-to-all-start.2 = ((f32[32,1,256]{2,1,0:T(1,128)}), f32[32,1,256]{2,1,0:T(1,128)S(1)}, u32[]{:S(2)}, u32[]{:S(2)}) async-start(f32[32,1,256]{2,1,0:T(1,128)} %compare_select_fusion.1), calls=%async_computation.2 | async-start | bytes 65536 | tf_op jit(solution)/shard_map/all_to_all | solution.py:179
  197.3 11.2 %all-to-all-start.3 = ((f32[32,1,256]{2,1,0:T(1,128)}), f32[32,1,256]{2,1,0:T(1,128)S(1)}, u32[]{:S(2)}, u32[]{:S(2)}) async-start(f32[32,1,256]{2,1,0:T(1,128)} %bitcast.12), calls=%async_computation.3 | async-start | bytes 65536 | tf_op jit(solution)/shard_map/all_to_all | solution.py:166
  201.2 78.4 %all-reduce.7.cloned.1.call-start = ((), (), s32[]{:S(2)}) async-start(), calls=%async_computation.6 | async-start | bytes 4194304 | tf_op jit(solution)/shard_map/psum | solution.py:171
  284.3 22.5 %copy-start.5 = (f32[4096,128]{1,0:T(8,128)S(1)}, f32[4096,128]{1,0:T(8,128)}, u32[]{:S(2)}) copy-start(f32[4096,128]{1,0:T(8,128)} %all-reduce.7.cloned.1.call-done) | copy-start | bytes 6291460
  299.3 14.8 %all-to-all-start.4 = ((f32[32,1,256]{2,1,0:T(1,128)}), f32[32,1,256]{2,1,0:T(1,128)S(1)}, u32[]{:S(2)}, u32[]{:S(2)}) async-start(f32[32,1,256]{2,1,0:T(1,128)} %compare_select_fusion), calls=%async_computation.4 | async-start | bytes 65536 | tf_op jit(solution)/shard_map/all_to_all | solution.py:179
Sparse Core Ops, SparseCore 0:
  28.2 62.2 all-reduce.8
  100.9 58.6 all-reduce.4
  224.7 54.7 all-reduce.6

commit v16 on v14

--- a/solution.py
+++ b/solution.py
@@ -33,8 +33,13 @@
 ACCS = 8
 
 
-def scatter_kernel(slots, pad, idx_ref, xs_ref, feat_ref, init_ref, out_ref, *accs):
-    accs[0][...] = init_ref[...]
+def scatter_kernel(slots, pad, has_init, idx_ref, xs_ref, feat_ref, *refs):
+    if has_init:
+        init_ref, out_ref, *accs = refs
+        accs[0][...] = init_ref[...]
+    else:
+        out_ref, *accs = refs
+        accs[0][...] = jnp.zeros(accs[0].shape, accs[0].dtype)
     for acc in accs[1:]:
         acc[...] = jnp.zeros(acc.shape, acc.dtype)
 
@@ -55,16 +60,18 @@
     out_ref[...] = total
 
 
-def row_scatter(idx, xs, feat, init, slots=128, pad=0):
+def row_scatter(idx, xs, feat, init, slots=128, pad=0, rows=None):
     smem = pl.BlockSpec(memory_space=pltpu.SMEM)
     vmem = pl.BlockSpec(memory_space=pltpu.VMEM)
+    shape = init.shape if init is not None else (rows, feat.shape[1])
+    operands = (idx, xs, feat) if init is None else (idx, xs, feat, init)
     return pl.pallas_call(
-        functools.partial(scatter_kernel, slots, pad),
-        out_shape=jax.ShapeDtypeStruct(init.shape, jnp.float32),
-        in_specs=[smem, smem, vmem, vmem],
+        functools.partial(scatter_kernel, slots, pad, init is not None),
+        out_shape=jax.ShapeDtypeStruct(shape, jnp.float32),
+        in_specs=[smem, smem] + [vmem] * (len(operands) - 2),
         out_specs=vmem,
-        scratch_shapes=[pltpu.VMEM(init.shape, jnp.float32) for _ in range(ACCS)],
-    )(idx, xs, feat, init)
+        scratch_shapes=[pltpu.VMEM(shape, jnp.float32) for _ in range(ACCS)],
+    )(*operands)
 
 
 def gather_kernel(idx_ref, table_ref, feat_ref, out_ref, rows_ref):
@@ -149,11 +156,10 @@
     current = weights
     residual = jnp.zeros(measured.shape, jnp.float32)
     for iteration in range(ITERS):
-        partial_coeff = jnp.zeros((measured.shape[1], coeffs), jnp.float32)
         if iteration == 0:
             partial_coeff = row_scatter(
                 vox_parts[0], first_x[:, :half].reshape(-1),
-                first.reshape(-1, coeffs), partial_coeff, half, pad,
+                first.reshape(-1, coeffs), None, half, pad, measured.shape[1],
             )
             partial_coeff = row_scatter(
                 vox_parts[1], first_x[:, half:].reshape(-1),
@@ -164,7 +170,7 @@
             local_x = lax.all_to_all(picked, "space", split_axis=0, concat_axis=0, tiled=True)
             local_x = jnp.where(live_here, local_x, 0.0)
             partial_coeff = row_scatter(
-                voxel_index, local_x.reshape(-1), local_feat, partial_coeff
+                voxel_index, local_x.reshape(-1), local_feat, None, rows=measured.shape[1]
             )
         coeff_sum = lax.psum(partial_coeff, "shell")
         if iteration == ITERS - 1:

time: 324 us -> 323 us (level)
  no operation moved by 1% of the time
where the time goes in v16:
time: 323 us; the launch traced here: 322 us
  waiting for transfers between devices  162 us (50%)
  Pallas kernels  61.5 us (19%)
  starting transfers between devices  35 us (11%)
  matrix products  25.8 us (8%)
  between operations  14 us (4%)
  local copies, waits for them, and re-layouts  13.7 us (4%)
  other arithmetic  9.85 us (3%)
    psum x2, waiting for transfers between devices, on_device(): coeff_sum = lax.psum(partial_coeff, 'shell')  106 us
    pallas_call x3, Pallas kernels, row_scatter(): pl.pallas_call(functools.partial(scatter_kernel, slots, pad, init is not...  34.8 us
    pallas_call x2, Pallas kernels, row_gather_dot(): pl.pallas_call(gather_kernel, out_shape=jax.ShapeDtypeStruct((8, feat.sha...  26.7 us
    all_to_all x1, waiting for transfers between devices, on_device(): first = lax.all_to_all(first, 'space', 0, 0, tiled=True)  23.4 us
    psum x1, waiting for transfers between devices, on_device(): gram = lax.psum(jnp.dot(dictionary, dictionary.T, precision=HI), 'shell')  16.3 us
    all_to_all x2, starting transfers between devices, on_device(): lax.all_to_all(local_grad, 'space', split_axis=0, concat_axis=0, tiled=True)  15.1 us
    all_to_all x2, waiting for transfers between devices, on_device(): lax.all_to_all(local_grad, 'space', split_axis=0, concat_axis=0, tiled=True)  9.66 us
    dot_general x2, matrix products, on_device(): adjoint = jnp.dot(coeff_sum, gram, precision=HI) - data_proj  9.43 us
  transfers between devices with their start and end apart: 8, of which 7 were waited for; matrix products, arithmetic and copies ran while one was open for 7% of the time, Pallas kernels for 3%

profile of v16, /device:TPU:1, one launch (start us, length us, event | category | flops | bytes accessed | tf_op | source)
XLA Modules:
  0.0 322.1 jit_solution(1012156899032190838)
XLA Ops:
  13.6 8.7 %all-to-all-start = ((f32[32,136,128]{2,1,0:T(8,128)}), f32[32,136,128]{2,1,0:T(8,128)S(1)}, u32[]{:S(2)}, u32[]{:S(2)}) async-start(f32[32,136,128]{2,1,0:T(8,128)} %maximum_maximum_fusion), calls=%async_computation | async-start | bytes 4456448 | tf_op jit(solution)/shard_map/all_to_all | solution.py:138
  23.3 4.8 %fusion.41 = f32[4096,128]{1,0:T(8,128)} fusion(f32[64,4096]{1,0:T(8,128)S(1)} %copy-done.6, f32[128,64]{0,1:T(8,128)S(1)} %copy-done), kind=kOutput, calls=%fused_computation.65 | convolution fusion | flops 402653184 | bytes 3178496 | tf_op jit(solution)/shard_map/dot_general | solution.py:145
  28.1 23.4 %all-to-all-done = f32[32,136,128]{2,1,0:T(8,128)S(1)} async-done(((f32[32,136,128]{2,1,0:T(8,128)}), f32[32,136,128]{2,1,0:T(8,128)S(1)}, u32[]{:S(2)}, u32[]{:S(2)}) %all-to-all-start) | async-done | bytes 2228256 | tf_op jit(solution)/shard_map/all_to_all | solution.py:138
  51.6 4.0 %slice.32 = f32[32,128,128]{2,1,0:T(8,128)} slice(f32[32,256,128]{2,1,0:T(8,128)} %bitcast.51), slice={[0:32], [128:256], [0:128]} | slice | bytes 4194304 | tf_op jit(solution)/shard_map/slice | solution.py:143
  55.6 7.0 %all-to-all-start.1 = ((f32[32,128,128]{2,1,0:T(8,128)}), f32[32,128,128]{2,1,0:T(8,128)}, u32[]{:S(2)}, u32[]{:S(2)}) async-start(f32[32,128,128]{2,1,0:T(8,128)} %slice.32), calls=%async_computation.1 | async-start | bytes 4194304 | tf_op jit(solution)/shard_map/all_to_all | solution.py:143
  64.5 9.8 %shard_map.86.refs_0_ = f32[4096,128]{1,0:T(8,128)} custom-call(s32[4096]{0:T(1024)} %get-tuple-element.16.idx_ref, f32[4096]{0:T(1024)} %get-tuple-element.14.xs_ref, f32[4352,128]{1,0:T(8,128)} %bitcast.49), custom_call_target="tpu_custom_call" | custom-call | tf_op jit(solution)/shard_map/pallas_call | solution.py:68
  74.3 16.3 %all-reduce.9.cloned.1.call-done = (f32[128,128]{1,0:T(8,128)}, f32[4096,128]{1,0:T(8,128)}) async-done(((f32[128,128]{1,0:T(8,128)}, f32[4096,128]{1,0:T(8,128)}), (f32[128,128]{1,0:T(8,128)}, f32[4096,128]{1,0:T(8,128)})) %all-reduce.9.cloned.1.call-update) | async-done | bytes 2162704 | tf_op jit(solution)/shard_map/psum | solution.py:144
  90.6 10.2 %shard_map.87 = f32[4096,128]{1,0:T(8,128)} custom-call(s32[4096]{0:T(1024)} %get-tuple-element.17.idx_ref, f32[4096]{0:T(1024)} %get-tuple-element.15.xs_ref, f32[4096,128]{1,0:T(8,128)} %bitcast.6.feat_ref, f32[4096,128]{1,0:T(8,128)} %shard_map.86.refs_0_), custom_call_target="tpu_custom_call" | custom-call | tf_op jit(solution)/shard_map/pallas_call | solution.py:68
  101.7 1.9 copy-done.3
  104.9 4.2 %pad_maximum_fusion = f32[32,256,128]{2,1,0:T(8,128)} fusion(f32[32,128,128]{2,1,0:T(8,128)} %all-to-all-done.1, f32[32,128,128]{2,1,0:T(8,128)S(1)} %slice.35), kind=kLoop, calls=%fused_computation.6 | loop fusion | flops 1048576 | bytes 8388608 | tf_op jit(solution)/shard_map/concatenate | solution.py:155
  109.1 50.6 %all-reduce.5.cloned.1.call-done = f32[4096,128]{1,0:T(8,128)} async-done(((f32[4096,128]{1,0:T(8,128)}), f32[4096,128]{1,0:T(8,128)}) %all-reduce.5.cloned.1.call-update) | async-done | bytes 2097168 | tf_op jit(solution)/shard_map/psum | solution.py:175
  159.7 4.7 %convolution_subtract_fusion.1.table_ref = f32[4096,128]{1,0:T(8,128)} fusion(f32[4096,128]{1,0:T(8,128)S(1)} %copy-done.4, f32[4096,128]{1,0:T(8,128)} %all-reduce.5.cloned.1.call-done, f32[128,128]{1,0:T(8,128)S(1)} %copy-done.7), kind=kOutput, calls=%fused_computation.3 | convolution fusion | flops 805830656 | bytes 6356992 | tf_op jit(solution)/shard_map/dot_general | solution.py:180
  164.4 13.3 %shard_map.88 = f32[8,1024]{1,0:T(8,128)} custom-call(s32[8192]{0:T(1024)} %bitcast.53, f32[4096,128]{1,0:T(8,128)} %convolution_subtract_fusion.1.table_ref, f32[8192,128]{1,0:T(8,128)} %bitcast.46), custom_call_target="tpu_custom_call" | custom-call | tf_op jit(solution)/shard_map/pallas_call | solution.py:108
  179.2 7.5 %all-to-all-start.2 = ((f32[32,1,256]{2,1,0:T(1,128)}), f32[32,1,256]{2,1,0:T(1,128)S(1)}, u32[]{:S(2)}, u32[]{:S(2)}) async-start(f32[32,1,256]{2,1,0:T(1,128)} %compare_select_fusion.1), calls=%async_computation.2 | async-start | bytes 65536 | tf_op jit(solution)/shard_map/all_to_all | solution.py:183
  188.2 5.8 %all-to-all-done.2 = f32[32,1,256]{2,1,0:T(1,128)S(1)} async-done(((f32[32,1,256]{2,1,0:T(1,128)}), f32[32,1,256]{2,1,0:T(1,128)S(1)}, u32[]{:S(2)}, u32[]{:S(2)}) %all-to-all-start.2) | async-done | bytes 32800 | tf_op jit(solution)/shard_map/all_to_all | solution.py:183
  197.4 3.9 %all-to-all-start.3 = ((f32[32,1,256]{2,1,0:T(1,128)}), f32[32,1,256]{2,1,0:T(1,128)S(1)}, u32[]{:S(2)}, u32[]{:S(2)}) async-start(f32[32,1,256]{2,1,0:T(1,128)} %bitcast.12), calls=%async_computation.3 | async-start | bytes 65536 | tf_op jit(solution)/shard_map/all_to_all | solution.py:170
  201.4 7.2 %all-to-all-done.3 = f32[32,1,256]{2,1,0:T(1,128)S(1)} async-done(((f32[32,1,256]{2,1,0:T(1,128)}), f32[32,1,256]{2,1,0:T(1,128)S(1)}, u32[]{:S(2)}, u32[]{:S(2)}) %all-to-all-start.3) | async-done | bytes 32800 | tf_op jit(solution)/shard_map/all_to_all | solution.py:170
  209.3 14.8 %shard_map.89 = f32[4096,128]{1,0:T(8,128)} custom-call(s32[8192]{0:T(1024)} %bitcast.54, f32[8192]{0:T(1024)} %broadcast_select_fusion.xs_ref, f32[8192,128]{1,0:T(8,128)} %bitcast.47), custom_call_target="tpu_custom_call" | custom-call | tf_op jit(solution)/shard_map/pallas_call | solution.py:68
  224.1 54.9 %all-reduce.7.cloned.1.call-done = f32[4096,128]{1,0:T(8,128)} async-done(((f32[4096,128]{1,0:T(8,128)}), f32[4096,128]{1,0:T(8,128)}) %all-reduce.7.cloned.1.call-update) | async-done | bytes 2097168 | tf_op jit(solution)/shard_map/psum | solution.py:175
  279.0 4.7 %convolution_subtract_fusion.table_ref = f32[4096,128]{1,0:T(8,128)} fusion(f32[4096,128]{1,0:T(8,128)S(1)} %copy-done.4, f32[4096,128]{1,0:T(8,128)} %all-reduce.7.cloned.1.call-done, f32[128,128]{1,0:T(8,128)S(1)} %copy-done.7), kind=kOutput, calls=%fused_computation.2 | convolution fusion | flops 805830656 | bytes 6356992 | tf_op jit(solution)/shard_map/dot_general | solution.py:180
  283.7 13.4 %shard_map.90 = f32[8,1024]{1,0:T(8,128)} custom-call(s32[8192]{0:T(1024)} %bitcast.55, f32[4096,128]{1,0:T(8,128)} %convolution_subtract_fusion.table_ref, f32[8192,128]{1,0:T(8,128)} %bitcast.48), custom_call_target="tpu_custom_call" | custom-call | tf_op jit(solution)/shard_map/pallas_call | solution.py:108
  298.7 7.5 %all-to-all-start.4 = ((f32[32,1,256]{2,1,0:T(1,128)}), f32[32,1,256]{2,1,0:T(1,128)S(1)}, u32[]{:S(2)}, u32[]{:S(2)}) async-start(f32[32,1,256]{2,1,0:T(1,128)} %compare_select_fusion), calls=%async_computation.4 | async-start | bytes 65536 | tf_op jit(solution)/shard_map/all_to_all | solution.py:183
  306.2 3.4 %fusion = f32[64,4096]{1,0:T(8,128)} fusion(f32[64,4096]{1,0:T(8,128)S(1)} %copy-done.6, f32[4096,128]{1,0:T(8,128)S(1)} %copy-done.5, f32[128,64]{0,1:T(8,128)S(1)} %copy-done), kind=kOutput, calls=%fused_computation.5 | convolution fusion | flops 402915328 | bytes 4227072 | tf_op jit(solution)/shard_map/jg,vj->gv/dot_general | solution.py:178
  309.6 3.9 %all-to-all-done.4 = f32[32,1,256]{2,1,0:T(1,128)S(1)} async-done(((f32[32,1,256]{2,1,0:T(1,128)}), f32[32,1,256]{2,1,0:T(1,128)S(1)}, u32[]{:S(2)}, u32[]{:S(2)}) %all-to-all-start.4) | async-done | bytes 32800 | tf_op jit(solution)/shard_map/all_to_all | solution.py:183
  (66 shorter events, 22.1 us)
Async XLA Ops:
  7.2 15.2 %copy-start = (f32[128,64]{0,1:T(8,128)S(1)}, f32[128,64]{0,1:T(8,128)}, u32[]{:S(2)}) copy-start(f32[128,64]{0,1:T(8,128)} %param.12) | copy-start | bytes 98308
  8.8 1.8 copy-start.10
  13.6 9.7 %copy-start.6 = (f32[64,4096]{1,0:T(8,128)S(1)}, f32[64,4096]{1,0:T(8,128)}, u32[]{:S(2)}) copy-start(f32[64,4096]{1,0:T(8,128)} %param.13) | copy-start | bytes 3145732
  13.6 38.0 %all-to-all-start = ((f32[32,136,128]{2,1,0:T(8,128)}), f32[32,136,128]{2,1,0:T(8,128)S(1)}, u32[]{:S(2)}, u32[]{:S(2)}) async-start(f32[32,136,128]{2,1,0:T(8,128)} %maximum_maximum_fusion), calls=%async_computation | async-start | bytes 4456448 | tf_op jit(solution)/shard_map/all_to_all | solution.py:138
  22.3 68.2 %all-reduce.9.cloned.1.call-start = ((), (), s32[]{:S(2)}) async-start(), calls=%async_computation.7 | async-start | bytes 4325376 | tf_op jit(solution)/shard_map/psum | solution.py:144
  51.6 11.9 %copy-start.1 = (f32[32,136,128]{2,1,0:T(8,128)}, f32[32,136,128]{2,1,0:T(8,128)S(1)}, u32[]{:S(2)}) copy-start(f32[32,136,128]{2,1,0:T(8,128)S(1)} %all-to-all-done) | copy-start | bytes 6684676
  55.6 7.2 %copy-start.8 = (s32[1,1,32,256]{3,2,1,0:T(8,128)S(1)}, s32[1,1,32,256]{3,2,1,0:T(8,128)}, u32[]{:S(2)}) copy-start(s32[1,1,32,256]{3,2,1,0:T(8,128)} %param.11) | copy-start | bytes 98308
  55.6 35.0 %all-to-all-start.1 = ((f32[32,128,128]{2,1,0:T(8,128)}), f32[32,128,128]{2,1,0:T(8,128)}, u32[]{:S(2)}, u32[]{:S(2)}) async-start(f32[32,128,128]{2,1,0:T(8,128)} %slice.32), calls=%async_computation.1 | async-start | bytes 4194304 | tf_op jit(solution)/shard_map/all_to_all | solution.py:143
  62.6 97.1 %all-reduce.5.cloned.1.call-start = ((), (), s32[]{:S(2)}) async-start(), calls=%async_computation.5 | async-start | bytes 4194304 | tf_op jit(solution)/shard_map/psum | solution.py:175
  90.6 10.9 %copy-start.2 = (f32[32,136,128]{2,1,0:T(8,128)S(1)}, f32[32,136,128]{2,1,0:T(8,128)}, u32[]{:S(2)}) copy-start(f32[32,136,128]{2,1,0:T(8,128)} %copy-done.1) | copy-start | bytes 6684676
  101.4 2.2 copy-start.3
  104.9 54.8 %copy-start.4 = (f32[4096,128]{1,0:T(8,128)S(1)}, f32[4096,128]{1,0:T(8,128)}, u32[]{:S(2)}) copy-start(f32[4096,128]{1,0:T(8,128)} %get-tuple-element.11) | copy-start | bytes 6291460
  104.9 54.8 %copy-start.7 = (f32[128,128]{1,0:T(8,128)S(1)}, f32[128,128]{1,0:T(8,128)}, u32[]{:S(2)}) copy-start(f32[128,128]{1,0:T(8,128)} %get-tuple-element.10) | copy-start | bytes 196612
  178.5 17.0 %copy-start.9 = (f32[2048]{0:T(1024)S(1)}, f32[2048]{0:T(1024)}, u32[]{:S(2)}) copy-start(f32[2048]{0:T(1024)} %param.7) | copy-start | bytes 24580
  179.2 14.8 %all-to-all-start.2 = ((f32[32,1,256]{2,1,0:T(1,128)}), f32[32,1,256]{2,1,0:T(1,128)S(1)}, u32[]{:S(2)}, u32[]{:S(2)}) async-start(f32[32,1,256]{2,1,0:T(1,128)} %compare_select_fusion.1), calls=%async_computation.2 | async-start | bytes 65536 | tf_op jit(solution)/shard_map/all_to_all | solution.py:183
  197.4 11.3 %all-to-all-start.3 = ((f32[32,1,256]{2,1,0:T(1,128)}), f32[32,1,256]{2,1,0:T(1,128)S(1)}, u32[]{:S(2)}, u32[]{:S(2)}) async-start(f32[32,1,256]{2,1,0:T(1,128)} %bitcast.12), calls=%async_computation.3 | async-start | bytes 65536 | tf_op jit(solution)/shard_map/all_to_all | solution.py:170
  201.3 77.7 %all-reduce.7.cloned.1.call-start = ((), (), s32[]{:S(2)}) async-start(), calls=%async_computation.6 | async-start | bytes 4194304 | tf_op jit(solution)/shard_map/psum | solution.py:175
  283.7 22.5 %copy-start.5 = (f32[4096,128]{1,0:T(8,128)S(1)}, f32[4096,128]{1,0:T(8,128)}, u32[]{:S(2)}) copy-start(f32[4096,128]{1,0:T(8,128)} %all-reduce.7.cloned.1.call-done) | copy-start | bytes 6291460
  298.7 14.8 %all-to-all-start.4 = ((f32[32,1,256]{2,1,0:T(1,128)}), f32[32,1,256]{2,1,0:T(1,128)S(1)}, u32[]{:S(2)}, u32[]{:S(2)}) async-start(f32[32,1,256]{2,1,0:T(1,128)} %compare_select_fusion), calls=%async_computation.4 | async-start | bytes 65536 | tf_op jit(solution)/shard_map/all_to_all | solution.py:183
Sparse Core Ops, SparseCore 0:
  28.3 62.2 all-reduce.8
  100.9 58.6 all-reduce.4
  224.2 54.7 all-reduce.6

commit v17 on v14

--- a/solution.py
+++ b/solution.py
@@ -69,12 +69,12 @@
 
 def gather_kernel(idx_ref, table_ref, feat_ref, out_ref, rows_ref):
     def body(step, carry):
-        for u in range(UNROLL):
-            k = step * UNROLL + u
+        for u in range(2 * UNROLL):
+            k = step * 2 * UNROLL + u
             rows_ref[pl.ds(k, 1), :] = table_ref[pl.ds(idx_ref[k], 1), :]
         return carry
 
-    lax.fori_loop(0, feat_ref.shape[0] // UNROLL, body, 0)
+    lax.fori_loop(0, feat_ref.shape[0] // (2 * UNROLL), body, 0)
     lanes = feat_ref.shape[1]
     chunk = out_ref.shape[1]
     ones = jnp.ones((8, lanes), jnp.bfloat16)

time: 324 us -> 323 us (level)
  no operation moved by 1% of the time
where the time goes in v17:
time: 323 us; the launch traced here: 322 us
  waiting for transfers between devices  160 us (50%)
  Pallas kernels  62.2 us (19%)
  starting transfers between devices  35 us (11%)
  matrix products  25.8 us (8%)
  local copies, waits for them, and re-layouts  15.2 us (5%)
  between operations  14 us (4%)
  other arithmetic  9.85 us (3%)
    psum x2, waiting for transfers between devices, on_device(): coeff_sum = lax.psum(partial_coeff, 'shell')  106 us
    pallas_call x3, Pallas kernels, row_scatter(): pl.pallas_call(functools.partial(scatter_kernel, slots, pad), out_shape=j...  36.1 us
    pallas_call x2, Pallas kernels, row_gather_dot(): pl.pallas_call(gather_kernel, out_shape=jax.ShapeDtypeStruct((8, feat.sha...  26.1 us
    all_to_all x1, waiting for transfers between devices, on_device(): first = lax.all_to_all(first, 'space', 0, 0, tiled=True)  23.5 us
    all_to_all x2, starting transfers between devices, on_device(): lax.all_to_all(local_grad, 'space', split_axis=0, concat_axis=0, tiled=True)  15.1 us
    psum x1, waiting for transfers between devices, on_device(): gram = lax.psum(jnp.dot(dictionary, dictionary.T, precision=HI), 'shell')  14.1 us
    all_to_all x2, waiting for transfers between devices, on_device(): lax.all_to_all(local_grad, 'space', split_axis=0, concat_axis=0, tiled=True)  9.66 us
    dot_general x2, matrix products, on_device(): adjoint = jnp.dot(coeff_sum, gram, precision=HI) - data_proj  9.44 us
  transfers between devices with their start and end apart: 8, of which 7 were waited for; matrix products, arithmetic and copies ran while one was open for 7% of the time, Pallas kernels for 3%

profile of v17, /device:TPU:1, one launch (start us, length us, event | category | flops | bytes accessed | tf_op | source)
XLA Modules:
  0.0 322.2 jit_solution(860139440757805993)
XLA Ops:
  13.6 8.7 %all-to-all-start = ((f32[32,136,128]{2,1,0:T(8,128)}), f32[32,136,128]{2,1,0:T(8,128)S(1)}, u32[]{:S(2)}, u32[]{:S(2)}) async-start(f32[32,136,128]{2,1,0:T(8,128)} %maximum_maximum_fusion), calls=%async_computation | async-start | bytes 4456448 | tf_op jit(solution)/shard_map/all_to_all | solution.py:131
  23.3 4.8 %fusion.41 = f32[4096,128]{1,0:T(8,128)} fusion(f32[64,4096]{1,0:T(8,128)S(1)} %copy-done.6, f32[128,64]{0,1:T(8,128)S(1)} %copy-done), kind=kOutput, calls=%fused_computation.65 | convolution fusion | flops 402653184 | bytes 3178496 | tf_op jit(solution)/shard_map/dot_general | solution.py:138
  28.1 23.5 %all-to-all-done = f32[32,136,128]{2,1,0:T(8,128)S(1)} async-done(((f32[32,136,128]{2,1,0:T(8,128)}), f32[32,136,128]{2,1,0:T(8,128)S(1)}, u32[]{:S(2)}, u32[]{:S(2)}) %all-to-all-start) | async-done | bytes 2228256 | tf_op jit(solution)/shard_map/all_to_all | solution.py:131
  51.6 4.0 %slice.32 = f32[32,128,128]{2,1,0:T(8,128)} slice(f32[32,256,128]{2,1,0:T(8,128)} %bitcast.51), slice={[0:32], [128:256], [0:128]} | slice | bytes 4194304 | tf_op jit(solution)/shard_map/slice | solution.py:136
  55.6 7.0 %all-to-all-start.1 = ((f32[32,128,128]{2,1,0:T(8,128)}), f32[32,128,128]{2,1,0:T(8,128)}, u32[]{:S(2)}, u32[]{:S(2)}) async-start(f32[32,128,128]{2,1,0:T(8,128)} %slice.32), calls=%async_computation.1 | async-start | bytes 4194304 | tf_op jit(solution)/shard_map/all_to_all | solution.py:136
  65.9 10.4 %shard_map.86.init_ref = f32[4096,128]{1,0:T(8,128)} custom-call(s32[4096]{0:T(1024)} %get-tuple-element.16.idx_ref, f32[4096]{0:T(1024)} %get-tuple-element.14.xs_ref, f32[4352,128]{1,0:T(8,128)} %bitcast.49, f32[4096,128]{1,0:T(8,128)} %broadcast_6_init_ref.2.init_ref), custom_call_target="tpu_custom_call" | custom-call | tf_op jit(solution)/shard_map/pallas_call | solution.py:61
  76.4 14.1 %all-reduce.9.cloned.1.call-done = (f32[128,128]{1,0:T(8,128)}, f32[4096,128]{1,0:T(8,128)}) async-done(((f32[128,128]{1,0:T(8,128)}, f32[4096,128]{1,0:T(8,128)}), (f32[128,128]{1,0:T(8,128)}, f32[4096,128]{1,0:T(8,128)})) %all-reduce.9.cloned.1.call-update) | async-done | bytes 2162704 | tf_op jit(solution)/shard_map/psum | solution.py:137
  90.5 10.2 %shard_map.87 = f32[4096,128]{1,0:T(8,128)} custom-call(s32[4096]{0:T(1024)} %get-tuple-element.17.idx_ref, f32[4096]{0:T(1024)} %get-tuple-element.15.xs_ref, f32[4096,128]{1,0:T(8,128)} %bitcast.6.feat_ref, f32[4096,128]{1,0:T(8,128)} %shard_map.86.init_ref), custom_call_target="tpu_custom_call" | custom-call | tf_op jit(solution)/shard_map/pallas_call | solution.py:61
  101.7 1.9 copy-done.3
  104.9 4.2 %pad_maximum_fusion = f32[32,256,128]{2,1,0:T(8,128)} fusion(f32[32,128,128]{2,1,0:T(8,128)} %all-to-all-done.1, f32[32,128,128]{2,1,0:T(8,128)S(1)} %slice.35), kind=kLoop, calls=%fused_computation.6 | loop fusion | flops 1048576 | bytes 8388608 | tf_op jit(solution)/shard_map/concatenate | solution.py:148
  109.0 50.6 %all-reduce.5.cloned.1.call-done = f32[4096,128]{1,0:T(8,128)} async-done(((f32[4096,128]{1,0:T(8,128)}), f32[4096,128]{1,0:T(8,128)}) %all-reduce.5.cloned.1.call-update) | async-done | bytes 2097168 | tf_op jit(solution)/shard_map/psum | solution.py:169
  159.6 4.7 %convolution_subtract_fusion.1.table_ref = f32[4096,128]{1,0:T(8,128)} fusion(f32[4096,128]{1,0:T(8,128)S(1)} %copy-done.4, f32[4096,128]{1,0:T(8,128)} %all-reduce.5.cloned.1.call-done, f32[128,128]{1,0:T(8,128)S(1)} %copy-done.7), kind=kOutput, calls=%fused_computation.3 | convolution fusion | flops 805830656 | bytes 6356992 | tf_op jit(solution)/shard_map/dot_general | solution.py:174
  164.4 13.0 %shard_map.88 = f32[8,1024]{1,0:T(8,128)} custom-call(s32[8192]{0:T(1024)} %bitcast.53, f32[4096,128]{1,0:T(8,128)} %convolution_subtract_fusion.1.table_ref, f32[8192,128]{1,0:T(8,128)} %bitcast.46), custom_call_target="tpu_custom_call" | custom-call | tf_op jit(solution)/shard_map/pallas_call | solution.py:101
  178.9 7.5 %all-to-all-start.2 = ((f32[32,1,256]{2,1,0:T(1,128)}), f32[32,1,256]{2,1,0:T(1,128)S(1)}, u32[]{:S(2)}, u32[]{:S(2)}) async-start(f32[32,1,256]{2,1,0:T(1,128)} %compare_select_fusion.1), calls=%async_computation.2 | async-start | bytes 65536 | tf_op jit(solution)/shard_map/all_to_all | solution.py:177
  187.9 5.8 %all-to-all-done.2 = f32[32,1,256]{2,1,0:T(1,128)S(1)} async-done(((f32[32,1,256]{2,1,0:T(1,128)}), f32[32,1,256]{2,1,0:T(1,128)S(1)}, u32[]{:S(2)}, u32[]{:S(2)}) %all-to-all-start.2) | async-done | bytes 32800 | tf_op jit(solution)/shard_map/all_to_all | solution.py:177
  197.1 3.9 %all-to-all-start.3 = ((f32[32,1,256]{2,1,0:T(1,128)}), f32[32,1,256]{2,1,0:T(1,128)S(1)}, u32[]{:S(2)}, u32[]{:S(2)}) async-start(f32[32,1,256]{2,1,0:T(1,128)} %bitcast.12), calls=%async_computation.3 | async-start | bytes 65536 | tf_op jit(solution)/shard_map/all_to_all | solution.py:164
  201.1 7.2 %all-to-all-done.3 = f32[32,1,256]{2,1,0:T(1,128)S(1)} async-done(((f32[32,1,256]{2,1,0:T(1,128)}), f32[32,1,256]{2,1,0:T(1,128)S(1)}, u32[]{:S(2)}, u32[]{:S(2)}) %all-to-all-start.3) | async-done | bytes 32800 | tf_op jit(solution)/shard_map/all_to_all | solution.py:164
  209.0 15.5 %shard_map.89 = f32[4096,128]{1,0:T(8,128)} custom-call(s32[8192]{0:T(1024)} %bitcast.54, f32[8192]{0:T(1024)} %broadcast_select_fusion.xs_ref, f32[8192,128]{1,0:T(8,128)} %bitcast.47, f32[4096,128]{1,0:T(8,128)} %broadcast_6_init_ref.2.init_ref), custom_call_target="tpu_custom_call" | custom-call | tf_op jit(solution)/shard_map/pallas_call | solution.py:61
  224.4 54.9 %all-reduce.7.cloned.1.call-done = f32[4096,128]{1,0:T(8,128)} async-done(((f32[4096,128]{1,0:T(8,128)}), f32[4096,128]{1,0:T(8,128)}) %all-reduce.7.cloned.1.call-update) | async-done | bytes 2097168 | tf_op jit(solution)/shard_map/psum | solution.py:169
  279.4 4.7 %convolution_subtract_fusion.table_ref = f32[4096,128]{1,0:T(8,128)} fusion(f32[4096,128]{1,0:T(8,128)S(1)} %copy-done.4, f32[4096,128]{1,0:T(8,128)} %all-reduce.7.cloned.1.call-done, f32[128,128]{1,0:T(8,128)S(1)} %copy-done.7), kind=kOutput, calls=%fused_computation.2 | convolution fusion | flops 805830656 | bytes 6356992 | tf_op jit(solution)/shard_map/dot_general | solution.py:174
  284.1 13.1 %shard_map.90 = f32[8,1024]{1,0:T(8,128)} custom-call(s32[8192]{0:T(1024)} %bitcast.55, f32[4096,128]{1,0:T(8,128)} %convolution_subtract_fusion.table_ref, f32[8192,128]{1,0:T(8,128)} %bitcast.48), custom_call_target="tpu_custom_call" | custom-call | tf_op jit(solution)/shard_map/pallas_call | solution.py:101
  298.7 7.5 %all-to-all-start.4 = ((f32[32,1,256]{2,1,0:T(1,128)}), f32[32,1,256]{2,1,0:T(1,128)S(1)}, u32[]{:S(2)}, u32[]{:S(2)}) async-start(f32[32,1,256]{2,1,0:T(1,128)} %compare_select_fusion), calls=%async_computation.4 | async-start | bytes 65536 | tf_op jit(solution)/shard_map/all_to_all | solution.py:177
  306.3 3.4 %fusion = f32[64,4096]{1,0:T(8,128)} fusion(f32[64,4096]{1,0:T(8,128)S(1)} %copy-done.6, f32[4096,128]{1,0:T(8,128)S(1)} %copy-done.5, f32[128,64]{0,1:T(8,128)S(1)} %copy-done), kind=kOutput, calls=%fused_computation.5 | convolution fusion | flops 402915328 | bytes 4227072 | tf_op jit(solution)/shard_map/jg,vj->gv/dot_general | solution.py:172
  309.7 3.9 %all-to-all-done.4 = f32[32,1,256]{2,1,0:T(1,128)S(1)} async-done(((f32[32,1,256]{2,1,0:T(1,128)}), f32[32,1,256]{2,1,0:T(1,128)S(1)}, u32[]{:S(2)}, u32[]{:S(2)}) %all-to-all-start.4) | async-done | bytes 32800 | tf_op jit(solution)/shard_map/all_to_all | solution.py:177
  (67 shorter events, 23.6 us)
Async XLA Ops:
  7.2 15.2 %copy-start = (f32[128,64]{0,1:T(8,128)S(1)}, f32[128,64]{0,1:T(8,128)}, u32[]{:S(2)}) copy-start(f32[128,64]{0,1:T(8,128)} %param.12) | copy-start | bytes 98308
  8.8 1.8 copy-start.10
  13.6 9.7 %copy-start.6 = (f32[64,4096]{1,0:T(8,128)S(1)}, f32[64,4096]{1,0:T(8,128)}, u32[]{:S(2)}) copy-start(f32[64,4096]{1,0:T(8,128)} %param.13) | copy-start | bytes 3145732
  13.6 38.0 %all-to-all-start = ((f32[32,136,128]{2,1,0:T(8,128)}), f32[32,136,128]{2,1,0:T(8,128)S(1)}, u32[]{:S(2)}, u32[]{:S(2)}) async-start(f32[32,136,128]{2,1,0:T(8,128)} %maximum_maximum_fusion), calls=%async_computation | async-start | bytes 4456448 | tf_op jit(solution)/shard_map/all_to_all | solution.py:131
  22.3 68.2 %all-reduce.9.cloned.1.call-start = ((), (), s32[]{:S(2)}) async-start(), calls=%async_computation.7 | async-start | bytes 4325376 | tf_op jit(solution)/shard_map/psum | solution.py:137
  51.6 11.8 %copy-start.1 = (f32[32,136,128]{2,1,0:T(8,128)}, f32[32,136,128]{2,1,0:T(8,128)S(1)}, u32[]{:S(2)}) copy-start(f32[32,136,128]{2,1,0:T(8,128)S(1)} %all-to-all-done) | copy-start | bytes 6684676
  55.6 7.2 %copy-start.8 = (s32[1,1,32,256]{3,2,1,0:T(8,128)S(1)}, s32[1,1,32,256]{3,2,1,0:T(8,128)}, u32[]{:S(2)}) copy-start(s32[1,1,32,256]{3,2,1,0:T(8,128)} %param.11) | copy-start | bytes 98308
  55.6 35.0 %all-to-all-start.1 = ((f32[32,128,128]{2,1,0:T(8,128)}), f32[32,128,128]{2,1,0:T(8,128)}, u32[]{:S(2)}, u32[]{:S(2)}) async-start(f32[32,128,128]{2,1,0:T(8,128)} %slice.32), calls=%async_computation.1 | async-start | bytes 4194304 | tf_op jit(solution)/shard_map/all_to_all | solution.py:136
  62.6 97.1 %all-reduce.5.cloned.1.call-start = ((), (), s32[]{:S(2)}) async-start(), calls=%async_computation.5 | async-start | bytes 4194304 | tf_op jit(solution)/shard_map/psum | solution.py:169
  90.5 10.9 %copy-start.2 = (f32[32,136,128]{2,1,0:T(8,128)S(1)}, f32[32,136,128]{2,1,0:T(8,128)}, u32[]{:S(2)}) copy-start(f32[32,136,128]{2,1,0:T(8,128)} %copy-done.1) | copy-start | bytes 6684676
  101.4 2.2 copy-start.3
  104.9 54.8 %copy-start.4 = (f32[4096,128]{1,0:T(8,128)S(1)}, f32[4096,128]{1,0:T(8,128)}, u32[]{:S(2)}) copy-start(f32[4096,128]{1,0:T(8,128)} %get-tuple-element.11) | copy-start | bytes 6291460
  104.9 54.8 %copy-start.7 = (f32[128,128]{1,0:T(8,128)S(1)}, f32[128,128]{1,0:T(8,128)}, u32[]{:S(2)}) copy-start(f32[128,128]{1,0:T(8,128)} %get-tuple-element.10) | copy-start | bytes 196612
  178.2 17.0 %copy-start.9 = (f32[2048]{0:T(1024)S(1)}, f32[2048]{0:T(1024)}, u32[]{:S(2)}) copy-start(f32[2048]{0:T(1024)} %param.7) | copy-start | bytes 24580
  178.9 14.8 %all-to-all-start.2 = ((f32[32,1,256]{2,1,0:T(1,128)}), f32[32,1,256]{2,1,0:T(1,128)S(1)}, u32[]{:S(2)}, u32[]{:S(2)}) async-start(f32[32,1,256]{2,1,0:T(1,128)} %compare_select_fusion.1), calls=%async_computation.2 | async-start | bytes 65536 | tf_op jit(solution)/shard_map/all_to_all | solution.py:177
  197.1 11.2 %all-to-all-start.3 = ((f32[32,1,256]{2,1,0:T(1,128)}), f32[32,1,256]{2,1,0:T(1,128)S(1)}, u32[]{:S(2)}, u32[]{:S(2)}) async-start(f32[32,1,256]{2,1,0:T(1,128)} %bitcast.12), calls=%async_computation.3 | async-start | bytes 65536 | tf_op jit(solution)/shard_map/all_to_all | solution.py:164
  201.0 78.4 %all-reduce.7.cloned.1.call-start = ((), (), s32[]{:S(2)}) async-start(), calls=%async_computation.6 | async-start | bytes 4194304 | tf_op jit(solution)/shard_map/psum | solution.py:169
  284.1 22.2 %copy-start.5 = (f32[4096,128]{1,0:T(8,128)S(1)}, f32[4096,128]{1,0:T(8,128)}, u32[]{:S(2)}) copy-start(f32[4096,128]{1,0:T(8,128)} %all-reduce.7.cloned.1.call-done) | copy-start | bytes 6291460
  298.7 14.8 %all-to-all-start.4 = ((f32[32,1,256]{2,1,0:T(1,128)}), f32[32,1,256]{2,1,0:T(1,128)S(1)}, u32[]{:S(2)}, u32[]{:S(2)}) async-start(f32[32,1,256]{2,1,0:T(1,128)} %compare_select_fusion), calls=%async_computation.4 | async-start | bytes 65536 | tf_op jit(solution)/shard_map/all_to_all | solution.py:177
Sparse Core Ops, SparseCore 0:
  28.2 62.2 all-reduce.8
  100.9 58.6 all-reduce.4
  224.6 54.7 all-reduce.6
